TPU v7x, 32 devices: a whole 2x2x4 slice. The times are simulated.
32 devices in a mesh: row: 4 (over z), col: 8 (over y, x, core).
Axes of the slice: x: 2, y: 2, z: 4, core: 2. Of those that a mesh axis runs over, the one named last changes fastest.
Arguments:
- tokens: bfloat16 [12288, 1024], P(('row', 'col')), may hold values from -6 to 6
- segment_ids: int32 [32, 384], P(('row', 'col')), may hold values from 0 to 3, never falling along the last dimension, each value on 1 to 192 neighbouring positions
- gain_in: float32 [1024], replicated, may hold values from 0.5 to 1.5
- w_qkv: bfloat16 [1024, 3072], replicated, may hold values from -0.1875 to 0.1875
- conv_w: float32 [4, 3072], replicated, may hold values from -3 to 3
- w_decay: bfloat16 [1024, 12], replicated, may hold values from -0.1875 to 0.1875
- a_log: float32 [6], replicated, may hold values from -7 to -2.5
- dt_bias: float32 [6], replicated, may hold values from -3 to 3
- w_gate_o: bfloat16 [1024, 1536], replicated, may hold values from -0.1875 to 0.1875
- gain_o: float32 [256], replicated, may hold values from 0.5 to 1.5
- w_out: bfloat16 [1536, 1024], replicated, may hold values from -0.3125 to 0.3125
- gain_mid: float32 [1024], replicated, may hold values from 0.5 to 1.5
- w_gate_up: bfloat16 [2, 1024, 2816], P(None, 'row', 'col'), may hold values from -0.1875 to 0.1875
- w_down: bfloat16 [2816, 1024], P('col', 'row'), may hold values from -0.109375 to 0.109375
- cotangent: bfloat16 [12288, 1024], P(('row', 'col')), may hold values from -6 to 6
Outputs:
- block_out: bfloat16 [12288, 1024], P(('row', 'col'))
- grad_tokens: float32 [12288, 1024], P(('row', 'col'))
- grad_gain_in: float32 [1024], replicated
- grad_qkv: float32 [1024, 3072], replicated
- grad_conv: float32 [4, 3072], replicated
- grad_decay: float32 [1024, 12], replicated
- grad_a_log: float32 [6], replicated
- grad_dt_bias: float32 [6], replicated
- grad_gate_o: float32 [1024, 1536], replicated
- grad_gain_o: float32 [256], replicated
- grad_out: float32 [1536, 1024], replicated
- grad_gain_mid: float32 [1024], replicated
- grad_gate_up: float32 [2, 1024, 2816], P(None, 'row', 'col')
- grad_down: float32 [2816, 1024], P('col', 'row')
Inputs may be any that keep to these rules, and one draw needn't show every extreme that they name: Each row of segment_ids (one device's 384 tokens) holds whole sequences: the numbers never fall along the row, and a sequence spans 1 to 192 positions.
All inputs are finite; a program needn't handle non-finite values.
Results may differ from a plain program's by a relative error of at most 0.015.
The roundings to bfloat16 on the way count: a program that leaves them out, or rounds other values in their place, can miss the bound.
Values may be sent and summed in bfloat16 or wider, within the bound.
No kernel may reach another device: no remote copies, remote signals or barrier semaphores. Data moves between devices by JAX's collectives and lax.ppermute only.
A program may use at most 384 MiB of HBM per device.

v0:
```python
import jax
import jax.numpy as jnp
from jax import lax
from jax.sharding import PartitionSpec as P

HEADS = 6
HEAD_K = 128
HEAD_V = 256
CONV = 4
STRETCH = 64


EPSILON = 1e-06


def rms_scale(values, gain_vec):
    return (
        values * lax.rsqrt(jnp.mean(values * values, axis=-1, keepdims=True) + EPSILON) * gain_vec
    )


def conv_silu(raw_proj, conv_weight, segments):
    length = raw_proj.shape[0]
    mixed = raw_proj * conv_weight[CONV - 1]
    for offset in range(1, CONV):
        shifted = jnp.concatenate(
            [jnp.zeros((offset, raw_proj.shape[1]), jnp.float32), raw_proj[: length - offset]],
            axis=0,
        )
        seg_shifted = jnp.concatenate(
            [jnp.full((offset,), -1, jnp.int32), segments[: length - offset]], axis=0
        )
        keep_tap = (seg_shifted == segments).astype(jnp.float32)[:, None]
        mixed = mixed + shifted * keep_tap * conv_weight[CONV - 1 - offset]
    return jax.nn.silu(mixed)


def head_blocks(array, stretch_count):
    shaped = array.reshape((stretch_count, STRETCH) + array.shape[1:])
    return jnp.swapaxes(shaped, 1, 2)


def delta_rule(queries, keys_unit, values_part, log_decay, write_rate, segments):
    length = queries.shape[0]
    stretch_count = length // STRETCH
    highest_precision = lax.Precision.HIGHEST
    seg_blocks = segments.reshape(stretch_count, STRETCH)
    seg_before = jnp.concatenate([jnp.full((1,), -1, jnp.int32), seg_blocks[:-1, -1]], axis=0)
    row_index = jnp.arange(STRETCH)[:, None]
    col_index = jnp.arange(STRETCH)[None, :]
    identity = jnp.eye(STRETCH, dtype=jnp.float32)

    def stretch_step(key_value_state, inputs):
        query_segment, key_segment, value_c, decay_c, rate_c, seg_c, seg_prev = inputs
        cumulative = jnp.cumsum(decay_c, axis=-1)
        live = (seg_c[:, None] == seg_c[None, :]) & (row_index >= col_index)
        gap_log = cumulative[:, :, None] - cumulative[:, None, :]
        decay_mat = jnp.where(live[None], jnp.exp(jnp.where(live[None], gap_log, 0.0)), 0.0)
        incoming_carry = jnp.exp(cumulative) * (seg_c == seg_prev).astype(jnp.float32)[None, :]
        key_gram = jnp.einsum("hck,hsk->hcs", key_segment, key_segment, precision=highest_precision)
        strict = jnp.where((row_index > col_index)[None], decay_mat, 0.0)
        lower_mat = identity[None] + rate_c[:, :, None] * strict * key_gram
        state_contribution = jnp.einsum(
            "jlf,jfs->jls", key_segment, key_value_state, precision=highest_precision
        )
        right_side = rate_c[:, :, None] * (
            value_c - incoming_carry[:, :, None] * state_contribution
        )
        pseudo_target = jax.scipy.linalg.solve_triangular(lower_mat, right_side, lower=True)
        scores = (
            jnp.einsum("hck,hsk->hcs", query_segment, key_segment, precision=highest_precision)
            * decay_mat
        )
        output_rows = incoming_carry[:, :, None] * jnp.einsum(
            "jlf,jfs->jls", query_segment, key_value_state, precision=highest_precision
        )
        output_rows = output_rows + jnp.einsum(
            "hcs,hsv->hcv", scores, pseudo_target, precision=highest_precision
        )
        weighted_values = key_segment * decay_mat[:, -1, :, None]
        updated_state = incoming_carry[:, -1][:, None, None] * key_value_state + jnp.einsum(
            "gub,gue->gbe", weighted_values, pseudo_target, precision=highest_precision
        )
        return (updated_state, output_rows)

    initial = jnp.zeros((HEADS, HEAD_K, HEAD_V), jnp.float32)
    inputs = (
        head_blocks(queries, stretch_count),
        head_blocks(keys_unit, stretch_count),
        head_blocks(values_part, stretch_count),
        head_blocks(log_decay, stretch_count),
        head_blocks(write_rate, stretch_count),
        seg_blocks,
        seg_before,
    )
    _, stacked = lax.scan(stretch_step, initial, inputs)
    return jnp.swapaxes(stacked, 1, 2).reshape(length, HEADS, HEAD_V)


def mixer(raw_proj, gate_logits, out_gate, segments, conv_weight, a_log, dt_bias, gain_o):
    length = raw_proj.shape[0]
    key_dim = HEADS * HEAD_K
    conv = conv_silu(raw_proj, conv_weight, segments)
    queries = conv[:, :key_dim].reshape(length, HEADS, HEAD_K)
    keys_raw = conv[:, key_dim : 2 * key_dim].reshape(length, HEADS, HEAD_K)
    values_part = conv[:, 2 * key_dim :].reshape(length, HEADS, HEAD_V)
    queries = (
        queries
        * lax.rsqrt(jnp.sum(queries * queries, axis=-1, keepdims=True) + EPSILON)
        * HEAD_K ** (-0.5)
    )
    keys_unit = keys_raw * lax.rsqrt(jnp.sum(keys_raw * keys_raw, axis=-1, keepdims=True) + EPSILON)
    log_decay = -jnp.exp(a_log) * jax.nn.softplus(gate_logits[:, :HEADS] + dt_bias)
    write_rate = jax.nn.sigmoid(gate_logits[:, HEADS:])
    delta_out = delta_rule(queries, keys_unit, values_part, log_decay, write_rate, segments)
    gate_vals = jax.nn.silu(out_gate).reshape(length, HEADS, HEAD_V)
    normed = (
        delta_out
        * lax.rsqrt(jnp.mean(delta_out * delta_out, axis=-1, keepdims=True) + EPSILON)
        * gain_o
        * gate_vals
    )
    return normed.reshape(length, HEADS * HEAD_V)


def contract_rows(left, right):
    return lax.dot_general(
        left, right, (((0,), (0,)), ((), ())), preferred_element_type=jnp.float32
    )


def contract_cols(left, right):
    return lax.dot_general(
        left, right, (((1,), (1,)), ((), ())), preferred_element_type=jnp.float32
    )


def swiglu_grads(normed_rows, gate_pre, up_proj, grad_hidden):
    sigmoid_g = jax.nn.sigmoid(gate_pre)
    grad_gate_pre = (
        grad_hidden * up_proj * sigmoid_g * (1.0 + gate_pre * (1.0 - sigmoid_g))
    ).astype(jnp.bfloat16)
    grad_up = (grad_hidden * gate_pre * sigmoid_g).astype(jnp.bfloat16)
    grad_gate_up = jnp.stack(
        [contract_rows(normed_rows, grad_gate_pre), contract_rows(normed_rows, grad_up)]
    )
    return (grad_gate_pre, grad_up, grad_gate_up)


def per_device(
    tokens,
    segment_ids,
    gain_in,
    w_qkv,
    conv_w,
    w_decay,
    a_log,
    dt_bias,
    w_gate_o,
    gain_o,
    w_out,
    gain_mid,
    w_gate_up,
    w_down,
    cotangent,
):
    segments = segment_ids[0]
    residual_in = tokens.astype(jnp.float32)
    normed_f, norm_in_back = jax.vjp(rms_scale, residual_in, gain_in)
    normed_in = normed_f.astype(jnp.bfloat16)
    raw_proj = jnp.dot(normed_in, w_qkv, preferred_element_type=jnp.float32)
    gate_logits = jnp.dot(normed_in, w_decay, preferred_element_type=jnp.float32)
    out_gate = jnp.dot(normed_in, w_gate_o, preferred_element_type=jnp.float32)

    def local_mixer(raw_a, logit_a, gate_a, conv_a, log_a, bias_a, gain_a):
        return mixer(raw_a, logit_a, gate_a, segments, conv_a, log_a, bias_a, gain_a)

    mixed_f, mixer_back = jax.vjp(
        local_mixer, raw_proj, gate_logits, out_gate, conv_w, a_log, dt_bias, gain_o
    )
    mixed = mixed_f.astype(jnp.bfloat16)
    middle = residual_in + jnp.dot(mixed, w_out, preferred_element_type=jnp.float32)
    normed_mf, norm_mid_back = jax.vjp(rms_scale, middle, gain_mid)
    normed_mid = normed_mf.astype(jnp.bfloat16)
    gate_up_rows, down_rows = (
        lax.all_gather(w_gate_up, "row", axis=1, tiled=True),
        lax.all_gather(w_down, "row", axis=1, tiled=True),
    )
    normed_all = lax.all_gather(normed_mid, "col", axis=0, tiled=True)
    gate_pre = jnp.dot(normed_all, gate_up_rows[0], preferred_element_type=jnp.float32)
    up_proj = jnp.dot(normed_all, gate_up_rows[1], preferred_element_type=jnp.float32)
    hidden = (jax.nn.silu(gate_pre) * up_proj).astype(jnp.bfloat16)
    ffn_out = lax.psum_scatter(
        jnp.dot(hidden, down_rows, preferred_element_type=jnp.float32).astype(jnp.bfloat16),
        "col",
        scatter_dimension=0,
        tiled=True,
    ).astype(jnp.float32)
    block_out = (middle + ffn_out).astype(jnp.bfloat16)
    cot_all = lax.all_gather(cotangent, "col", axis=0, tiled=True)
    grad_hidden = contract_cols(cot_all, down_rows)
    grad_gate_pre, grad_up, grad_gu_part = swiglu_grads(normed_all, gate_pre, up_proj, grad_hidden)
    grad_down_part = contract_rows(hidden, cot_all)
    grad_normed_mid = lax.psum_scatter(
        contract_cols(grad_gate_pre, gate_up_rows[0]) + contract_cols(grad_up, gate_up_rows[1]),
        "col",
        scatter_dimension=0,
        tiled=True,
    )
    grad_gate_up, grad_down = (
        lax.psum_scatter(
            grad_gu_part.astype(jnp.bfloat16), "row", scatter_dimension=1, tiled=True
        ).astype(jnp.float32),
        lax.psum_scatter(
            grad_down_part.astype(jnp.bfloat16), "row", scatter_dimension=1, tiled=True
        ).astype(jnp.float32),
    )
    grad_mid_norm, grad_gain_mid = norm_mid_back(grad_normed_mid)
    grad_middle = cotangent.astype(jnp.float32) + grad_mid_norm
    grad_middle_b = grad_middle.astype(jnp.bfloat16)
    grad_out = contract_rows(mixed, grad_middle_b)
    grad_mixed = contract_cols(grad_middle_b, w_out)
    grad_raw, grad_logits, grad_gate_out, grad_conv, grad_a_log, grad_dt_bias, grad_gain_o = (
        mixer_back(grad_mixed)
    )
    grad_raw_b = grad_raw.astype(jnp.bfloat16)
    grad_logits_b = grad_logits.astype(jnp.bfloat16)
    grad_gate_b = grad_gate_out.astype(jnp.bfloat16)
    grad_qkv = contract_rows(normed_in, grad_raw_b)
    grad_decay = contract_rows(normed_in, grad_logits_b)
    grad_gate_o = contract_rows(normed_in, grad_gate_b)
    grad_normed_in = (
        contract_cols(grad_raw_b, w_qkv)
        + contract_cols(grad_logits_b, w_decay)
        + contract_cols(grad_gate_b, w_gate_o)
    )
    grad_in_norm, grad_gain_in = norm_in_back(grad_normed_in)
    grad_tokens = grad_middle + grad_in_norm
    summed = lax.psum(
        (
            grad_gain_in,
            grad_qkv,
            grad_conv,
            grad_decay,
            grad_a_log,
            grad_dt_bias,
            grad_gate_o,
            grad_gain_o,
            grad_out,
            grad_gain_mid,
        ),
        ("row", "col"),
    )
    return (
        block_out,
        grad_tokens,
        summed[0],
        summed[1],
        summed[2],
        summed[3],
        summed[4],
        summed[5],
        summed[6],
        summed[7],
        summed[8],
        summed[9],
        grad_gate_up,
        grad_down,
    )


def solution(mesh):
    in_specs = (
        P(("row", "col"), None),
        P(("row", "col"), None),
        P(),
        P(),
        P(),
        P(),
        P(),
        P(),
        P(),
        P(),
        P(),
        P(),
        P(None, "row", "col"),
        P("col", "row"),
        P(("row", "col"), None),
    )
    out_specs = (
        P(("row", "col"), None),
        P(("row", "col"), None),
        P(),
        P(),
        P(),
        P(),
        P(),
        P(),
        P(),
        P(),
        P(),
        P(),
        P(None, "row", "col"),
        P("col", "row"),
    )
    return jax.shard_map(
        per_device, mesh=mesh, in_specs=in_specs, out_specs=out_specs, check_vma=False
    )
```

profile of v0, /device:TPU:0, one launch (start us, length us, event | category | flops | bytes accessed | tf_op | source)
XLA Modules:
  0.0 1777.1 jit_solution(7396442341129983852)
XLA Ops:
  13.9 5.0 fusion.215
  19.1 6.2 fusion.162
  49.5 3.8 reshape.604
  53.4 4.1 copy.145
  73.5 382.2 %while.91 = (s32[]{:T(128)}, f32[6,128,256]{2,1,0:T(8,128)}, f32[6,6,64,256]{3,2,1,0:T(8,128)}, pred[6,6,64,64]{3,2,1,0:T(32,128)(4,1)}, f32[6,6,64,64]{3,2,1,0:...) while((s32[]{:T(128)}, f32[6,128,256]{2,1,0:T(8,128)}, ...), condition=%wide.region_5.6_spmd.clone.clone, body=%wide.region_3.5_spmd.clone.clone.sunk | while | flops 682103424 | bytes 14885434 | solution.py:96
  87.4 30.2 %custom-call.47 = f32[6,1,64,64]{2,3,1,0:T(8,128)S(1)} custom-call(f32[6,1,64,64]{3,2,1,0:T(8,128)} %get-tuple-element.2606), custom_call_target="InvertDiagBlocksLowerTriangular" | custom-call | tf_op jit(solution)/shard_map/jvp()/while/body/eval_jaxpr/jit(_solve_triangular)/vmap()/triangular_solve | solution.py:69
  149.6 30.2 %custom-call.47 = f32[6,1,64,64]{2,3,1,0:T(8,128)S(1)} custom-call(f32[6,1,64,64]{3,2,1,0:T(8,128)} %get-tuple-element.2606), custom_call_target="InvertDiagBlocksLowerTriangular" | custom-call | tf_op jit(solution)/shard_map/jvp()/while/body/eval_jaxpr/jit(_solve_triangular)/vmap()/triangular_solve | solution.py:69
  213.4 30.2 %custom-call.47 = f32[6,1,64,64]{2,3,1,0:T(8,128)S(1)} custom-call(f32[6,1,64,64]{3,2,1,0:T(8,128)} %get-tuple-element.2606), custom_call_target="InvertDiagBlocksLowerTriangular" | custom-call | tf_op jit(solution)/shard_map/jvp()/while/body/eval_jaxpr/jit(_solve_triangular)/vmap()/triangular_solve | solution.py:69
  277.5 30.2 %custom-call.47 = f32[6,1,64,64]{2,3,1,0:T(8,128)S(1)} custom-call(f32[6,1,64,64]{3,2,1,0:T(8,128)} %get-tuple-element.2606), custom_call_target="InvertDiagBlocksLowerTriangular" | custom-call | tf_op jit(solution)/shard_map/jvp()/while/body/eval_jaxpr/jit(_solve_triangular)/vmap()/triangular_solve | solution.py:69
  341.5 30.2 %custom-call.47 = f32[6,1,64,64]{2,3,1,0:T(8,128)S(1)} custom-call(f32[6,1,64,64]{3,2,1,0:T(8,128)} %get-tuple-element.2606), custom_call_target="InvertDiagBlocksLowerTriangular" | custom-call | tf_op jit(solution)/shard_map/jvp()/while/body/eval_jaxpr/jit(_solve_triangular)/vmap()/triangular_solve | solution.py:69
  405.5 30.2 %custom-call.47 = f32[6,1,64,64]{2,3,1,0:T(8,128)S(1)} custom-call(f32[6,1,64,64]{3,2,1,0:T(8,128)} %get-tuple-element.2606), custom_call_target="InvertDiagBlocksLowerTriangular" | custom-call | tf_op jit(solution)/shard_map/jvp()/while/body/eval_jaxpr/jit(_solve_triangular)/vmap()/triangular_solve | solution.py:69
  467.8 6.8 multiply_convert_fusion.3
  479.1 21.1 %all_gather.14 = bf16[352,1024]{1,0:T(8,128)(2,1)} all-gather(bf16[352,256]{1,0:T(8,128)(2,1)S(1)} %copy-done.46), channel_id=1, replica_groups=mesh['row'=4,'col'=8] {'row'}, dimensions={1}, use_global_device_ids=true | all-gather | bytes 901120 | tf_op jit(solution)/shard_map/all_gather | solution.py:187
  500.2 26.4 %all-gather.4.cloned.1.call-done = bf16[3072,1024]{1,0:T(8,128)(2,1)} async-done(((bf16[384,1024]{1,0:T(8,128)(2,1)}), bf16[3072,1024]{1,0:T(8,128)(2,1)}) %all-gather.4.cloned.1.call-update) | async-done | bytes 6291472 | tf_op jit(solution)/shard_map/all_gather | solution.py:189
  526.6 7.6 fusion.185
  534.1 4.5 fusion.186
  538.7 35.2 %all-gather.8.cloned.1.call-done = bf16[3072,1024]{1,0:T(8,128)(2,1)} async-done(((bf16[384,1024]{1,0:T(8,128)(2,1)}), bf16[3072,1024]{1,0:T(8,128)(2,1)}) %all-gather.8.cloned.1.call-update) | async-done | bytes 6291472 | tf_op jit(solution)/shard_map/all_gather | solution.py:200
  573.9 10.8 multiply_convert_fusion
  584.7 3.5 fusion.184
  588.2 7.0 convolution_add_fusion.9
  595.3 7.9 convolution_convert_fusion
  608.2 8.9 convolution_convert_fusion.3
  617.2 6.0 fusion.180
  623.2 6.2 fusion.181
  631.0 56.7 %reduce-scatter.7.cloned.1.call-done = f32[384,1024]{1,0:T(8,128)} async-done(((f32[3072,1024]{1,0:T(8,128)}), f32[384,1024]{1,0:T(8,128)}) %reduce-scatter.7.cloned.1.call-update) | async-done | bytes 1572880 | tf_op jit(solution)/shard_map/reduce_scatter | solution.py:204
  690.6 62.7 %reduce-scatter.5.cloned.1.call-done = bf16[384,1024]{1,0:T(8,128)(2,1)} async-done(((bf16[3072,1024]{1,0:T(8,128)(2,1)}), bf16[384,1024]{1,0:T(8,128)(2,1)}) %reduce-scatter.5.cloned.1.call-update) | async-done | bytes 786448 | tf_op jit(solution)/shard_map/reduce_scatter | solution.py:193
  753.3 3.9 fusion.176
  758.1 4.1 fusion.187
  762.2 4.0 mul.1147
  766.2 4.6 fusion.165
  771.1 3.5 fusion.163
  780.8 371.9 %while.90 = (s32[]{:T(128)}, f32[6,128,256]{2,1,0:T(8,128)S(1)}, f32[6,6,64,128]{3,2,1,0:T(8,128)}, f32[6,6,64,128]{3,2,1,0:T(8,128)}, f32[6,6,64,256]{3,2,1,0:T...) while((s32[]{:T(128)}, f32[6,128,256]{2,1,0:T(8,128)S(1)}, ...), condition=%wide.region_22.23_spmd.clone, body=%wide.region_12.22_spmd.clone.sunk | while | flops 1382281216 | bytes 33189216 | solution.py:96
  785.9 29.5 %custom-call.46 = f32[6,1,64,64]{2,3,1,0:T(8,128)S(1)} custom-call(f32[6,1,64,64]{3,2,1,0:T(8,128)S(1)} %select_bitcast_fusion.3), custom_call_target="InvertDiagBlocksLowerTriangular" | custom-call | tf_op jit(solution)/shard_map/transpose(jvp())/while/body/eval_jaxpr/jit(_solve_triangular)/vmap()/triangular_solve | solution.py:69
  847.8 29.5 %custom-call.46 = f32[6,1,64,64]{2,3,1,0:T(8,128)S(1)} custom-call(f32[6,1,64,64]{3,2,1,0:T(8,128)S(1)} %select_bitcast_fusion.3), custom_call_target="InvertDiagBlocksLowerTriangular" | custom-call | tf_op jit(solution)/shard_map/transpose(jvp())/while/body/eval_jaxpr/jit(_solve_triangular)/vmap()/triangular_solve | solution.py:69
  909.7 29.5 %custom-call.46 = f32[6,1,64,64]{2,3,1,0:T(8,128)S(1)} custom-call(f32[6,1,64,64]{3,2,1,0:T(8,128)S(1)} %select_bitcast_fusion.3), custom_call_target="InvertDiagBlocksLowerTriangular" | custom-call | tf_op jit(solution)/shard_map/transpose(jvp())/while/body/eval_jaxpr/jit(_solve_triangular)/vmap()/triangular_solve | solution.py:69
  971.6 29.5 %custom-call.46 = f32[6,1,64,64]{2,3,1,0:T(8,128)S(1)} custom-call(f32[6,1,64,64]{3,2,1,0:T(8,128)S(1)} %select_bitcast_fusion.3), custom_call_target="InvertDiagBlocksLowerTriangular" | custom-call | tf_op jit(solution)/shard_map/transpose(jvp())/while/body/eval_jaxpr/jit(_solve_triangular)/vmap()/triangular_solve | solution.py:69
  1033.5 29.5 %custom-call.46 = f32[6,1,64,64]{2,3,1,0:T(8,128)S(1)} custom-call(f32[6,1,64,64]{3,2,1,0:T(8,128)S(1)} %select_bitcast_fusion.3), custom_call_target="InvertDiagBlocksLowerTriangular" | custom-call | tf_op jit(solution)/shard_map/transpose(jvp())/while/body/eval_jaxpr/jit(_solve_triangular)/vmap()/triangular_solve | solution.py:69
  1095.3 29.5 %custom-call.46 = f32[6,1,64,64]{2,3,1,0:T(8,128)S(1)} custom-call(f32[6,1,64,64]{3,2,1,0:T(8,128)S(1)} %select_bitcast_fusion.3), custom_call_target="InvertDiagBlocksLowerTriangular" | custom-call | tf_op jit(solution)/shard_map/transpose(jvp())/while/body/eval_jaxpr/jit(_solve_triangular)/vmap()/triangular_solve | solution.py:69
  1175.4 6.3 multiply_reduce_fusion.3
  1190.8 3.5 fusion.226
  1197.3 6.4 add_convert_fusion
  1208.8 4.5 fusion.188
  1213.4 6.7 fusion.211
  1220.4 5.9 fusion.208
  1232.9 114.4 %all-reduce.24.cloned.1.call-done = (f32[1024]{0:T(1024)}, f32[4,3072]{1,0:T(4,128)}, f32[1024,12]{0,1:T(8,128)}, f32[6]{0:T(128)}, f32[6]{0:T(128)}, /*index=5*/f32[256]{0:T(256)}, f32[1024]{0:T(1024)}) async-done(((f32[1024]{0:T(1024)}, f32[4,3072]{1,0:T(4,128)}, f32[1024,12]{0,1:T(8,128)}, f32[6]{0:T(128)}, f32[6]{0:T(128)}, /*index=5*/f32[256]{0:T(256)}, f32[1024]{0:T(1024)}), (f32[1024]{0:T(1024)}, ...) | async-done | bytes 107584 | tf_op jit(solution)/shard_map/psum | solution.py:239
  1347.3 397.7 %all-reduce.26.cloned.1.call-done = (f32[1024,3072]{1,0:T(8,128)}, f32[1024,1536]{1,0:T(8,128)}, f32[1536,1024]{1,0:T(8,128)}) async-done(((f32[1024,3072]{1,0:T(8,128)}, f32[1024,1536]{1,0:T(8,128)}, f32[1536,1024]{1,0:T(8,128)}), (f32[1024,3072]{1,0:T(8,128)}, f32[1024,1536]{1,0:T(8,128)}, f32[1536,1024]{1,0:T(8,128)})) %all-reduce.26.cloned.1.call-update) | async-done | bytes 25165840 | tf_op jit(solution)/shard_map/psum | solution.py:239
  1746.2 11.0 copy.377
  1759.5 6.1 copy.382
  (845 shorter events, 528.9 us)
Async XLA Ops:
  7.2 467.3 %copy-start = (bf16[1536,1024]{1,0:T(8,128)(2,1)S(1)}, bf16[1536,1024]{1,0:T(8,128)(2,1)}, u32[]{:S(2)}) copy-start(bf16[1536,1024]{1,0:T(8,128)(2,1)} %param.29) | copy-start | bytes 9437188
  7.2 493.0 %all-gather.6.cloned.1.call-start = ((), (), s32[]{:S(2)}) async-start(), calls=%async_computation.5 | async-start | bytes 1802240 | tf_op jit(solution)/shard_map/all_gather | solution.py:186
  7.9 518.6 %all-gather.4.cloned.1.call-start = ((), (), s32[]{:S(2)}) async-start(), calls=%async_computation.4 | async-start | bytes 7077888 | tf_op jit(solution)/shard_map/all_gather | solution.py:189
  12.2 45.3 %copy-start.49 = (f32[384]{0:T(512)}, f32[384]{0:T(512)S(1)}, u32[]{:S(2)}) copy-start(f32[384]{0:T(512)S(1)} %fusion.204) | copy-start | bytes 4612
  19.0 6.3 copy-start.3
  19.0 6.2 copy-start.75
  19.0 6.2 copy-start.77
  19.0 6.2 copy-start.79
  57.9 7.2 copy-start.68
  123.7 7.8 copy-start.48
  123.7 7.8 copy-start.53
  186.2 9.2 copy-start.48
  186.2 9.2 copy-start.53
  250.1 9.2 copy-start.48
  250.1 9.2 copy-start.53
  314.1 9.2 copy-start.48
  314.1 9.2 copy-start.53
  378.2 9.2 copy-start.48
  378.2 9.2 copy-start.53
  442.2 9.2 copy-start.48
  442.2 9.2 copy-start.53
  467.7 6.8 copy-start.11
  478.3 95.6 %all-gather.8.cloned.1.call-start = ((), (), s32[]{:S(2)}) async-start(), calls=%async_computation.7 | async-start | bytes 7077888 | tf_op jit(solution)/shard_map/all_gather | solution.py:200
  479.0 208.7 %reduce-scatter.7.cloned.1.call-start = ((), (), s32[]{:S(2)}) async-start(), calls=%async_computation.8 | async-start | bytes 14155776 | tf_op jit(solution)/shard_map/reduce_scatter | solution.py:204
  526.6 7.6 copy-start.38
  526.6 7.6 copy-start.90
  573.9 10.8 copy-start.39
  595.3 158.0 %reduce-scatter.5.cloned.1.call-start = ((), (), s32[]{:S(2)}) async-start(), calls=%async_computation.6 | async-start | bytes 7077888 | tf_op jit(solution)/shard_map/reduce_scatter | solution.py:193
  603.3 623.0 %reduce-scatter.11.cloned.1.call-start = ((), (), s32[]{:S(2)}) async-start(), calls=%async_computation.10 | async-start | bytes 901120 | tf_op jit(solution)/shard_map/reduce_scatter | solution.py:214
  617.2 610.8 %reduce-scatter.9.cloned.1.call-start = ((), (), s32[]{:S(2)}) async-start(), calls=%async_computation.9 | async-start | bytes 1802240 | tf_op jit(solution)/shard_map/reduce_scatter | solution.py:211
  617.2 6.0 copy-start.25
  630.8 716.5 %all-reduce.24.cloned.1.call-start = ((), (), s32[]{:S(2)}) async-start(), calls=%async_computation.11 | async-start | bytes 249856 | tf_op jit(solution)/shard_map/psum | solution.py:239
  1166.8 5.6 slice-start.4
  1175.4 6.3 copy-start.67
  1181.6 6.1 copy-start.4
  1187.7 7.3 copy-start.92
  1190.7 6.5 slice-start.2
  1190.8 6.4 slice-start.3
  1190.8 6.4 copy-start.55
  1190.8 12.8 slice-start.8
  1197.3 6.4 slice-start.9
  1220.1 524.8 %all-reduce.26.cloned.1.call-start = ((), (), s32[]{:S(2)}) async-start(), calls=%async_computation.12 | async-start | bytes 50331648 | tf_op jit(solution)/shard_map/psum | solution.py:239
  1746.2 11.0 copy-start.71
  1746.2 11.7 copy-start.70
  1746.2 12.3 copy-start.94
  1746.2 12.8 copy-start.93
  1759.5 6.1 copy-start.89
  1759.5 6.7 copy-start.23
  (123 other events, 362.7 us)
Sparse Core Ops, SparseCore 0:
  9.6 38.3 all-gather.5
  478.4 48.0 all-gather.3
  528.5 45.3 all-gather.7
  595.4 92.2 reduce-scatter.6
  691.5 61.7 reduce-scatter.4
  756.0 22.9 reduce-scatter.10
  781.4 32.4 reduce-scatter.8
  1220.2 126.9 all-reduce.23
  1354.8 390.0 all-reduce.25
where the time goes:
time: 1790 us; the launch traced here: 1780 us
  waiting for transfers between devices  695 us (39%)
  other arithmetic  517 us (29%)
  matrix products  346 us (19%)
  local copies, waits for them, and re-layouts  180 us (10%)
  blocking collectives  21.1 us (1%)
    psum x2, waiting for transfers between devices, per_device(): lax.psum((grad_gain_in, grad_qkv, grad_conv, grad_decay, grad_a_log, grad...  512 us
    another operation x24, other arithmetic, stretch_step(): jax.scipy.linalg.solve_triangular(lower_mat, right_side, lower=True)  364 us
    reduce_scatter x1, waiting for transfers between devices, per_device(): lax.psum_scatter(jnp.dot(hidden, down_rows, preferred_element_type=jnp.fl...  62.7 us
    reduce_scatter x1, waiting for transfers between devices, per_device(): lax.psum_scatter(contract_cols(grad_gate_pre, gate_up_rows[0]) + contract...  56.7 us
    unnamed x207, local copies, waits for them, and re-layouts  44.7 us
    dot_general x18, matrix products, stretch_step(): jnp.einsum('jlf,jfs->jls', query_segment, key_value_state, precision=high...  41.2 us
    dot_general x7, matrix products, contract_rows(): lax.dot_general(left, right, (((0,), (0,)), ((), ())), preferred_element_...  39.3 us
    dot_general x18, matrix products, stretch_step(): jnp.einsum('jlf,jfs->jls', key_segment, key_value_state, precision=highes...  36.8 us
  transfers between devices with their start and end apart: 9, of which 6 were waited for; matrix products, arithmetic and copies ran while one was open for 55% of the time, Pallas kernels for 0%

commit v1 on v0

--- a/solution.py
+++ b/solution.py
@@ -8,6 +8,7 @@
 HEAD_V = 256
 CONV = 4
 STRETCH = 64
+HI = lax.Precision.HIGHEST
 
 
 EPSILON = 1e-06
@@ -40,61 +41,100 @@
     return jnp.swapaxes(shaped, 1, 2)
 
 
+LEAF = 8
+
+
+def _mm(a, b):
+    return jnp.einsum("...ij,...jk->...ik", a, b, precision=HI)
+
+
+def _unit_lower_inverse_fwd_impl(strict_part):
+    n = strict_part.shape[-1]
+    lead = strict_part.shape[:-2]
+    nb = n // LEAF
+    eye = jnp.eye(LEAF, dtype=strict_part.dtype)
+    diag = jnp.stack(
+        [strict_part[..., i * LEAF:(i + 1) * LEAF, i * LEAF:(i + 1) * LEAF] for i in range(nb)], axis=-3
+    )
+    sq = _mm(diag, diag)
+    blocks = _mm(_mm(eye - diag, eye + sq), eye + _mm(sq, sq))
+    size = LEAF
+    while size < n:
+        count = n // (2 * size)
+        upper_inv = blocks[..., 0::2, :, :]
+        lower_inv = blocks[..., 1::2, :, :]
+        cross = jnp.stack(
+            [strict_part[..., (2 * p + 1) * size:(2 * p + 2) * size, 2 * p * size:(2 * p + 1) * size] for p in range(count)],
+            axis=-3,
+        )
+        corner = -_mm(lower_inv, _mm(cross, upper_inv))
+        zeros = jnp.zeros_like(corner)
+        top = jnp.concatenate([upper_inv, zeros], axis=-1)
+        bottom = jnp.concatenate([corner, lower_inv], axis=-1)
+        blocks = jnp.concatenate([top, bottom], axis=-2)
+        size *= 2
+    return blocks[..., 0, :, :]
+
+
+@jax.custom_vjp
+def unit_lower_inverse(strict_part):
+    return _unit_lower_inverse_fwd_impl(strict_part)
+
+
+def _uli_fwd(strict_part):
+    inv = _unit_lower_inverse_fwd_impl(strict_part)
+    return inv, inv
+
+
+def _uli_bwd(inv, grad):
+    n = inv.shape[-1]
+    below = jnp.arange(n)[:, None] > jnp.arange(n)[None, :]
+    inv_t = jnp.swapaxes(inv, -1, -2)
+    return (jnp.where(below, -_mm(inv_t, _mm(grad, inv_t)), 0.0),)
+
+
+unit_lower_inverse.defvjp(_uli_fwd, _uli_bwd)
+
+
 def delta_rule(queries, keys_unit, values_part, log_decay, write_rate, segments):
     length = queries.shape[0]
-    stretch_count = length // STRETCH
-    highest_precision = lax.Precision.HIGHEST
-    seg_blocks = segments.reshape(stretch_count, STRETCH)
-    seg_before = jnp.concatenate([jnp.full((1,), -1, jnp.int32), seg_blocks[:-1, -1]], axis=0)
-    row_index = jnp.arange(STRETCH)[:, None]
-    col_index = jnp.arange(STRETCH)[None, :]
-    identity = jnp.eye(STRETCH, dtype=jnp.float32)
-
-    def stretch_step(key_value_state, inputs):
-        query_segment, key_segment, value_c, decay_c, rate_c, seg_c, seg_prev = inputs
-        cumulative = jnp.cumsum(decay_c, axis=-1)
-        live = (seg_c[:, None] == seg_c[None, :]) & (row_index >= col_index)
-        gap_log = cumulative[:, :, None] - cumulative[:, None, :]
-        decay_mat = jnp.where(live[None], jnp.exp(jnp.where(live[None], gap_log, 0.0)), 0.0)
-        incoming_carry = jnp.exp(cumulative) * (seg_c == seg_prev).astype(jnp.float32)[None, :]
-        key_gram = jnp.einsum("hck,hsk->hcs", key_segment, key_segment, precision=highest_precision)
-        strict = jnp.where((row_index > col_index)[None], decay_mat, 0.0)
-        lower_mat = identity[None] + rate_c[:, :, None] * strict * key_gram
-        state_contribution = jnp.einsum(
-            "jlf,jfs->jls", key_segment, key_value_state, precision=highest_precision
-        )
-        right_side = rate_c[:, :, None] * (
-            value_c - incoming_carry[:, :, None] * state_contribution
-        )
-        pseudo_target = jax.scipy.linalg.solve_triangular(lower_mat, right_side, lower=True)
-        scores = (
-            jnp.einsum("hck,hsk->hcs", query_segment, key_segment, precision=highest_precision)
-            * decay_mat
-        )
-        output_rows = incoming_carry[:, :, None] * jnp.einsum(
-            "jlf,jfs->jls", query_segment, key_value_state, precision=highest_precision
-        )
-        output_rows = output_rows + jnp.einsum(
-            "hcs,hsv->hcv", scores, pseudo_target, precision=highest_precision
-        )
-        weighted_values = key_segment * decay_mat[:, -1, :, None]
-        updated_state = incoming_carry[:, -1][:, None, None] * key_value_state + jnp.einsum(
-            "gub,gue->gbe", weighted_values, pseudo_target, precision=highest_precision
-        )
-        return (updated_state, output_rows)
-
-    initial = jnp.zeros((HEADS, HEAD_K, HEAD_V), jnp.float32)
-    inputs = (
-        head_blocks(queries, stretch_count),
-        head_blocks(keys_unit, stretch_count),
-        head_blocks(values_part, stretch_count),
-        head_blocks(log_decay, stretch_count),
-        head_blocks(write_rate, stretch_count),
-        seg_blocks,
-        seg_before,
-    )
-    _, stacked = lax.scan(stretch_step, initial, inputs)
-    return jnp.swapaxes(stacked, 1, 2).reshape(length, HEADS, HEAD_V)
+    nc = length // STRETCH
+    q = head_blocks(queries, nc)
+    k = head_blocks(keys_unit, nc)
+    v = head_blocks(values_part, nc)
+    g = head_blocks(log_decay, nc)
+    beta = head_blocks(write_rate, nc)
+    seg = segments.reshape(nc, STRETCH)
+    seg_prev = jnp.concatenate([jnp.full((1,), -1, jnp.int32), seg[:-1, -1]], axis=0)
+    row = jnp.arange(STRETCH)[:, None]
+    col = jnp.arange(STRETCH)[None, :]
+    cum = jnp.cumsum(g, axis=-1)
+    live = ((seg[:, :, None] == seg[:, None, :]) & (row >= col))[:, None]
+    gap = cum[..., :, None] - cum[..., None, :]
+    decay_mat = jnp.where(live, jnp.exp(jnp.where(live, gap, 0.0)), 0.0)
+    carry = jnp.exp(cum) * (seg == seg_prev[:, None]).astype(jnp.float32)[:, None, :]
+    gram = jnp.einsum("nhck,nhsk->nhcs", k, k, precision=HI)
+    strict = jnp.where((row > col)[None, None], decay_mat, 0.0)
+    inverse = unit_lower_inverse(beta[..., None] * strict * gram)
+    rhs = jnp.concatenate([beta[..., None] * v, (beta * carry)[..., None] * k], axis=-1)
+    sol = jnp.einsum("nhcs,nhsv->nhcv", inverse, rhs, precision=HI)
+    u, w = sol[..., :HEAD_V], sol[..., HEAD_V:]
+    kw = k * decay_mat[..., -1, :, None]
+    m = jnp.einsum("nhck,nhcj->nhkj", kw, w, precision=HI)
+    nn = jnp.einsum("nhck,nhcv->nhkv", kw, u, precision=HI)
+    a_last = carry[..., -1]
+    states = [jnp.zeros((HEADS, HEAD_K, HEAD_V), jnp.float32)]
+    s = nn[0]
+    states.append(s)
+    for c in range(1, nc - 1):
+        s = a_last[c][:, None, None] * s - jnp.einsum("hkj,hjv->hkv", m[c], s, precision=HI) + nn[c]
+        states.append(s)
+    st = jnp.stack(states)
+    p = u - jnp.einsum("nhck,nhkv->nhcv", w, st, precision=HI)
+    scores = jnp.einsum("nhck,nhsk->nhcs", q, k, precision=HI) * decay_mat
+    out = carry[..., None] * jnp.einsum("nhck,nhkv->nhcv", q, st, precision=HI)
+    out = out + jnp.einsum("nhcs,nhsv->nhcv", scores, p, precision=HI)
+    return jnp.swapaxes(out, 1, 2).reshape(length, HEADS, HEAD_V)
 
 
 def mixer(raw_proj, gate_logits, out_gate, segments, conv_weight, a_log, dt_bias, gain_o):

time: 1790 us -> 1170 us (0.65)
  other arithmetic: 517 us -> 79.1 us
  matrix products: 346 us -> 252 us
  local copies, waits for them, and re-layouts: 180 us -> 105 us
    another operation x54 -> x2, other arithmetic: 373 us -> 4.12 us  [delta_rule(): cum = jnp.cumsum(g, axis=-1)]
    dot_general x114 -> x48, matrix products: 206 us -> 141 us  [the longest x12 22.6 us: delta_rule(): jnp.einsum('hkj,hjv->hkv', m[c], s, precision=HI)]
    dynamic_update_slice x30 -> x0, other arithmetic: 36.7 us -> none  [delta_rule(): _, stacked = lax.scan(stretch_step, initial, inputs)]
    another operation x18 -> x0, matrix products: 33.5 us -> none  [stretch_step(): jax.scipy.linalg.solve_triangular(lower_mat, right_side, lower=True)]
    dynamic_update_slice x30 -> x0, local copies, waits for them, and re-layouts: 18.7 us -> none  [delta_rule(): _, stacked = lax.scan(stretch_step, initial, inputs)]
    unnamed x207 -> x346, local copies, waits for them, and re-layouts: 44.7 us -> 44.4 us
  transfers between devices with their start and end apart: 9 -> 9, of which waited for: 6 -> 6; matrix products, arithmetic and copies ran while one was open for 55% -> 32% of each run, Pallas kernels for 0% -> 0%
where the time goes in v1:
time: 1170 us
  waiting for transfers between devices  696 us (59%)
  matrix products  252 us (22%)
  local copies, waits for them, and re-layouts  105 us (9%)
  other arithmetic  79.1 us (7%)
  blocking collectives  21.1 us (2%)
  between operations  16.1 us (1%)
    psum x2, waiting for transfers between devices, per_device(): lax.psum((grad_gain_in, grad_qkv, grad_conv, grad_decay, grad_a_log, grad...  512 us
    reduce_scatter x1, waiting for transfers between devices, per_device(): lax.psum_scatter(jnp.dot(hidden, down_rows, preferred_element_type=jnp.fl...  62.7 us
    reduce_scatter x1, waiting for transfers between devices, per_device(): lax.psum_scatter(contract_cols(grad_gate_pre, gate_up_rows[0]) + contract...  57.5 us
    unnamed x346, local copies, waits for them, and re-layouts  44.4 us
    dot_general x7, matrix products, contract_rows(): lax.dot_general(left, right, (((0,), (0,)), ((), ())), preferred_element_...  39.1 us
    dot_general x7, matrix products, contract_cols(): lax.dot_general(left, right, (((1,), (1,)), ((), ())), preferred_element_...  36.4 us
    all_gather x1, waiting for transfers between devices, per_device(): cot_all = lax.all_gather(cotangent, 'col', axis=0, tiled=True)  35.2 us
    all_gather x1, waiting for transfers between devices, per_device(): normed_all = lax.all_gather(normed_mid, 'col', axis=0, tiled=True)  26.4 us
  transfers between devices with their start and end apart: 9, of which 6 were waited for; matrix products, arithmetic and copies ran while one was open for 32% of the time, Pallas kernels for 0%

profile of v1, /device:TPU:0, one launch (start us, length us, event | category | flops | bytes accessed | tf_op | source)
XLA Modules:
  0.0 1168.5 jit_solution(4948760767497699421)
XLA Ops:
  13.9 5.0 fusion.228
  19.1 6.2 fusion.5
  47.9 3.6 fusion.70
  74.3 4.0 reshape.398
  86.6 5.7 fusion.94
  92.3 6.1 fusion.25
  109.2 3.6 bitcast_dynamic-update-slice_fusion.2
  123.0 6.4 slice_subtract_fusion
  146.8 6.7 multiply_convert_fusion.3
  158.1 21.1 %all_gather.14 = bf16[352,1024]{1,0:T(8,128)(2,1)} all-gather(bf16[352,256]{1,0:T(8,128)(2,1)S(1)} %copy-done.98), channel_id=1, replica_groups=mesh['row'=4,'col'=8] {'row'}, dimensions={1}, use_global_device_ids=true | all-gather | bytes 901120 | tf_op jit(solution)/shard_map/all_gather | solution.py:227
  179.2 26.4 %all-gather.4.cloned.1.call-done = bf16[3072,1024]{1,0:T(8,128)(2,1)} async-done(((bf16[384,1024]{1,0:T(8,128)(2,1)}), bf16[3072,1024]{1,0:T(8,128)(2,1)}) %all-gather.4.cloned.1.call-update) | async-done | bytes 6291472 | tf_op jit(solution)/shard_map/all_gather | solution.py:229
  205.6 7.6 fusion.117
  213.1 4.5 fusion.118
  217.7 35.2 %all-gather.8.cloned.1.call-done = bf16[3072,1024]{1,0:T(8,128)(2,1)} async-done(((bf16[384,1024]{1,0:T(8,128)(2,1)}), bf16[3072,1024]{1,0:T(8,128)(2,1)}) %all-gather.8.cloned.1.call-update) | async-done | bytes 6291472 | tf_op jit(solution)/shard_map/all_gather | solution.py:240
  252.9 10.8 multiply_convert_fusion
  263.7 3.5 fusion.116
  267.2 7.1 convolution_add_fusion
  274.4 7.9 convolution_convert_fusion
  286.9 8.8 convolution_convert_fusion.3
  295.7 6.0 fusion.62
  301.7 6.3 fusion.63
  309.3 57.5 %reduce-scatter.7.cloned.1.call-done = f32[384,1024]{1,0:T(8,128)} async-done(((f32[3072,1024]{1,0:T(8,128)}), f32[384,1024]{1,0:T(8,128)}) %reduce-scatter.7.cloned.1.call-update) | async-done | bytes 1572880 | tf_op jit(solution)/shard_map/reduce_scatter | solution.py:244
  369.7 62.7 %reduce-scatter.5.cloned.1.call-done = bf16[384,1024]{1,0:T(8,128)(2,1)} async-done(((bf16[3072,1024]{1,0:T(8,128)(2,1)}), bf16[384,1024]{1,0:T(8,128)(2,1)}) %reduce-scatter.5.cloned.1.call-update) | async-done | bytes 786448 | tf_op jit(solution)/shard_map/reduce_scatter | solution.py:233
  432.4 3.8 fusion.34
  437.2 4.2 fusion.159
  441.4 4.0 mul.830
  445.4 3.9 multiply_reduce_fusion.4
  455.1 5.0 fusion.19
  462.5 4.3 convolution_add_fusion.1
  481.3 4.6 fusion.9
  487.9 5.1 fusion.41
  493.0 4.3 fusion.6
  497.4 3.7 fusion.7
  507.7 5.0 fusion.81
  514.2 3.8 fusion.45
  518.1 4.9 multiply_reduce_fusion.11
  534.0 6.3 broadcast_multiply_fusion
  557.5 3.5 add_add_fusion.4
  561.4 6.1 multiply_reduce_fusion.3
  586.6 6.2 add_convert_fusion
  592.9 4.9 fusion.243
  600.2 4.5 fusion.160
  604.8 6.7 fusion.224
  611.6 5.9 fusion.221
  624.1 114.5 %all-reduce.42.cloned.1.call-done = (f32[1024]{0:T(1024)}, f32[4,3072]{1,0:T(4,128)}, f32[1024,12]{0,1:T(8,128)}, f32[6]{0:T(128)}, f32[6]{0:T(128)}, /*index=5*/f32[256]{0:T(256)}, f32[1024]{0:T(1024)}) async-done(((f32[1024]{0:T(1024)}, f32[4,3072]{1,0:T(4,128)}, f32[1024,12]{0,1:T(8,128)}, f32[6]{0:T(128)}, f32[6]{0:T(128)}, /*index=5*/f32[256]{0:T(256)}, f32[1024]{0:T(1024)}), (f32[1024]{0:T(1024)}, ...) | async-done | bytes 107584 | tf_op jit(solution)/shard_map/psum | solution.py:279
  738.6 397.7 %all-reduce.44.cloned.1.call-done = (f32[1024,3072]{1,0:T(8,128)}, f32[1024,1536]{1,0:T(8,128)}, f32[1536,1024]{1,0:T(8,128)}) async-done(((f32[1024,3072]{1,0:T(8,128)}, f32[1024,1536]{1,0:T(8,128)}, f32[1536,1024]{1,0:T(8,128)}), (f32[1024,3072]{1,0:T(8,128)}, f32[1024,1536]{1,0:T(8,128)}, f32[1536,1024]{1,0:T(8,128)})) %all-reduce.44.cloned.1.call-update) | async-done | bytes 25165840 | tf_op jit(solution)/shard_map/psum | solution.py:279
  1137.6 11.0 copy.259
  1150.9 6.1 copy.264
  (522 shorter events, 209.8 us)
Async XLA Ops:
  7.2 146.3 %copy-start = (bf16[1536,1024]{1,0:T(8,128)(2,1)S(1)}, bf16[1536,1024]{1,0:T(8,128)(2,1)}, u32[]{:S(2)}) copy-start(bf16[1536,1024]{1,0:T(8,128)(2,1)} %param.25) | copy-start | bytes 9437188
  7.2 172.0 %all-gather.6.cloned.1.call-start = ((), (), s32[]{:S(2)}) async-start(), calls=%async_computation.5 | async-start | bytes 1802240 | tf_op jit(solution)/shard_map/all_gather | solution.py:226
  7.9 197.6 %all-gather.4.cloned.1.call-start = ((), (), s32[]{:S(2)}) async-start(), calls=%async_computation.4 | async-start | bytes 7077888 | tf_op jit(solution)/shard_map/all_gather | solution.py:229
  12.2 134.6 %copy-start.99 = (f32[384]{0:T(512)}, f32[384]{0:T(512)S(1)}, u32[]{:S(2)}) copy-start(f32[384]{0:T(512)S(1)} %fusion.185) | copy-start | bytes 4612
  19.0 6.3 copy-start.2
  33.4 8.9 copy-start.96
  37.6 40.7 %copy-start.87 = (f32[6,64,6]{1,2,0:T(8,128)}, f32[6,64,6]{1,2,0:T(8,128)S(1)}, u32[]{:S(2)}) copy-start(f32[6,64,6]{1,2,0:T(8,128)S(1)} %copy.234) | copy-start | bytes 27652
  105.0 7.9 copy-start.130
  105.0 7.9 copy-start.134
  105.0 11.1 copy-start.136
  105.0 14.2 %copy-start.132 = (f32[6]{0:T(128)}, f32[6]{0:T(128)S(1)}, u32[]{:S(2)}) copy-start(f32[6]{0:T(128)S(1)} %get-tuple-element.28) | copy-start | bytes 76
  123.0 6.4 copy-start.8
  123.0 6.4 copy-start.19
  146.8 6.7 copy-start.128
  146.8 6.7 copy-start.22
  157.3 95.6 %all-gather.8.cloned.1.call-start = ((), (), s32[]{:S(2)}) async-start(), calls=%async_computation.7 | async-start | bytes 7077888 | tf_op jit(solution)/shard_map/all_gather | solution.py:240
  158.0 208.8 %reduce-scatter.7.cloned.1.call-start = ((), (), s32[]{:S(2)}) async-start(), calls=%async_computation.8 | async-start | bytes 14155776 | tf_op jit(solution)/shard_map/reduce_scatter | solution.py:244
  205.6 7.6 copy-start.85
  205.6 7.6 copy-start.144
  252.9 10.8 copy-start.86
  274.4 158.0 %reduce-scatter.5.cloned.1.call-start = ((), (), s32[]{:S(2)}) async-start(), calls=%async_computation.6 | async-start | bytes 7077888 | tf_op jit(solution)/shard_map/reduce_scatter | solution.py:233
  282.4 335.1 %reduce-scatter.11.cloned.1.call-start = ((), (), s32[]{:S(2)}) async-start(), calls=%async_computation.10 | async-start | bytes 901120 | tf_op jit(solution)/shard_map/reduce_scatter | solution.py:254
  295.7 323.5 %reduce-scatter.9.cloned.1.call-start = ((), (), s32[]{:S(2)}) async-start(), calls=%async_computation.9 | async-start | bytes 1802240 | tf_op jit(solution)/shard_map/reduce_scatter | solution.py:251
  295.7 6.0 copy-start.69
  309.3 60.4 %copy-start.127 = (f32[384]{0:T(512)S(1)}, f32[384]{0:T(512)}, u32[]{:S(2)}) copy-start(f32[384]{0:T(512)} %copy-done.126) | copy-start | bytes 4612
  309.3 429.3 %all-reduce.42.cloned.1.call-start = ((), (), s32[]{:S(2)}) async-start(), calls=%async_computation.11 | async-start | bytes 249856 | tf_op jit(solution)/shard_map/psum | solution.py:279
  369.7 66.6 %copy-start.129 = (f32[1536]{0:T(1024)S(1)}, f32[1536]{0:T(1024)}, u32[]{:S(2)}) copy-start(f32[1536]{0:T(1024)} %copy-done.128) | copy-start | bytes 18436
  452.5 7.6 copy-start.9
  455.0 46.0 %copy-start.36 = (f32[6,6,64,64]{2,3,1,0:T(8,128)}, f32[6,6,64,64]{2,3,1,0:T(8,128)S(1)}, u32[]{:S(2)}) copy-start(f32[6,6,64,64]{2,3,1,0:T(8,128)S(1)} %fusion.242) | copy-start | bytes 1769476
  466.9 10.9 copy-start.24
  478.2 9.6 slice-start.4
  481.2 6.6 slice-start.5
  501.1 6.6 copy-start.30
  507.7 6.5 copy-start.21
  507.7 6.5 copy-start.95
  523.0 7.2 copy-start.31
  524.7 9.2 slice-start.6
  561.4 6.1 copy-start.112
  567.5 6.1 copy-start.3
  580.1 6.5 slice-start.2
  580.2 6.4 slice-start.3
  611.5 524.8 %all-reduce.44.cloned.1.call-start = ((), (), s32[]{:S(2)}) async-start(), calls=%async_computation.12 | async-start | bytes 50331648 | tf_op jit(solution)/shard_map/psum | solution.py:279
  1137.6 11.0 copy-start.116
  1137.6 11.7 copy-start.115
  1137.6 12.3 %copy-start.148 = (f32[6]{0:T(128)S(1)}, f32[6]{0:T(128)}, u32[]{:S(2)}) copy-start(f32[6]{0:T(128)} %get-tuple-element.127) | copy-start | bytes 76
  1137.6 12.8 %copy-start.147 = (f32[6]{0:T(128)S(1)}, f32[6]{0:T(128)}, u32[]{:S(2)}) copy-start(f32[6]{0:T(128)} %get-tuple-element.128) | copy-start | bytes 76
  1150.9 6.1 copy-start.143
  1150.9 6.7 copy-start.65
  (123 other events, 399.7 us)
Sparse Core Ops, SparseCore 0:
  9.6 38.3 all-gather.5
  157.4 48.0 all-gather.3
  207.5 45.3 all-gather.7
  274.5 92.2 reduce-scatter.6
  370.6 61.7 reduce-scatter.4
  435.1 22.9 reduce-scatter.10
  460.4 32.3 reduce-scatter.8
  611.6 126.9 all-reduce.41
  746.2 390.0 all-reduce.43

commit v2 on v1

--- a/solution.py
+++ b/solution.py
@@ -219,25 +219,22 @@
         local_mixer, raw_proj, gate_logits, out_gate, conv_w, a_log, dt_bias, gain_o
     )
     mixed = mixed_f.astype(jnp.bfloat16)
+    gate_up_rows, down_rows = (
+        lax.all_gather(w_gate_up, "row", axis=1, tiled=True),
+        lax.all_gather(w_down, "row", axis=1, tiled=True),
+    )
+    cot_all = lax.all_gather(cotangent, "col", axis=0, tiled=True)
+    mixed, gate_up_rows, down_rows, cot_all = lax.optimization_barrier(
+        (mixed, gate_up_rows, down_rows, cot_all)
+    )
     middle = residual_in + jnp.dot(mixed, w_out, preferred_element_type=jnp.float32)
     normed_mf, norm_mid_back = jax.vjp(rms_scale, middle, gain_mid)
     normed_mid = normed_mf.astype(jnp.bfloat16)
-    gate_up_rows, down_rows = (
-        lax.all_gather(w_gate_up, "row", axis=1, tiled=True),
-        lax.all_gather(w_down, "row", axis=1, tiled=True),
-    )
     normed_all = lax.all_gather(normed_mid, "col", axis=0, tiled=True)
     gate_pre = jnp.dot(normed_all, gate_up_rows[0], preferred_element_type=jnp.float32)
     up_proj = jnp.dot(normed_all, gate_up_rows[1], preferred_element_type=jnp.float32)
     hidden = (jax.nn.silu(gate_pre) * up_proj).astype(jnp.bfloat16)
-    ffn_out = lax.psum_scatter(
-        jnp.dot(hidden, down_rows, preferred_element_type=jnp.float32).astype(jnp.bfloat16),
-        "col",
-        scatter_dimension=0,
-        tiled=True,
-    ).astype(jnp.float32)
-    block_out = (middle + ffn_out).astype(jnp.bfloat16)
-    cot_all = lax.all_gather(cotangent, "col", axis=0, tiled=True)
+    ffn_part = jnp.dot(hidden, down_rows, preferred_element_type=jnp.float32).astype(jnp.bfloat16)
     grad_hidden = contract_cols(cot_all, down_rows)
     grad_gate_pre, grad_up, grad_gu_part = swiglu_grads(normed_all, gate_pre, up_proj, grad_hidden)
     grad_down_part = contract_rows(hidden, cot_all)
@@ -247,6 +244,10 @@
         scatter_dimension=0,
         tiled=True,
     )
+    grad_normed_mid, ffn_part, grad_gu_part, grad_down_part = lax.optimization_barrier(
+        (grad_normed_mid, ffn_part, grad_gu_part, grad_down_part)
+    )
+    ffn_out = lax.psum_scatter(ffn_part, "col", scatter_dimension=0, tiled=True)
     grad_gate_up, grad_down = (
         lax.psum_scatter(
             grad_gu_part.astype(jnp.bfloat16), "row", scatter_dimension=1, tiled=True
@@ -266,9 +267,12 @@
     grad_raw_b = grad_raw.astype(jnp.bfloat16)
     grad_logits_b = grad_logits.astype(jnp.bfloat16)
     grad_gate_b = grad_gate_out.astype(jnp.bfloat16)
+    ffn_out, grad_raw_b = lax.optimization_barrier((ffn_out, grad_raw_b))
+    block_out = (middle + ffn_out.astype(jnp.float32)).astype(jnp.bfloat16)
     grad_qkv = contract_rows(normed_in, grad_raw_b)
     grad_decay = contract_rows(normed_in, grad_logits_b)
     grad_gate_o = contract_rows(normed_in, grad_gate_b)
+    early = summed_bf16((grad_out, grad_gate_o))
     grad_normed_in = (
         contract_cols(grad_raw_b, w_qkv)
         + contract_cols(grad_logits_b, w_decay)
@@ -276,39 +280,57 @@
     )
     grad_in_norm, grad_gain_in = norm_in_back(grad_normed_in)
     grad_tokens = grad_middle + grad_in_norm
-    summed = lax.psum(
-        (
-            grad_gain_in,
-            grad_qkv,
-            grad_conv,
-            grad_decay,
-            grad_a_log,
-            grad_dt_bias,
-            grad_gate_o,
-            grad_gain_o,
-            grad_out,
-            grad_gain_mid,
-        ),
-        ("row", "col"),
+    late = summed_bf16((grad_qkv,), after=early[0])
+    small = summed_f32(
+        (grad_gain_in, grad_conv, grad_decay, grad_a_log, grad_dt_bias, grad_gain_o, grad_gain_mid)
     )
     return (
         block_out,
         grad_tokens,
-        summed[0],
-        summed[1],
-        summed[2],
-        summed[3],
-        summed[4],
-        summed[5],
-        summed[6],
-        summed[7],
-        summed[8],
-        summed[9],
+        small[0],
+        late[0],
+        small[1],
+        small[2],
+        small[3],
+        small[4],
+        early[1],
+        small[5],
+        early[0],
+        small[6],
         grad_gate_up,
         grad_down,
     )
 
 
+def split_flat(total, parts):
+    out, at = [], 0
+    for p in parts:
+        out.append(total[at : at + p.size].reshape(p.shape).astype(jnp.float32))
+        at += p.size
+    return out
+
+
+def summed_f32(parts):
+    flat = jnp.concatenate([p.reshape(-1) for p in parts])
+    for axis in ("col", "row"):
+        n = lax.axis_size(axis)
+        if n & (n - 1):
+            flat = lax.psum(flat, axis)
+            continue
+        step = 1
+        while step < n:
+            flat = flat + lax.ppermute(flat, axis, [(i, i ^ step) for i in range(n)])
+            step *= 2
+    return split_flat(flat, parts)
+
+
+def summed_bf16(parts, after=None):
+    flat = jnp.concatenate([p.astype(jnp.bfloat16).reshape(-1) for p in parts])
+    if after is not None:
+        flat, _ = lax.optimization_barrier((flat, after))
+    return split_flat(lax.psum(flat, ("row", "col")), parts)
+
+
 def solution(mesh):
     in_specs = (
         P(("row", "col"), None),

time: 1170 us -> 862 us (0.74)
  waiting for transfers between devices: 696 us -> 340 us
  other arithmetic: 79.1 us -> 101 us
  local copies, waits for them, and re-layouts: 105 us -> 126 us
    psum x2, waiting for transfers between devices: 512 us -> 145 us  [summed_bf16(): return split_flat(lax.psum(flat, ('row', 'col')), parts)]
    all_gather x1, waiting for transfers between devices: 35.2 us -> 0.01 us  [per_device(): cot_all = lax.all_gather(cotangent, 'col', axis=0, tiled=True)]
    reduce_scatter x1, waiting for transfers between devices: 0.01 us -> 28.8 us  [per_device(): lax.psum_scatter(grad_gu_part.astype(jnp.bfloat16), 'row', scatter_dimens...]
    convert_element_type x0 -> x3, local copies, waits for them, and re-layouts: none -> 24.8 us  [split_flat(): out.append(total[at:at + p.size].reshape(p.shape).astype(jnp.float32))]
    ppermute x0 -> x5, waiting for transfers between devices: none -> 18.1 us  [summed_f32(): flat = flat + lax.ppermute(flat, axis, [(i, i ^ step) for i in range(n)])]
    convert_element_type x0 -> x3, other arithmetic: none -> 17.5 us  [the longest x2 16.3 us: split_flat(): out.append(total[at:at + p.size].reshape(p.shape).astype(jnp.float32))]
    unnamed x346 -> x326, local copies, waits for them, and re-layouts: 44.4 us -> 27.2 us
    all_gather x1, waiting for transfers between devices: 26.4 us -> 38.2 us  [per_device(): normed_all = lax.all_gather(normed_mid, 'col', axis=0, tiled=True)]
  transfers between devices with their start and end apart: 9 -> 14, of which waited for: 6 -> 10; matrix products, arithmetic and copies ran while one was open for 32% -> 42% of each run, Pallas kernels for 0% -> 0%
where the time goes in v2:
time: 862 us; the launch traced here: 851 us
  waiting for transfers between devices  340 us (39%)
  matrix products  242 us (28%)
  local copies, waits for them, and re-layouts  126 us (15%)
  other arithmetic  101 us (12%)
  blocking collectives  20.9 us (2%)
  between operations  16.5 us (2%)
    psum x2, waiting for transfers between devices, summed_bf16(): return split_flat(lax.psum(flat, ('row', 'col')), parts)  145 us
    reduce_scatter x1, waiting for transfers between devices, per_device(): lax.psum_scatter(contract_cols(grad_gate_pre, gate_up_rows[0]) + contract...  57.2 us
    reduce_scatter x1, waiting for transfers between devices, per_device(): ffn_out = lax.psum_scatter(ffn_part, 'col', scatter_dimension=0, tiled=True)  51.1 us
    all_gather x1, waiting for transfers between devices, per_device(): normed_all = lax.all_gather(normed_mid, 'col', axis=0, tiled=True)  38.2 us
    dot_general x7, matrix products, contract_rows(): lax.dot_general(left, right, (((0,), (0,)), ((), ())), preferred_element_...  33.7 us
    dot_general x7, matrix products, contract_cols(): lax.dot_general(left, right, (((1,), (1,)), ((), ())), preferred_element_...  33.3 us
    reduce_scatter x1, waiting for transfers between devices, per_device(): lax.psum_scatter(grad_gu_part.astype(jnp.bfloat16), 'row', scatter_dimens...  28.8 us
    unnamed x326, local copies, waits for them, and re-layouts  27.2 us
  transfers between devices with their start and end apart: 14, of which 10 were waited for; matrix products, arithmetic and copies ran while one was open for 42% of the time, Pallas kernels for 0%

profile of v2, /device:TPU:0, one launch (start us, length us, event | category | flops | bytes accessed | tf_op | source)
XLA Modules:
  0.0 850.5 jit_solution(14353560125100526584)
XLA Ops:
  12.4 5.0 fusion.232
  17.5 6.2 fusion.5
  58.3 4.2 reshape.444
  90.2 4.6 fusion.25
  94.9 4.4 fusion.93
  125.6 20.9 %all_gather.13 = bf16[352,1024]{1,0:T(8,128)(2,1)} all-gather(bf16[352,256]{1,0:T(8,128)(2,1)S(1)} %copy-done.97), channel_id=1, replica_groups=mesh['row'=4,'col'=8] {'row'}, dimensions={1}, use_global_device_ids=true | all-gather | bytes 901120 | tf_op jit(solution)/shard_map/all_gather | solution.py:224
  146.5 7.0 multiply_convert_fusion.3
  159.0 7.4 fusion.249
  166.4 38.2 %all-gather.8.cloned.1.call-done = bf16[3072,1024]{1,0:T(8,128)(2,1)} async-done(((bf16[384,1024]{1,0:T(8,128)(2,1)}), bf16[3072,1024]{1,0:T(8,128)(2,1)}) %all-gather.8.cloned.1.call-update) | async-done | bytes 6291472 | tf_op jit(solution)/shard_map/all_gather | solution.py:233
  204.6 5.5 fusion.115
  211.1 6.4 multiply_convert_fusion
  221.0 6.6 convolution_add_fusion
  232.1 7.0 convolution_bitcast_fusion.1
  239.1 6.7 convolution_bitcast_fusion
  247.0 8.1 convolution_convert_fusion
  255.2 7.7 fusion.250
  262.9 57.2 %reduce-scatter.5.cloned.1.call-done = f32[384,1024]{1,0:T(8,128)} async-done(((f32[3072,1024]{1,0:T(8,128)}), f32[384,1024]{1,0:T(8,128)}) %reduce-scatter.5.cloned.1.call-update) | async-done | bytes 1572880 | tf_op jit(solution)/shard_map/reduce_scatter | solution.py:241
  329.4 4.3 fusion.14
  333.7 4.0 mul.830
  344.2 5.0 fusion.19
  351.7 6.2 convolution_add_fusion.1
  371.0 6.8 reshape.460
  377.8 8.0 pad_maximum_fusion
  398.1 7.2 fusion.42
  411.8 4.6 fusion.9
  416.4 4.8 fusion.80
  422.6 8.3 fusion.6
  434.6 4.2 fusion.251
  439.0 4.1 fusion.46
  456.5 6.1 broadcast_multiply_fusion
  491.6 5.2 add_add_fusion.4
  498.2 6.1 multiply_reduce_fusion.3
  511.1 4.7 fusion.253
  518.7 8.0 add_convert_fusion
  526.7 15.2 %all-reduce.40.cloned.1.call-done = bf16[3145728]{0:T(1024)(128)(2,1)} async-done(((bf16[3145728]{0:T(1024)(128)(2,1)}), bf16[3145728]{0:T(1024)(128)(2,1)}) %all-reduce.40.cloned.1.call-update) | async-done | bytes 6291472 | tf_op jit(solution)/shard_map/psum | solution.py:331
  541.9 7.0 slice_convert_fusion
  548.9 7.4 reshape.463
  556.3 51.1 %reduce-scatter.7.cloned.1.call-done = bf16[384,1024]{1,0:T(8,128)(2,1)} async-done(((bf16[3072,1024]{1,0:T(8,128)(2,1)}), bf16[384,1024]{1,0:T(8,128)(2,1)}) %reduce-scatter.7.cloned.1.call-update) | async-done | bytes 786448 | tf_op jit(solution)/shard_map/reduce_scatter | solution.py:250
  607.3 3.9 convert_bitcast_fusion
  611.2 4.6 copy.197
  615.9 10.3 %convert_element_type.140 = bf16[1024,3072]{1,0:T(8,128)(2,1)} reshape(bf16[3145728]{0:T(1024)(128)(2,1)} %bitcast.392) | data formatting | bytes 12582912 | tf_op jit(solution)/shard_map/convert_element_type | solution.py:308
  627.7 4.9 fusion.252
  639.1 28.8 %reduce-scatter.9.cloned.1.call-done = bf16[2,256,352]{1,2,0:T(8,128)(2,1)} async-done(((bf16[2,1024,352]{1,2,0:T(8,128)(2,1)}), bf16[2,256,352]{1,2,0:T(8,128)(2,1)}) %reduce-scatter.9.cloned.1.call-update) | async-done | bytes 360464 | tf_op jit(solution)/shard_map/reduce_scatter | solution.py:252
  669.8 7.1 reshape.464
  678.6 5.4 collective-permute-done.2
  692.8 7.7 collective-permute-done.4
  704.4 129.8 %all-reduce.42.cloned.1.call-done = bf16[1024,3072]{1,0:T(8,128)(2,1)} async-done(((bf16[1024,3072]{1,0:T(8,128)(2,1)}), bf16[1024,3072]{1,0:T(8,128)(2,1)}) %all-reduce.42.cloned.1.call-update) | async-done | bytes 6291472 | tf_op jit(solution)/shard_map/psum | solution.py:331
  834.3 9.4 %convert_element_type.141 = f32[1024,3072]{1,0:T(8,128)} convert(bf16[1024,3072]{1,0:T(8,128)(2,1)} %all-reduce.42.cloned.1.call-done) | non-fusion elementwise | flops 3145728 | bytes 18874368 | tf_op jit(solution)/shard_map/convert_element_type | solution.py:308
  (531 shorter events, 240.5 us)
Async XLA Ops:
  7.2 146.4 %copy-start = (bf16[1536,1024]{1,0:T(8,128)(2,1)S(1)}, bf16[1536,1024]{1,0:T(8,128)(2,1)}, u32[]{:S(2)}) copy-start(bf16[1536,1024]{1,0:T(8,128)(2,1)} %param.25) | copy-start | bytes 9437188
  7.2 146.3 %all-gather.4.cloned.1.call-start = ((), (), s32[]{:S(2)}) async-start(), calls=%async_computation.4 | async-start | bytes 1802240 | tf_op jit(solution)/shard_map/all_gather | solution.py:223
  8.0 145.6 %all-gather.6.cloned.1.call-start = ((), (), s32[]{:S(2)}) async-start(), calls=%async_computation.5 | async-start | bytes 7077888 | tf_op jit(solution)/shard_map/all_gather | solution.py:226
  8.7 195.9 %all-gather.8.cloned.1.call-start = ((), (), s32[]{:S(2)}) async-start(), calls=%async_computation.6 | async-start | bytes 7077888 | tf_op jit(solution)/shard_map/all_gather | solution.py:233
  12.2 21.8 %copy-start.119 = (f32[384]{0:T(512)}, f32[384]{0:T(512)S(1)}, u32[]{:S(2)}) copy-start(f32[384]{0:T(512)S(1)} %fusion.191) | copy-start | bytes 4612
  17.4 6.3 copy-start.2
  31.9 9.1 %copy-start.95 = (pred[64,64]{0,1:T(8,128)(4,1)}, pred[64,64]{0,1:T(8,128)(4,1)S(1)}, u32[]{:S(2)}) copy-start(pred[64,64]{0,1:T(8,128)(4,1)S(1)} %iota_compare_fusion.3) | copy-start | bytes 12292
  36.5 47.3 %copy-start.88 = (f32[6,64,6]{1,2,0:T(8,128)}, f32[6,64,6]{1,2,0:T(8,128)S(1)}, u32[]{:S(2)}) copy-start(f32[6,64,6]{1,2,0:T(8,128)S(1)} %copy.242) | copy-start | bytes 27652
  38.0 10.8 %slice-start.4 = ((s8[4718592]{0:T(1024)(128)(4,1)}), s8[4194304]{0:T(1024)(128)(4,1)S(1)}, s32[]{:S(2)}) async-start(s8[4718592]{0:T(1024)(128)(4,1)} %bitcast.390), calls=%async_computation.17 | async-start | bytes 8388608
  41.0 7.9 slice-start.5
  64.7 34.6 %copy-start.127 = (f32[6]{0:T(128)}, f32[6]{0:T(128)S(1)}, u32[]{:S(2)}) copy-start(f32[6]{0:T(128)S(1)} %get-tuple-element.81) | copy-start | bytes 76
  64.7 35.5 %copy-start.131 = (f32[6]{0:T(128)}, f32[6]{0:T(128)S(1)}, u32[]{:S(2)}) copy-start(f32[6]{0:T(128)S(1)} %get-tuple-element.80) | copy-start | bytes 76
  64.8 36.5 %copy-start.133 = (f32[6]{0:T(128)}, f32[6]{0:T(128)S(1)}, u32[]{:S(2)}) copy-start(f32[6]{0:T(128)S(1)} %get-tuple-element.79) | copy-start | bytes 76
  64.8 37.4 %copy-start.129 = (f32[6]{0:T(128)}, f32[6]{0:T(128)S(1)}, u32[]{:S(2)}) copy-start(f32[6]{0:T(128)S(1)} %get-tuple-element.78) | copy-start | bytes 76
  90.2 15.8 %copy-start.14 = (f32[6,6,64,384]{3,2,1,0:T(8,128)}, f32[6,6,64,384]{3,2,1,0:T(8,128)S(1)}, u32[]{:S(2)}) copy-start(f32[6,6,64,384]{3,2,1,0:T(8,128)S(1)} %fusion.8) | copy-start | bytes 10616836
  94.9 7.3 copy-start.27
  106.0 6.3 copy-start.35
  158.8 161.3 %reduce-scatter.5.cloned.1.call-start = ((), (), s32[]{:S(2)}) async-start(), calls=%async_computation.7 | async-start | bytes 14155776 | tf_op jit(solution)/shard_map/reduce_scatter | solution.py:241
  204.6 5.5 copy-start.87
  204.6 5.5 copy-start.139
  204.6 6.5 copy-start.145
  227.6 314.3 %all-reduce.40.cloned.1.call-start = ((), (), s32[]{:S(2)}) async-start(), calls=%async_computation.9 | async-start | bytes 12582912 | tf_op jit(solution)/shard_map/psum | solution.py:331
  232.1 7.0 copy-start.71
  351.7 6.3 copy-start.29
  351.7 6.3 copy-start.52
  351.7 8.6 %copy-start.50 = (f32[6,6,128,128]{3,2,1,0:T(8,128)S(1)}, f32[6,6,128,128]{3,2,1,0:T(8,128)}, u32[]{:S(2)}) copy-start(f32[6,6,128,128]{3,2,1,0:T(8,128)} %copy-done.49) | copy-start | bytes 7077892
  385.9 221.5 %reduce-scatter.7.cloned.1.call-start = ((), (), s32[]{:S(2)}) async-start(), calls=%async_computation.8 | async-start | bytes 7077888 | tf_op jit(solution)/shard_map/reduce_scatter | solution.py:250
  398.1 7.2 copy-start.66
  431.0 206.5 %reduce-scatter.11.cloned.1.call-start = ((), (), s32[]{:S(2)}) async-start(), calls=%async_computation.12 | async-start | bytes 901120 | tf_op jit(solution)/shard_map/reduce_scatter | solution.py:255
  448.6 7.9 slice-start.2
  451.1 5.4 slice-start.3
  490.3 6.6 slice-start.6
  491.6 5.6 slice-start
  491.6 5.6 slice-start.1
  491.6 5.8 slice-start.7
  491.6 6.6 copy-start.61
  498.2 6.2 copy-start.109
  510.8 157.1 %reduce-scatter.9.cloned.1.call-start = ((), (), s32[]{:S(2)}) async-start(), calls=%async_computation.11 | async-start | bytes 1802240 | tf_op jit(solution)/shard_map/reduce_scatter | solution.py:252
  518.6 315.6 %all-reduce.42.cloned.1.call-start = ((), (), s32[]{:S(2)}) async-start(), calls=%async_computation.10 | async-start | bytes 12582912 | tf_op jit(solution)/shard_map/psum | solution.py:331
  634.5 1.3 collective-permute-start
  635.9 41.1 %collective-permute-start.1 = (f32[26892]{0:T(1024)S(1)}, f32[26892]{0:T(1024)S(1)}, u32[]{:S(2)}, u32[]{:S(2)}) collective-permute-start(f32[26892]{0:T(1024)S(1)} %add.277), channel_id=1, source_target_pairs={{0,2},{1,3},{2,0},{3,1},{4,6},{5,7},{6,4},{7,5},{8,10},{9,11},{10,... | collective-permute-start | bytes 322712 | tf_op jit(solution)/shard_map/ppermute | solution.py:322
  669.8 8.7 %copy-start.122 = (f32[384]{0:T(512)S(1)}, f32[384]{0:T(512)}, u32[]{:S(2)}) copy-start(f32[384]{0:T(512)} %copy-done.121) | copy-start | bytes 4612
  677.0 7.0 collective-permute-start.2
  684.0 7.3 collective-permute-start.3
  684.1 7.6 copy-start.25
  684.1 7.5 copy-start.90
  691.3 9.2 %collective-permute-start.4 = (f32[26892]{0:T(1024)S(1)}, f32[26892]{0:T(1024)S(1)}, u32[]{:S(2)}, u32[]{:S(2)}) collective-permute-start(f32[26892]{0:T(1024)S(1)} %add.280), channel_id=1, source_target_pairs={{0,16},{8,24},{16,0},{24,8},{1,17},{9,25},{17,1},{25,9},{2,18},{10... | collective-permute-start | bytes 322712 | tf_op jit(solution)/shard_map/ppermute | solution.py:322
  834.3 9.4 %copy-start.1 = (bf16[1536,1024]{1,0:T(8,128)(2,1)S(1)}, bf16[1536,1024]{1,0:T(8,128)(2,1)}, u32[]{:S(2)}) copy-start(bf16[1536,1024]{1,0:T(8,128)(2,1)} %param.25) | copy-start | bytes 9437188
  (121 other events, 388.2 us)
Sparse Core Ops, SparseCore 0:
  9.6 38.3 all-gather.3
  49.8 43.5 all-gather.5
  158.9 45.6 all-gather.7
  227.7 92.2 reduce-scatter.4
  386.0 155.9 all-reduce.39
  545.7 61.5 reduce-scatter.6
  610.2 22.9 reduce-scatter.10
  635.5 32.3 reduce-scatter.8
  674.2 160.0 all-reduce.41

commit v3 on v2

--- a/solution.py
+++ b/solution.py
@@ -50,7 +50,6 @@
 
 def _unit_lower_inverse_fwd_impl(strict_part):
     n = strict_part.shape[-1]
-    lead = strict_part.shape[:-2]
     nb = n // LEAF
     eye = jnp.eye(LEAF, dtype=strict_part.dtype)
     diag = jnp.stack(
@@ -187,7 +186,7 @@
     return (grad_gate_pre, grad_up, grad_gate_up)
 
 
-def per_device(
+def per_device_body(
     tokens,
     segment_ids,
     gain_in,
@@ -228,6 +227,7 @@
         (mixed, gate_up_rows, down_rows, cot_all)
     )
     middle = residual_in + jnp.dot(mixed, w_out, preferred_element_type=jnp.float32)
+    middle_out = lax.optimization_barrier(middle)
     normed_mf, norm_mid_back = jax.vjp(rms_scale, middle, gain_mid)
     normed_mid = normed_mf.astype(jnp.bfloat16)
     normed_all = lax.all_gather(normed_mid, "col", axis=0, tiled=True)
@@ -238,15 +238,11 @@
     grad_hidden = contract_cols(cot_all, down_rows)
     grad_gate_pre, grad_up, grad_gu_part = swiglu_grads(normed_all, gate_pre, up_proj, grad_hidden)
     grad_down_part = contract_rows(hidden, cot_all)
-    grad_normed_mid = lax.psum_scatter(
-        contract_cols(grad_gate_pre, gate_up_rows[0]) + contract_cols(grad_up, gate_up_rows[1]),
-        "col",
-        scatter_dimension=0,
-        tiled=True,
-    )
-    grad_normed_mid, ffn_part, grad_gu_part, grad_down_part = lax.optimization_barrier(
-        (grad_normed_mid, ffn_part, grad_gu_part, grad_down_part)
-    )
+    grad_nm_part = (
+        contract_cols(grad_gate_pre, gate_up_rows[0]) + contract_cols(grad_up, gate_up_rows[1])
+    ).astype(jnp.bfloat16)
+    grad_normed_mid = lax.psum_scatter(grad_nm_part, "col", scatter_dimension=0, tiled=True)
+    grad_normed_mid = grad_normed_mid.astype(jnp.float32)
     ffn_out = lax.psum_scatter(ffn_part, "col", scatter_dimension=0, tiled=True)
     grad_gate_up, grad_down = (
         lax.psum_scatter(
@@ -267,12 +263,11 @@
     grad_raw_b = grad_raw.astype(jnp.bfloat16)
     grad_logits_b = grad_logits.astype(jnp.bfloat16)
     grad_gate_b = grad_gate_out.astype(jnp.bfloat16)
-    ffn_out, grad_raw_b = lax.optimization_barrier((ffn_out, grad_raw_b))
-    block_out = (middle + ffn_out.astype(jnp.float32)).astype(jnp.bfloat16)
     grad_qkv = contract_rows(normed_in, grad_raw_b)
     grad_decay = contract_rows(normed_in, grad_logits_b)
     grad_gate_o = contract_rows(normed_in, grad_gate_b)
     early = summed_bf16((grad_out, grad_gate_o))
+    block_out = (middle_out + ffn_out.astype(jnp.float32)).astype(jnp.bfloat16)
     grad_normed_in = (
         contract_cols(grad_raw_b, w_qkv)
         + contract_cols(grad_logits_b, w_decay)
@@ -366,5 +361,5 @@
         P("col", "row"),
     )
     return jax.shard_map(
-        per_device, mesh=mesh, in_specs=in_specs, out_specs=out_specs, check_vma=False
-    )
+        per_device_body, mesh=mesh, in_specs=in_specs, out_specs=out_specs, check_vma=False
+    )

time: 862 us -> 808 us (0.937)
  waiting for transfers between devices: 340 us -> 302 us
  matrix products: 242 us -> 222 us
    reduce_scatter x4, waiting for transfers between devices: 137 us -> 101 us  [the longest x1 61.8 us: per_device_body(): lax.psum_scatter(grad_nm_part, 'col', scatter_dimension=0, tiled=True)]
    concatenate x1, other arithmetic: 8.03 us -> 23.2 us  [summed_bf16(): flat = jnp.concatenate([p.astype(jnp.bfloat16).reshape(-1) for p in parts])]
    ppermute x5, waiting for transfers between devices: 18.1 us -> 5.52 us  [summed_f32(): flat = flat + lax.ppermute(flat, axis, [(i, i ^ step) for i in range(n)])]
    unnamed x326 -> x382, local copies, waits for them, and re-layouts: 27.2 us -> 30.9 us
  transfers between devices with their start and end apart: 14 -> 14, of which waited for: 10 -> 8; matrix products, arithmetic and copies ran while one was open for 42% -> 44% of each run, Pallas kernels for 0% -> 0%
where the time goes in v3:
time: 808 us; the launch traced here: 800 us
  waiting for transfers between devices  302 us (37%)
  matrix products  222 us (27%)
  local copies, waits for them, and re-layouts  124 us (15%)
  other arithmetic  108 us (13%)
  blocking collectives  20.8 us (3%)
  between operations  16.6 us (2%)
    psum x2, waiting for transfers between devices, summed_bf16(): return split_flat(lax.psum(flat, ('row', 'col')), parts)  148 us
    reduce_scatter x1, waiting for transfers between devices, per_device_body(): lax.psum_scatter(grad_nm_part, 'col', scatter_dimension=0, tiled=True)  61.8 us
    all_gather x1, waiting for transfers between devices, per_device_body(): normed_all = lax.all_gather(normed_mid, 'col', axis=0, tiled=True)  45.8 us
    reduce_scatter x1, waiting for transfers between devices, per_device_body(): ffn_out = lax.psum_scatter(ffn_part, 'col', scatter_dimension=0, tiled=True)  39.5 us
    dot_general x7, matrix products, contract_cols(): lax.dot_general(left, right, (((1,), (1,)), ((), ())), preferred_element_...  31.9 us
    dot_general x7, matrix products, contract_rows(): lax.dot_general(left, right, (((0,), (0,)), ((), ())), preferred_element_...  31.1 us
    unnamed x382, local copies, waits for them, and re-layouts  30.9 us
    convert_element_type x3, local copies, waits for them, and re-layouts, split_flat(): out.append(total[at:at + p.size].reshape(p.shape).astype(jnp.float32))  24.7 us
  transfers between devices with their start and end apart: 14, of which 8 were waited for; matrix products, arithmetic and copies ran while one was open for 44% of the time, Pallas kernels for 0%

profile of v3, /device:TPU:0, one launch (start us, length us, event | category | flops | bytes accessed | tf_op | source)
XLA Modules:
  0.0 799.6 jit_solution(10248799651432655640)
XLA Ops:
  13.7 5.0 fusion.238
  18.9 6.2 fusion.5
  42.3 3.9 reshape.444
  60.4 3.6 fusion.75
  89.9 3.5 fusion.8
  93.5 4.6 fusion.25
  98.2 4.2 fusion.99
  115.0 4.1 multiply_reduce_fusion.7
  128.4 20.8 %all_gather.13 = bf16[352,1024]{1,0:T(8,128)(2,1)} all-gather(bf16[352,256]{1,0:T(8,128)(2,1)S(1)} %copy-done.107), channel_id=1, replica_groups=mesh['row'=4,'col'=8] {'row'}, dimensions={1}, use_global_device_ids=true | all-gather | bytes 901120 | tf_op jit(solution)/shard_map/all_gather | solution.py:223
  149.2 4.3 multiply_convert_fusion.3
  158.8 45.8 %all-gather.8.cloned.1.call-done = bf16[3072,1024]{1,0:T(8,128)(2,1)} async-done(((bf16[384,1024]{1,0:T(8,128)(2,1)}), bf16[3072,1024]{1,0:T(8,128)(2,1)}) %all-gather.8.cloned.1.call-update) | async-done | bytes 6291472 | tf_op jit(solution)/shard_map/all_gather | solution.py:233
  204.7 5.5 fusion.120
  212.7 5.7 multiply_convert_fusion
  221.9 6.7 add_convert_fusion
  228.7 61.8 %reduce-scatter.7.cloned.1.call-done = bf16[384,1024]{1,0:T(8,128)(2,1)} async-done(((bf16[3072,1024]{1,0:T(8,128)(2,1)}), bf16[384,1024]{1,0:T(8,128)(2,1)}) %reduce-scatter.7.cloned.1.call-update) | async-done | bytes 786448 | tf_op jit(solution)/shard_map/reduce_scatter | solution.py:244
  300.0 3.8 fusion.172
  304.8 4.3 convolution_convert_fusion.1
  309.0 6.1 reshape.460
  317.8 23.2 %pad_maximum_fusion = bf16[3145728]{0:T(1024)(128)(2,1)} fusion(bf16[1572864]{0:T(1024)(128)(2,1)S(1)} %reshape.460, bf16[1572864]{0:T(1024)(128)(2,1)S(1)} %bitcast.395), kind=kLoop, calls=%fused_computation.2 | loop fusion | flops 12582912 | bytes 12582912 | tf_op jit(solution)/shard_map/concatenate | solution.py:323
  341.1 6.8 convolution_convert_fusion.5
  348.2 5.3 fusion.68
  353.6 5.3 fusion.67
  363.8 7.0 convolution_convert_fusion
  372.7 3.8 fusion.257
  376.5 4.0 mul.830
  380.6 3.9 multiply_reduce_fusion.4
  384.5 4.0 multiply_reduce_fusion.5
  393.5 5.0 fusion.19
  398.6 4.5 convolution_add_fusion
  416.5 4.8 fusion.9
  426.1 5.1 fusion.46
  431.2 4.8 fusion.6
  436.0 3.7 fusion.7
  446.4 4.5 fusion.86
  459.7 7.3 multiply_reduce_fusion.9
  474.2 6.4 broadcast_multiply_fusion
  507.0 6.6 multiply_reduce_fusion.3
  520.1 4.6 convert_bitcast_fusion
  524.7 4.6 copy.197
  530.6 6.9 slice_convert_fusion
  537.5 7.1 reshape.463
  544.6 10.3 %convert_element_type.146 = bf16[1024,3072]{1,0:T(8,128)(2,1)} reshape(bf16[3145728]{0:T(1024)(128)(2,1)} %bitcast.392) | data formatting | bytes 12582912 | tf_op jit(solution)/shard_map/convert_element_type | solution.py:303
  555.4 5.8 fusion.256
  571.7 3.6 collective-permute-done.2
  582.5 39.5 %reduce-scatter.5.cloned.1.call-done = bf16[384,1024]{1,0:T(8,128)(2,1)} async-done(((bf16[3072,1024]{1,0:T(8,128)(2,1)}), bf16[384,1024]{1,0:T(8,128)(2,1)}) %reduce-scatter.5.cloned.1.call-update) | async-done | bytes 786448 | tf_op jit(solution)/shard_map/reduce_scatter | solution.py:246
  628.1 7.3 reshape.464
  635.5 148.0 %all-reduce.42.cloned.1.call-done = bf16[1024,3072]{1,0:T(8,128)(2,1)} async-done(((bf16[1024,3072]{1,0:T(8,128)(2,1)}), bf16[1024,3072]{1,0:T(8,128)(2,1)}) %all-reduce.42.cloned.1.call-update) | async-done | bytes 6291472 | tf_op jit(solution)/shard_map/psum | solution.py:326
  783.5 9.4 %convert_element_type.147 = f32[1024,3072]{1,0:T(8,128)} convert(bf16[1024,3072]{1,0:T(8,128)(2,1)} %all-reduce.42.cloned.1.call-done) | non-fusion elementwise | flops 3145728 | bytes 18874368 | tf_op jit(solution)/shard_map/convert_element_type | solution.py:303
  (589 shorter events, 220.0 us)
Async XLA Ops:
  7.2 146.3 %copy-start = (bf16[1536,1024]{1,0:T(8,128)(2,1)S(1)}, bf16[1536,1024]{1,0:T(8,128)(2,1)}, u32[]{:S(2)}) copy-start(bf16[1536,1024]{1,0:T(8,128)(2,1)} %param.25) | copy-start | bytes 9437188
  7.2 146.3 %all-gather.4.cloned.1.call-start = ((), (), s32[]{:S(2)}) async-start(), calls=%async_computation.4 | async-start | bytes 1802240 | tf_op jit(solution)/shard_map/all_gather | solution.py:222
  8.0 145.5 %all-gather.6.cloned.1.call-start = ((), (), s32[]{:S(2)}) async-start(), calls=%async_computation.5 | async-start | bytes 7077888 | tf_op jit(solution)/shard_map/all_gather | solution.py:225
  8.7 196.0 %all-gather.8.cloned.1.call-start = ((), (), s32[]{:S(2)}) async-start(), calls=%async_computation.6 | async-start | bytes 7077888 | tf_op jit(solution)/shard_map/all_gather | solution.py:233
  10.9 43.9 %copy-start.105 = (pred[64,64]{0,1:T(8,128)(4,1)}, pred[64,64]{0,1:T(8,128)(4,1)S(1)}, u32[]{:S(2)}) copy-start(pred[64,64]{0,1:T(8,128)(4,1)S(1)} %iota_compare_fusion.3) | copy-start | bytes 12292
  40.3 11.1 %copy-start.127 = (f32[6,64]{1,0:T(8,128)}, f32[6,64]{1,0:T(8,128)S(1)}, u32[]{:S(2)}) copy-start(f32[6,64]{1,0:T(8,128)S(1)} %compare_convert_fusion) | copy-start | bytes 4612
  42.2 9.3 %copy-start.100 = (f32[6,64,6]{1,0,2:T(8,128)}, f32[6,64,6]{1,0,2:T(8,128)S(1)}, u32[]{:S(2)}) copy-start(f32[6,64,6]{1,0,2:T(8,128)S(1)} %reshape.441) | copy-start | bytes 27652
  42.2 44.8 %copy-start.86 = (f32[6,64,6]{1,2,0:T(8,128)}, f32[6,64,6]{1,2,0:T(8,128)S(1)}, u32[]{:S(2)}) copy-start(f32[6,64,6]{1,2,0:T(8,128)S(1)} %copy.242) | copy-start | bytes 27652
  42.3 72.6 %copy-start.73 = (pred[6,64,64]{1,2,0:T(8,128)(4,1)}, pred[6,64,64]{1,2,0:T(8,128)(4,1)S(1)}, u32[]{:S(2)}) copy-start(pred[6,64,64]{1,2,0:T(8,128)(4,1)S(1)} %compare_and_fusion) | copy-start | bytes 73732
  48.2 63.7 %copy-start.95 = (f32[6,64,6]{1,2,0:T(8,128)}, f32[6,64,6]{1,2,0:T(8,128)S(1)}, u32[]{:S(2)}) copy-start(f32[6,64,6]{1,2,0:T(8,128)S(1)} %copy.109) | copy-start | bytes 27652
  51.5 63.5 %copy-start.51 = (f32[6,6,64]{2,1,0:T(8,128)}, f32[6,6,64]{2,1,0:T(8,128)S(1)}, u32[]{:S(2)}) copy-start(f32[6,6,64]{2,1,0:T(8,128)S(1)} %reduce_window_sum.22) | copy-start | bytes 27652
  51.5 63.5 %copy-start.89 = (f32[6,6,64]{2,1,0:T(8,128)}, f32[6,6,64]{2,1,0:T(8,128)S(1)}, u32[]{:S(2)}) copy-start(f32[6,6,64]{2,1,0:T(8,128)S(1)} %get-tuple-element.78) | copy-start | bytes 27652
  66.8 36.5 %copy-start.150 = (f32[6]{0:T(128)}, f32[6]{0:T(128)S(1)}, u32[]{:S(2)}) copy-start(f32[6]{0:T(128)S(1)} %get-tuple-element.68) | copy-start | bytes 76
  66.9 37.4 %copy-start.152 = (f32[6]{0:T(128)}, f32[6]{0:T(128)S(1)}, u32[]{:S(2)}) copy-start(f32[6]{0:T(128)S(1)} %get-tuple-element.67) | copy-start | bytes 76
  66.9 38.4 %copy-start.148 = (f32[6]{0:T(128)}, f32[6]{0:T(128)S(1)}, u32[]{:S(2)}) copy-start(f32[6]{0:T(128)S(1)} %get-tuple-element.66) | copy-start | bytes 76
  84.7 13.4 %copy-start.97 = (f32[6,6,64]{2,1,0:T(8,128)}, f32[6,6,64]{2,1,0:T(8,128)S(1)}, u32[]{:S(2)}) copy-start(f32[6,6,64]{2,1,0:T(8,128)S(1)} %slice_reduce_fusion) | copy-start | bytes 27652
  93.5 15.6 %copy-start.9 = (f32[6,6,64,384]{3,2,1,0:T(8,128)}, f32[6,6,64,384]{3,2,1,0:T(8,128)S(1)}, u32[]{:S(2)}) copy-start(f32[6,6,64,384]{3,2,1,0:T(8,128)S(1)} %fusion.8) | copy-start | bytes 10616836
  98.1 7.1 copy-start.20
  119.1 261.4 %copy-start.99 = (f32[6,64,6]{1,2,0:T(8,128)}, f32[6,64,6]{1,2,0:T(8,128)S(1)}, u32[]{:S(2)}) copy-start(f32[6,64,6]{1,2,0:T(8,128)S(1)} %fusion.184) | copy-start | bytes 27652
  124.0 25.2 %copy-start.164 = (bf16[1024,1536]{1,0:T(8,128)(2,1)S(1)}, bf16[1024,1536]{1,0:T(8,128)(2,1)}, u32[]{:S(2)}) copy-start(bf16[1024,1536]{1,0:T(8,128)(2,1)} %param.23) | copy-start | bytes 9437188
  127.2 21.9 %copy-start.57 = (bf16[384,1024]{1,0:T(8,128)(2,1)S(1)}, bf16[384,1024]{1,0:T(8,128)(2,1)}, u32[]{:S(2)}) copy-start(bf16[384,1024]{1,0:T(8,128)(2,1)} %param.15) | copy-start | bytes 2359300
  127.3 21.9 %copy-start.77 = (f32[384,1536]{1,0:T(8,128)S(1)}, f32[384,1536]{1,0:T(8,128)}, u32[]{:S(2)}) copy-start(f32[384,1536]{1,0:T(8,128)} %copy.132) | copy-start | bytes 7077892
  128.4 20.8 %copy-start.79 = (f32[48,8,6,256]{3,1,2,0:T(8,128)}, f32[48,8,6,256]{3,1,2,0:T(8,128)S(1)}, u32[]{:S(2)}) copy-start(f32[48,8,6,256]{3,1,2,0:T(8,128)S(1)} %copy.192) | copy-start | bytes 7077892
  158.8 131.8 %reduce-scatter.7.cloned.1.call-start = ((), (), s32[]{:S(2)}) async-start(), calls=%async_computation.8 | async-start | bytes 7077888 | tf_op jit(solution)/shard_map/reduce_scatter | solution.py:244
  204.7 8.0 %slice-start.10 = ((s8[6291456]{0:T(1024)(128)(4,1)}), s8[4194304]{0:T(1024)(128)(4,1)S(1)}, s32[]{:S(2)}) async-start(s8[6291456]{0:T(1024)(128)(4,1)} %bitcast.448), calls=%async_computation.23 | async-start | bytes 8388608
  228.7 302.0 %all-reduce.40.cloned.1.call-start = ((), (), s32[]{:S(2)}) async-start(), calls=%async_computation.9 | async-start | bytes 12582912 | tf_op jit(solution)/shard_map/psum | solution.py:326
  341.1 225.4 %reduce-scatter.11.cloned.1.call-start = ((), (), s32[]{:S(2)}) async-start(), calls=%async_computation.12 | async-start | bytes 901120 | tf_op jit(solution)/shard_map/reduce_scatter | solution.py:251
  341.1 7.1 copy-start.56
  348.0 220.2 %reduce-scatter.9.cloned.1.call-start = ((), (), s32[]{:S(2)}) async-start(), calls=%async_computation.11 | async-start | bytes 1802240 | tf_op jit(solution)/shard_map/reduce_scatter | solution.py:248
  360.2 261.7 %reduce-scatter.5.cloned.1.call-start = ((), (), s32[]{:S(2)}) async-start(), calls=%async_computation.7 | async-start | bytes 7077888 | tf_op jit(solution)/shard_map/reduce_scatter | solution.py:246
  370.8 412.7 %all-reduce.42.cloned.1.call-start = ((), (), s32[]{:S(2)}) async-start(), calls=%async_computation.10 | async-start | bytes 12582912 | tf_op jit(solution)/shard_map/psum | solution.py:326
  391.0 59.8 %copy-start.29 = (f32[6,6,64,64]{2,3,1,0:T(8,128)}, f32[6,6,64,64]{2,3,1,0:T(8,128)S(1)}, u32[]{:S(2)}) copy-start(f32[6,6,64,64]{2,3,1,0:T(8,128)S(1)} %fusion.255) | copy-start | bytes 1769476
  416.5 9.5 %slice-start.2 = ((s8[4718592]{0:T(1024)(128)(4,1)}), s8[4194304]{0:T(1024)(128)(4,1)S(1)}, s32[]{:S(2)}) async-start(s8[4718592]{0:T(1024)(128)(4,1)} %bitcast.386), calls=%async_computation.15 | async-start | bytes 8388608
  459.7 7.3 copy-start.53
  459.7 7.3 copy-start.72
  459.7 7.3 copy-start.75
  459.7 7.3 copy-start.88
  467.0 7.2 slice-start.4
  494.2 7.9 slice-start.6
  563.9 7.8 copy-start.139
  564.0 1.3 collective-permute-start
  565.3 5.2 collective-permute-start.1
  568.2 8.6 %copy-start.63 = (f32[384,1024]{1,0:T(8,128)S(1)}, f32[384,1024]{1,0:T(8,128)}, u32[]{:S(2)}) copy-start(f32[384,1024]{1,0:T(8,128)} %get-tuple-element.154) | copy-start | bytes 4718596
  570.5 4.8 collective-permute-start.2
  575.3 4.8 collective-permute-start.3
  576.7 45.2 %copy-start.19 = (f32[384,1024]{1,0:T(8,128)S(1)}, f32[384,1024]{1,0:T(8,128)}, u32[]{:S(2)}) copy-start(f32[384,1024]{1,0:T(8,128)} %copy-done.17) | copy-start | bytes 4718596
  580.2 44.0 %collective-permute-start.4 = (f32[26892]{0:T(1024)S(1)}, f32[26892]{0:T(1024)S(1)}, u32[]{:S(2)}, u32[]{:S(2)}) collective-permute-start(f32[26892]{0:T(1024)S(1)} %add.280), channel_id=1, source_target_pairs={{0,16},{8,24},{16,0},{24,8},{1,17},{9,25},{17,1},{25,9},{2,18},{10... | collective-permute-start | bytes 322712 | tf_op jit(solution)/shard_map/ppermute | solution.py:317
  783.5 9.4 %copy-start.1 = (bf16[1536,1024]{1,0:T(8,128)(2,1)S(1)}, bf16[1536,1024]{1,0:T(8,128)(2,1)}, u32[]{:S(2)}) copy-start(bf16[1536,1024]{1,0:T(8,128)(2,1)} %param.25) | copy-start | bytes 9437188
  (149 other events, 482.5 us)
Sparse Core Ops, SparseCore 0:
  9.6 38.3 all-gather.3
  49.8 43.5 all-gather.5
  158.9 45.7 all-gather.7
  228.8 61.7 reduce-scatter.6
  341.2 155.9 all-reduce.39
  499.9 22.8 reduce-scatter.10
  525.0 32.3 reduce-scatter.8
  561.4 60.5 reduce-scatter.4
  627.6 155.8 all-reduce.41

commit v4 on v3

--- a/solution.py
+++ b/solution.py
@@ -243,14 +243,10 @@
     ).astype(jnp.bfloat16)
     grad_normed_mid = lax.psum_scatter(grad_nm_part, "col", scatter_dimension=0, tiled=True)
     grad_normed_mid = grad_normed_mid.astype(jnp.float32)
-    ffn_out = lax.psum_scatter(ffn_part, "col", scatter_dimension=0, tiled=True)
+    ffn_out = summed_by_exchange(ffn_part, "col", 0)
     grad_gate_up, grad_down = (
-        lax.psum_scatter(
-            grad_gu_part.astype(jnp.bfloat16), "row", scatter_dimension=1, tiled=True
-        ).astype(jnp.float32),
-        lax.psum_scatter(
-            grad_down_part.astype(jnp.bfloat16), "row", scatter_dimension=1, tiled=True
-        ).astype(jnp.float32),
+        summed_by_exchange(grad_gu_part.astype(jnp.bfloat16), "row", 1),
+        summed_by_exchange(grad_down_part.astype(jnp.bfloat16), "row", 1),
     )
     grad_mid_norm, grad_gain_mid = norm_mid_back(grad_normed_mid)
     grad_middle = cotangent.astype(jnp.float32) + grad_mid_norm
@@ -267,7 +263,7 @@
     grad_decay = contract_rows(normed_in, grad_logits_b)
     grad_gate_o = contract_rows(normed_in, grad_gate_b)
     early = summed_bf16((grad_out, grad_gate_o))
-    block_out = (middle_out + ffn_out.astype(jnp.float32)).astype(jnp.bfloat16)
+    block_out = (middle_out + ffn_out).astype(jnp.bfloat16)
     grad_normed_in = (
         contract_cols(grad_raw_b, w_qkv)
         + contract_cols(grad_logits_b, w_decay)
@@ -297,6 +293,14 @@
     )
 
 
+def summed_by_exchange(part, axis, dim):
+    n = lax.axis_size(axis)
+    shape = part.shape
+    pieces = part.reshape(shape[:dim] + (n, shape[dim] // n) + shape[dim + 1 :])
+    got = lax.all_to_all(pieces, axis, dim, dim, tiled=False)
+    return jnp.sum(got.astype(jnp.float32), axis=dim)
+
+
 def split_flat(total, parts):
     out, at = [], 0
     for p in parts:

time: 808 us -> 839 us (1.038)
  starting transfers between devices: 6.58 us -> 22.1 us
  local copies, waits for them, and re-layouts: 124 us -> 135 us
    psum x2, waiting for transfers between devices: 148 us -> 236 us  [summed_bf16(): return split_flat(lax.psum(flat, ('row', 'col')), parts)]
    reduce_scatter x1, waiting for transfers between devices: 61.8 us -> 5.78 us  [per_device_body(): lax.psum_scatter(grad_nm_part, 'col', scatter_dimension=0, tiled=True)]
    reduce_scatter x3 -> x0, waiting for transfers between devices: 39.5 us -> none  [the longest x1 39.5 us: per_device_body(): ffn_out = lax.psum_scatter(ffn_part, 'col', scatter_dimension=0, tiled=True)]
    all_to_all x0 -> x3, starting transfers between devices: none -> 14.5 us  [summed_by_exchange(): got = lax.all_to_all(pieces, axis, dim, dim, tiled=False)]
    ppermute x5, waiting for transfers between devices: 5.52 us -> 17.3 us  [summed_f32(): flat = flat + lax.ppermute(flat, axis, [(i, i ^ step) for i in range(n)])]
    reduce_sum x0 -> x3, other arithmetic: none -> 9.19 us  [summed_by_exchange(): return jnp.sum(got.astype(jnp.float32), axis=dim)]
    another operation x0 -> x4, local copies, waits for them, and re-layouts: none -> 8.49 us  [swiglu_grads(): jnp.stack([contract_rows(normed_rows, grad_gate_pre), contract_rows(norme...]
    unnamed x382 -> x374, local copies, waits for them, and re-layouts: 30.9 us -> 29.6 us
  transfers between devices with their start and end apart: 14 -> 14, of which waited for: 8 -> 8; matrix products, arithmetic and copies ran while one was open for 44% -> 49% of each run, Pallas kernels for 0% -> 0%
where the time goes in v4:
time: 839 us; the launch traced here: 831 us
  waiting for transfers between devices  306 us (36%)
  matrix products  219 us (26%)
  local copies, waits for them, and re-layouts  135 us (16%)
  other arithmetic  110 us (13%)
  starting transfers between devices  22.1 us (3%)
  blocking collectives  21.1 us (3%)
  between operations  16.8 us (2%)
    psum x2, waiting for transfers between devices, summed_bf16(): return split_flat(lax.psum(flat, ('row', 'col')), parts)  236 us
    all_gather x1, waiting for transfers between devices, per_device_body(): normed_all = lax.all_gather(normed_mid, 'col', axis=0, tiled=True)  45.6 us
    dot_general x7, matrix products, contract_rows(): lax.dot_general(left, right, (((0,), (0,)), ((), ())), preferred_element_...  32.3 us
    dot_general x7, matrix products, contract_cols(): lax.dot_general(left, right, (((1,), (1,)), ((), ())), preferred_element_...  30.7 us
    unnamed x374, local copies, waits for them, and re-layouts  29.6 us
    convert_element_type x3, local copies, waits for them, and re-layouts, split_flat(): out.append(total[at:at + p.size].reshape(p.shape).astype(jnp.float32))  24.6 us
    concatenate x1, other arithmetic, summed_bf16(): flat = jnp.concatenate([p.astype(jnp.bfloat16).reshape(-1) for p in parts])  23.6 us
    all_gather x1, blocking collectives, per_device_body(): lax.all_gather(w_down, 'row', axis=1, tiled=True)  21.1 us
  transfers between devices with their start and end apart: 14, of which 8 were waited for; matrix products, arithmetic and copies ran while one was open for 49% of the time, Pallas kernels for 0%

profile of v4, /device:TPU:0, one launch (start us, length us, event | category | flops | bytes accessed | tf_op | source)
XLA Modules:
  0.0 830.6 jit_solution(15170718910475666356)
XLA Ops:
  13.7 5.0 fusion.236
  19.5 6.9 fusion.5
  43.8 3.9 reshape.457
  94.9 4.6 fusion.25
  99.6 4.2 fusion.97
  116.4 4.1 multiply_reduce_fusion.7
  130.0 21.1 %all_gather.13 = bf16[352,1024]{1,0:T(8,128)(2,1)} all-gather(bf16[352,256]{1,0:T(8,128)(2,1)S(1)} %copy-done.107), channel_id=1, replica_groups=mesh['row'=4,'col'=8] {'row'}, dimensions={1}, use_global_device_ids=true | all-gather | bytes 901120 | tf_op jit(solution)/shard_map/all_gather | solution.py:223
  160.0 45.6 %all-gather.8.cloned.1.call-done = bf16[3072,1024]{1,0:T(8,128)(2,1)} async-done(((bf16[384,1024]{1,0:T(8,128)(2,1)}), bf16[3072,1024]{1,0:T(8,128)(2,1)}) %all-gather.8.cloned.1.call-update) | async-done | bytes 6291472 | tf_op jit(solution)/shard_map/all_gather | solution.py:233
  205.6 5.5 fusion.118
  213.7 5.8 multiply_convert_fusion
  223.0 6.7 add_convert_fusion
  236.2 7.0 convolution_convert_fusion.5
  244.1 4.6 all-to-all-start.2
  248.7 6.7 convolution_convert_fusion.4
  260.1 6.8 convolution_convert_fusion.3
  273.2 5.4 convolution_convert_fusion
  278.6 5.1 all-to-all-start.1
  285.9 5.8 reduce-scatter.2.cloned.1.call-done
  301.1 4.1 fusion.170
  305.2 4.0 mul.830
  309.2 3.9 multiply_reduce_fusion.4
  313.1 4.0 multiply_reduce_fusion.5
  322.1 5.0 fusion.19
  327.1 4.3 convolution_add_fusion
  344.8 4.8 fusion.9
  354.4 5.1 fusion.46
  359.5 4.8 fusion.6
  374.8 4.5 fusion.84
  388.0 7.2 multiply_reduce_fusion.9
  402.4 6.4 broadcast_multiply_fusion
  419.5 5.7 reshape.474
  427.9 23.6 %pad_maximum_fusion = bf16[3145728]{0:T(1024)(128)(2,1)} fusion(bf16[1572864]{0:T(1024)(128)(2,1)S(1)} %reshape.474, bf16[1572864]{0:T(1024)(128)(2,1)S(1)} %bitcast.400), kind=kLoop, calls=%fused_computation.3 | loop fusion | flops 12582912 | bytes 12582912 | tf_op jit(solution)/shard_map/concatenate | solution.py:327
  471.7 6.9 multiply_reduce_fusion.3
  483.8 4.1 convert_bitcast_fusion
  488.0 4.6 copy.201
  492.6 5.1 fusion.254
  497.7 4.8 all-to-all-start
  502.5 126.3 %all-reduce.40.cloned.1.call-done = bf16[3145728]{0:T(1024)(128)(2,1)} async-done(((bf16[3145728]{0:T(1024)(128)(2,1)}), bf16[3145728]{0:T(1024)(128)(2,1)}) %all-reduce.40.cloned.1.call-update) | async-done | bytes 6291472 | tf_op jit(solution)/shard_map/psum | solution.py:330
  628.8 6.8 slice_convert_fusion
  635.6 7.1 reshape.478
  642.7 10.3 %convert_element_type.147 = bf16[1024,3072]{1,0:T(8,128)(2,1)} reshape(bf16[3145728]{0:T(1024)(128)(2,1)} %bitcast.397) | data formatting | bytes 12582912 | tf_op jit(solution)/shard_map/convert_element_type | solution.py:307
  662.9 4.6 convert_reduce_fusion
  672.1 4.1 collective-permute-done.2
  678.1 5.5 collective-permute-done.3
  687.3 6.0 collective-permute-done.4
  697.2 7.2 reshape.479
  704.4 109.8 %all-reduce.42.cloned.1.call-done = bf16[1024,3072]{1,0:T(8,128)(2,1)} async-done(((bf16[1024,3072]{1,0:T(8,128)(2,1)}), bf16[1024,3072]{1,0:T(8,128)(2,1)}) %all-reduce.42.cloned.1.call-update) | async-done | bytes 6291472 | tf_op jit(solution)/shard_map/psum | solution.py:330
  814.2 9.4 %convert_element_type.148 = f32[1024,3072]{1,0:T(8,128)} convert(bf16[1024,3072]{1,0:T(8,128)(2,1)} %all-reduce.42.cloned.1.call-done) | non-fusion elementwise | flops 3145728 | bytes 18874368 | tf_op jit(solution)/shard_map/convert_element_type | solution.py:307
  (584 shorter events, 249.1 us)
Async XLA Ops:
  7.2 147.6 %copy-start = (bf16[1536,1024]{1,0:T(8,128)(2,1)S(1)}, bf16[1536,1024]{1,0:T(8,128)(2,1)}, u32[]{:S(2)}) copy-start(bf16[1536,1024]{1,0:T(8,128)(2,1)} %param.25) | copy-start | bytes 9437188
  7.2 147.5 %all-gather.4.cloned.1.call-start = ((), (), s32[]{:S(2)}) async-start(), calls=%async_computation.4 | async-start | bytes 1802240 | tf_op jit(solution)/shard_map/all_gather | solution.py:222
  8.0 146.8 %all-gather.6.cloned.1.call-start = ((), (), s32[]{:S(2)}) async-start(), calls=%async_computation.5 | async-start | bytes 7077888 | tf_op jit(solution)/shard_map/all_gather | solution.py:225
  8.7 196.9 %all-gather.8.cloned.1.call-start = ((), (), s32[]{:S(2)}) async-start(), calls=%async_computation.6 | async-start | bytes 7077888 | tf_op jit(solution)/shard_map/all_gather | solution.py:233
  10.9 45.0 %copy-start.105 = (pred[64,64]{0,1:T(8,128)(4,1)}, pred[64,64]{0,1:T(8,128)(4,1)S(1)}, u32[]{:S(2)}) copy-start(pred[64,64]{0,1:T(8,128)(4,1)S(1)} %iota_compare_fusion.3) | copy-start | bytes 12292
  13.5 137.6 %copy-start.131 = (f32[384]{0:T(512)}, f32[384]{0:T(512)S(1)}, u32[]{:S(2)}) copy-start(f32[384]{0:T(512)S(1)} %fusion.195) | copy-start | bytes 4612
  18.7 7.7 copy-start.2
  41.8 11.1 %copy-start.127 = (f32[6,64]{1,0:T(8,128)}, f32[6,64]{1,0:T(8,128)S(1)}, u32[]{:S(2)}) copy-start(f32[6,64]{1,0:T(8,128)S(1)} %compare_convert_fusion) | copy-start | bytes 4612
  43.6 9.3 %copy-start.100 = (f32[6,64,6]{1,0,2:T(8,128)}, f32[6,64,6]{1,0,2:T(8,128)S(1)}, u32[]{:S(2)}) copy-start(f32[6,64,6]{1,0,2:T(8,128)S(1)} %reshape.454) | copy-start | bytes 27652
  43.6 44.6 %copy-start.86 = (f32[6,64,6]{1,2,0:T(8,128)}, f32[6,64,6]{1,2,0:T(8,128)S(1)}, u32[]{:S(2)}) copy-start(f32[6,64,6]{1,2,0:T(8,128)S(1)} %copy.248) | copy-start | bytes 27652
  43.7 72.6 %copy-start.75 = (pred[6,64,64]{1,2,0:T(8,128)(4,1)}, pred[6,64,64]{1,2,0:T(8,128)(4,1)S(1)}, u32[]{:S(2)}) copy-start(pred[6,64,64]{1,2,0:T(8,128)(4,1)S(1)} %compare_and_fusion) | copy-start | bytes 73732
  49.6 63.7 %copy-start.95 = (f32[6,64,6]{1,2,0:T(8,128)}, f32[6,64,6]{1,2,0:T(8,128)S(1)}, u32[]{:S(2)}) copy-start(f32[6,64,6]{1,2,0:T(8,128)S(1)} %copy.109) | copy-start | bytes 27652
  52.9 63.5 %copy-start.51 = (f32[6,6,64]{2,1,0:T(8,128)}, f32[6,6,64]{2,1,0:T(8,128)S(1)}, u32[]{:S(2)}) copy-start(f32[6,6,64]{2,1,0:T(8,128)S(1)} %reduce_window_sum.22) | copy-start | bytes 27652
  52.9 63.5 %copy-start.89 = (f32[6,6,64]{2,1,0:T(8,128)}, f32[6,6,64]{2,1,0:T(8,128)S(1)}, u32[]{:S(2)}) copy-start(f32[6,6,64]{2,1,0:T(8,128)S(1)} %get-tuple-element.78) | copy-start | bytes 27652
  68.0 35.9 %copy-start.142 = (f32[6]{0:T(128)}, f32[6]{0:T(128)S(1)}, u32[]{:S(2)}) copy-start(f32[6]{0:T(128)S(1)} %get-tuple-element.69) | copy-start | bytes 76
  68.0 36.8 %copy-start.146 = (f32[6]{0:T(128)}, f32[6]{0:T(128)S(1)}, u32[]{:S(2)}) copy-start(f32[6]{0:T(128)S(1)} %get-tuple-element.68) | copy-start | bytes 76
  68.0 37.7 %copy-start.148 = (f32[6]{0:T(128)}, f32[6]{0:T(128)S(1)}, u32[]{:S(2)}) copy-start(f32[6]{0:T(128)S(1)} %get-tuple-element.67) | copy-start | bytes 76
  68.0 38.6 %copy-start.144 = (f32[6]{0:T(128)}, f32[6]{0:T(128)S(1)}, u32[]{:S(2)}) copy-start(f32[6]{0:T(128)S(1)} %get-tuple-element.66) | copy-start | bytes 76
  86.0 13.6 %copy-start.97 = (f32[6,6,64]{2,1,0:T(8,128)}, f32[6,6,64]{2,1,0:T(8,128)S(1)}, u32[]{:S(2)}) copy-start(f32[6,6,64]{2,1,0:T(8,128)S(1)} %slice_reduce_fusion) | copy-start | bytes 27652
  94.9 15.6 %copy-start.9 = (f32[6,6,64,384]{3,2,1,0:T(8,128)}, f32[6,6,64,384]{3,2,1,0:T(8,128)S(1)}, u32[]{:S(2)}) copy-start(f32[6,6,64,384]{3,2,1,0:T(8,128)S(1)} %fusion.8) | copy-start | bytes 10616836
  120.6 188.6 %copy-start.99 = (f32[6,64,6]{1,2,0:T(8,128)}, f32[6,64,6]{1,2,0:T(8,128)S(1)}, u32[]{:S(2)}) copy-start(f32[6,64,6]{1,2,0:T(8,128)S(1)} %fusion.182) | copy-start | bytes 27652
  125.6 25.5 %copy-start.160 = (bf16[1024,1536]{1,0:T(8,128)(2,1)S(1)}, bf16[1024,1536]{1,0:T(8,128)(2,1)}, u32[]{:S(2)}) copy-start(bf16[1024,1536]{1,0:T(8,128)(2,1)} %param.23) | copy-start | bytes 9437188
  128.8 22.2 %copy-start.56 = (bf16[384,1024]{1,0:T(8,128)(2,1)S(1)}, bf16[384,1024]{1,0:T(8,128)(2,1)}, u32[]{:S(2)}) copy-start(bf16[384,1024]{1,0:T(8,128)(2,1)} %param.15) | copy-start | bytes 2359300
  128.8 22.2 %copy-start.80 = (f32[384,1536]{1,0:T(8,128)S(1)}, f32[384,1536]{1,0:T(8,128)}, u32[]{:S(2)}) copy-start(f32[384,1536]{1,0:T(8,128)} %copy.132) | copy-start | bytes 7077892
  130.0 21.1 %copy-start.82 = (f32[48,8,6,256]{3,1,2,0:T(8,128)}, f32[48,8,6,256]{3,1,2,0:T(8,128)S(1)}, u32[]{:S(2)}) copy-start(f32[48,8,6,256]{3,1,2,0:T(8,128)S(1)} %copy.196) | copy-start | bytes 7077892
  160.0 131.6 %reduce-scatter.2.cloned.1.call-start = ((), (), s32[]{:S(2)}) async-start(), calls=%async_computation.7 | async-start | bytes 7077888 | tf_op jit(solution)/shard_map/reduce_scatter | solution.py:244
  205.6 8.0 slice-start.10
  244.1 34.4 %all-to-all-start.2 = ((bf16[352,4,256]{2,0,1:T(8,128)(2,1)}), bf16[352,4,256]{2,0,1:T(8,128)(2,1)}, u32[]{:S(2)}, u32[]{:S(2)}) async-start(bf16[352,4,256]{2,0,1:T(8,128)(2,1)} %bitcast.424), calls=%async_computation.3 | async-start | bytes 1441792 | tf_op jit(solution)/shard_map/all_to_all | solution.py:300
  278.6 219.1 %all-to-all-start.1 = ((bf16[2,4,256,352]{2,3,0,1:T(8,128)(2,1)}), bf16[2,4,256,352]{2,3,0,1:T(8,128)(2,1)}, u32[]{:S(2)}, u32[]{:S(2)}) async-start(bf16[2,4,256,352]{2,3,0,1:T(8,128)(2,1)} %pad_maximum_fusion.4), calls=%async_computation.2 | async-start | bytes 2883584 | tf_op jit(solution)/shard_map/all_to_all | solution.py:300
  283.7 345.2 %all-reduce.40.cloned.1.call-start = ((), (), s32[]{:S(2)}) async-start(), calls=%async_computation.8 | async-start | bytes 12582912 | tf_op jit(solution)/shard_map/psum | solution.py:330
  319.6 59.6 %copy-start.29 = (f32[6,6,64,64]{2,3,1,0:T(8,128)}, f32[6,6,64,64]{2,3,1,0:T(8,128)S(1)}, u32[]{:S(2)}) copy-start(f32[6,6,64,64]{2,3,1,0:T(8,128)S(1)} %fusion.253) | copy-start | bytes 1769476
  344.8 9.6 %slice-start.2 = ((s8[4718592]{0:T(1024)(128)(4,1)}), s8[4194304]{0:T(1024)(128)(4,1)S(1)}, s32[]{:S(2)}) async-start(s8[4718592]{0:T(1024)(128)(4,1)} %bitcast.391), calls=%async_computation.12 | async-start | bytes 8388608
  388.0 7.3 copy-start.53
  388.0 7.3 copy-start.74
  388.0 7.3 copy-start.77
  458.8 7.9 slice-start.6
  497.7 165.2 %all-to-all-start = ((bf16[8,384,1024]{2,1,0:T(8,128)(2,1)}), bf16[8,384,1024]{2,1,0:T(8,128)(2,1)}, u32[]{:S(2)}, u32[]{:S(2)}) async-start(bf16[8,384,1024]{2,1,0:T(8,128)(2,1)} %bitcast.415), calls=%async_computation | async-start | bytes 12582912 | tf_op jit(solution)/shard_map/all_to_all | solution.py:300
  502.5 311.7 %all-reduce.42.cloned.1.call-start = ((), (), s32[]{:S(2)}) async-start(), calls=%async_computation.9 | async-start | bytes 12582912 | tf_op jit(solution)/shard_map/psum | solution.py:330
  658.7 2.6 collective-permute-start
  661.3 9.7 %copy-start.19 = (f32[384,1024]{1,0:T(8,128)S(1)}, f32[384,1024]{1,0:T(8,128)}, u32[]{:S(2)}) copy-start(f32[384,1024]{1,0:T(8,128)} %copy-done.17) | copy-start | bytes 4718596
  661.3 7.9 collective-permute-start.1
  669.3 8.8 %copy-start.134 = (f32[384]{0:T(512)S(1)}, f32[384]{0:T(512)}, u32[]{:S(2)}) copy-start(f32[384]{0:T(512)} %copy-done.133) | copy-start | bytes 4612
  669.3 16.4 %copy-start.63 = (f32[384,1024]{1,0:T(8,128)S(1)}, f32[384,1024]{1,0:T(8,128)}, u32[]{:S(2)}) copy-start(f32[384,1024]{1,0:T(8,128)} %copy-done.62) | copy-start | bytes 4718596
  669.3 16.4 %copy-start.64 = (f32[384,1024]{1,0:T(8,128)S(1)}, f32[384,1024]{1,0:T(8,128)}, u32[]{:S(2)}) copy-start(f32[384,1024]{1,0:T(8,128)} %get-tuple-element.154) | copy-start | bytes 4718596
  669.3 6.9 collective-permute-start.2
  676.3 7.3 collective-permute-start.3
  683.6 9.7 %collective-permute-start.4 = (f32[26892]{0:T(1024)S(1)}, f32[26892]{0:T(1024)S(1)}, u32[]{:S(2)}, u32[]{:S(2)}) collective-permute-start(f32[26892]{0:T(1024)S(1)} %add.274), channel_id=1, source_target_pairs={{0,16},{8,24},{16,0},{24,8},{1,17},{9,25},{17,1},{25,9},{2,18},{10... | collective-permute-start | bytes 322712 | tf_op jit(solution)/shard_map/ppermute | solution.py:321
  814.2 9.4 %copy-start.1 = (bf16[1536,1024]{1,0:T(8,128)(2,1)S(1)}, bf16[1536,1024]{1,0:T(8,128)(2,1)}, u32[]{:S(2)}) copy-start(bf16[1536,1024]{1,0:T(8,128)(2,1)} %param.25) | copy-start | bytes 9437188
  (145 other events, 440.2 us)
Sparse Core Ops, SparseCore 0:
  9.6 38.3 all-gather.3
  49.8 43.5 all-gather.5
  160.1 45.4 all-gather.7
  229.9 61.7 reduce-scatter.1
  451.7 177.0 all-reduce.39
  653.2 160.9 all-reduce.41

commit v5 on v4

--- a/solution.py
+++ b/solution.py
@@ -136,7 +136,7 @@
     return jnp.swapaxes(out, 1, 2).reshape(length, HEADS, HEAD_V)
 
 
-def mixer(raw_proj, gate_logits, out_gate, segments, conv_weight, a_log, dt_bias, gain_o):
+def mixer_core(raw_proj, gate_logits, segments, conv_weight, a_log, dt_bias):
     length = raw_proj.shape[0]
     key_dim = HEADS * HEAD_K
     conv = conv_silu(raw_proj, conv_weight, segments)
@@ -151,7 +151,11 @@
     keys_unit = keys_raw * lax.rsqrt(jnp.sum(keys_raw * keys_raw, axis=-1, keepdims=True) + EPSILON)
     log_decay = -jnp.exp(a_log) * jax.nn.softplus(gate_logits[:, :HEADS] + dt_bias)
     write_rate = jax.nn.sigmoid(gate_logits[:, HEADS:])
-    delta_out = delta_rule(queries, keys_unit, values_part, log_decay, write_rate, segments)
+    return delta_rule(queries, keys_unit, values_part, log_decay, write_rate, segments)
+
+
+def out_norm(delta_out, out_gate, gain_o):
+    length = delta_out.shape[0]
     gate_vals = jax.nn.silu(out_gate).reshape(length, HEADS, HEAD_V)
     normed = (
         delta_out
@@ -211,12 +215,11 @@
     gate_logits = jnp.dot(normed_in, w_decay, preferred_element_type=jnp.float32)
     out_gate = jnp.dot(normed_in, w_gate_o, preferred_element_type=jnp.float32)
 
-    def local_mixer(raw_a, logit_a, gate_a, conv_a, log_a, bias_a, gain_a):
-        return mixer(raw_a, logit_a, gate_a, segments, conv_a, log_a, bias_a, gain_a)
-
-    mixed_f, mixer_back = jax.vjp(
-        local_mixer, raw_proj, gate_logits, out_gate, conv_w, a_log, dt_bias, gain_o
-    )
+    def local_core(raw_a, logit_a, conv_a, log_a, bias_a):
+        return mixer_core(raw_a, logit_a, segments, conv_a, log_a, bias_a)
+
+    delta_out, core_back = jax.vjp(local_core, raw_proj, gate_logits, conv_w, a_log, dt_bias)
+    mixed_f, out_norm_back = jax.vjp(out_norm, delta_out, out_gate, gain_o)
     mixed = mixed_f.astype(jnp.bfloat16)
     gate_up_rows, down_rows = (
         lax.all_gather(w_gate_up, "row", axis=1, tiled=True),
@@ -253,16 +256,19 @@
     grad_middle_b = grad_middle.astype(jnp.bfloat16)
     grad_out = contract_rows(mixed, grad_middle_b)
     grad_mixed = contract_cols(grad_middle_b, w_out)
-    grad_raw, grad_logits, grad_gate_out, grad_conv, grad_a_log, grad_dt_bias, grad_gain_o = (
-        mixer_back(grad_mixed)
-    )
+    grad_delta, grad_gate_out, grad_gain_o = out_norm_back(grad_mixed)
+    grad_gate_b = grad_gate_out.astype(jnp.bfloat16)
+    grad_gate_o = contract_rows(normed_in, grad_gate_b)
+    early_parts = (grad_out, grad_gate_o)
+    early_flat = flat_bf16(early_parts)
+    early_flat, grad_delta = lax.optimization_barrier((early_flat, grad_delta))
+    early_total = lax.psum(early_flat, ("row", "col"))
+    early = split_flat(early_total, early_parts)
+    grad_raw, grad_logits, grad_conv, grad_a_log, grad_dt_bias = core_back(grad_delta)
     grad_raw_b = grad_raw.astype(jnp.bfloat16)
     grad_logits_b = grad_logits.astype(jnp.bfloat16)
-    grad_gate_b = grad_gate_out.astype(jnp.bfloat16)
     grad_qkv = contract_rows(normed_in, grad_raw_b)
     grad_decay = contract_rows(normed_in, grad_logits_b)
-    grad_gate_o = contract_rows(normed_in, grad_gate_b)
-    early = summed_bf16((grad_out, grad_gate_o))
     block_out = (middle_out + ffn_out).astype(jnp.bfloat16)
     grad_normed_in = (
         contract_cols(grad_raw_b, w_qkv)
@@ -323,8 +329,12 @@
     return split_flat(flat, parts)
 
 
+def flat_bf16(parts):
+    return jnp.concatenate([p.astype(jnp.bfloat16).reshape(-1) for p in parts])
+
+
 def summed_bf16(parts, after=None):
-    flat = jnp.concatenate([p.astype(jnp.bfloat16).reshape(-1) for p in parts])
+    flat = flat_bf16(parts)
     if after is not None:
         flat, _ = lax.optimization_barrier((flat, after))
     return split_flat(lax.psum(flat, ("row", "col")), parts)

time: 839 us -> 888 us (1.058)
  waiting for transfers between devices: 306 us -> 326 us
  local copies, waits for them, and re-layouts: 135 us -> 152 us
    psum x0 -> x1, waiting for transfers between devices: none -> 149 us  [per_device_body(): early_total = lax.psum(early_flat, ('row', 'col'))]
    psum x2 -> x1, waiting for transfers between devices: 236 us -> 109 us  [summed_bf16(): return split_flat(lax.psum(flat, ('row', 'col')), parts)]
    concatenate x1, other arithmetic: 23.6 us -> 13.5 us  [flat_bf16(): return jnp.concatenate([p.astype(jnp.bfloat16).reshape(-1) for p in parts])]
    mul x11 -> x12, local copies, waits for them, and re-layouts: 14.6 us -> 22.4 us  [the longest x6 10.8 us: out_norm(): delta_out * lax.rsqrt(jnp.mean(delta_out * delta_out, axis=-1, keepdims=T...]
    unnamed x374 -> x320, local copies, waits for them, and re-layouts: 29.6 us -> 25.7 us
  transfers between devices with their start and end apart: 14 -> 14, of which waited for: 8 -> 9; matrix products, arithmetic and copies ran while one was open for 49% -> 51% of each run, Pallas kernels for 0% -> 0%
where the time goes in v5:
time: 888 us; the launch traced here: 876 us
  waiting for transfers between devices  326 us (37%)
  matrix products  227 us (26%)
  local copies, waits for them, and re-layouts  152 us (17%)
  other arithmetic  114 us (13%)
  blocking collectives  20.9 us (2%)
  starting transfers between devices  19.9 us (2%)
  between operations  16.6 us (2%)
    psum x1, waiting for transfers between devices, per_device_body(): early_total = lax.psum(early_flat, ('row', 'col'))  149 us
    psum x1, waiting for transfers between devices, summed_bf16(): return split_flat(lax.psum(flat, ('row', 'col')), parts)  109 us
    all_gather x1, waiting for transfers between devices, per_device_body(): normed_all = lax.all_gather(normed_mid, 'col', axis=0, tiled=True)  45.5 us
    dot_general x7, matrix products, contract_rows(): lax.dot_general(left, right, (((0,), (0,)), ((), ())), preferred_element_...  35.5 us
    dot_general x7, matrix products, contract_cols(): lax.dot_general(left, right, (((1,), (1,)), ((), ())), preferred_element_...  33.7 us
    unnamed x320, local copies, waits for them, and re-layouts  25.7 us
    convert_element_type x3, local copies, waits for them, and re-layouts, split_flat(): out.append(total[at:at + p.size].reshape(p.shape).astype(jnp.float32))  24.6 us
    all_gather x1, blocking collectives, per_device_body(): lax.all_gather(w_down, 'row', axis=1, tiled=True)  20.9 us
  transfers between devices with their start and end apart: 14, of which 9 were waited for; matrix products, arithmetic and copies ran while one was open for 51% of the time, Pallas kernels for 0%

profile of v5, /device:TPU:0, one launch (start us, length us, event | category | flops | bytes accessed | tf_op | source)
XLA Modules:
  0.0 876.3 jit_solution(9176789695041032190)
XLA Ops:
  12.4 5.0 fusion.237
  17.5 6.2 fusion.5
  58.1 4.3 reshape.456
  90.2 4.6 fusion.27
  94.9 4.4 fusion.99
  124.4 20.9 %all_gather.13 = bf16[352,1024]{1,0:T(8,128)(2,1)} all-gather(bf16[352,256]{1,0:T(8,128)(2,1)S(1)} %copy-done.98), channel_id=1, replica_groups=mesh['row'=4,'col'=8] {'row'}, dimensions={1}, use_global_device_ids=true | all-gather | bytes 901120 | tf_op jit(solution)/shard_map/all_gather | solution.py:226
  145.3 7.0 multiply_convert_fusion.3
  157.8 45.5 %all-gather.8.cloned.1.call-done = bf16[3072,1024]{1,0:T(8,128)(2,1)} async-done(((bf16[384,1024]{1,0:T(8,128)(2,1)}), bf16[3072,1024]{1,0:T(8,128)(2,1)}) %all-gather.8.cloned.1.call-update) | async-done | bytes 6291472 | tf_op jit(solution)/shard_map/all_gather | solution.py:236
  203.3 5.5 fusion.119
  211.3 5.5 multiply_convert_fusion
  220.4 6.7 add_convert_fusion
  237.7 7.8 convolution_convert_fusion.4
  250.4 6.8 convolution_convert_fusion.5
  258.2 4.8 all-to-all-start.2
  262.9 6.8 convolution_convert_fusion.3
  276.0 5.4 convolution_convert_fusion
  282.1 4.3 all-to-all-start.1
  294.5 5.7 fusion.171
  300.3 4.1 mul.840
  306.4 5.4 fusion.29
  319.9 6.8 reshape.460
  326.8 13.5 %pad_maximum_fusion = bf16[3145728]{0:T(1024)(128)(2,1)} fusion(bf16[1572864]{0:T(1024)(128)(2,1)} %reshape.460, bf16[1572864]{0:T(1024)(128)(2,1)S(1)} %bitcast.422), kind=kLoop, calls=%fused_computation.3 | loop fusion | flops 12582912 | bytes 12582912 | tf_op jit(solution)/shard_map/concatenate | solution.py:333
  340.3 4.2 add_add_fusion
  346.9 4.9 fusion.14
  351.9 5.0 fusion.22
  359.4 4.3 convolution_add_fusion
  377.8 4.6 fusion.9
  384.4 5.1 fusion.50
  389.5 4.6 fusion.6
  404.6 4.7 fusion.86
  414.7 4.9 multiply_reduce_fusion.8
  429.3 6.5 broadcast_multiply_fusion
  468.8 6.1 multiply_reduce_fusion.3
  484.5 8.8 %add_convert_fusion.1 = bf16[384,3072]{1,0:T(8,128)(2,1)S(1)} fusion(f32[384,3072]{1,0:T(8,128)} %copy-done.3, f32[383,3072]{1,0:T(8,128)} %fusion.2, f32[382,3072]{1,0:T(8,128)} %fusion.3, f32[381,3072]{1,0:T(8,128)} %fusion.4, f32[3072]{0:T(1024)S(1)} %bitcast.461), kind=kLoop, calls=%fused_computation.18 | loop fusion | flops 5898240 | bytes 21172224 | tf_op jit(solution)/shard_map/convert_element_type | solution.py:268
  497.3 4.6 copy.277
  513.5 6.6 fusion.253
  520.1 4.7 all-to-all-start
  524.9 149.3 %all-reduce.40.cloned.1.call-done = bf16[3145728]{0:T(1024)(128)(2,1)} async-done(((bf16[3145728]{0:T(1024)(128)(2,1)}), bf16[3145728]{0:T(1024)(128)(2,1)}) %all-reduce.40.cloned.1.call-update) | async-done | bytes 6291472 | tf_op jit(solution)/shard_map/psum | solution.py:265
  674.2 7.0 slice_convert_fusion
  681.2 7.1 reshape.479
  688.2 10.3 %convert_element_type.147 = bf16[1024,3072]{1,0:T(8,128)(2,1)} reshape(bf16[3145728]{0:T(1024)(128)(2,1)} %bitcast.419) | data formatting | bytes 12582912 | tf_op jit(solution)/shard_map/convert_element_type | solution.py:313
  708.6 4.6 convert_reduce_fusion
  717.6 4.8 collective-permute-done.2
  723.4 6.4 collective-permute-done.3
  733.2 6.3 collective-permute-done.4
  743.5 7.2 reshape.480
  750.7 109.1 %all-reduce.42.cloned.1.call-done = bf16[1024,3072]{1,0:T(8,128)(2,1)} async-done(((bf16[1024,3072]{1,0:T(8,128)(2,1)}), bf16[1024,3072]{1,0:T(8,128)(2,1)}) %all-reduce.42.cloned.1.call-update) | async-done | bytes 6291472 | tf_op jit(solution)/shard_map/psum | solution.py:340
  859.9 9.4 %convert_element_type.148 = f32[1024,3072]{1,0:T(8,128)} convert(bf16[1024,3072]{1,0:T(8,128)(2,1)} %all-reduce.42.cloned.1.call-done) | non-fusion elementwise | flops 3145728 | bytes 18874368 | tf_op jit(solution)/shard_map/convert_element_type | solution.py:313
  (538 shorter events, 271.4 us)
Async XLA Ops:
  7.2 145.1 %copy-start = (bf16[1536,1024]{1,0:T(8,128)(2,1)S(1)}, bf16[1536,1024]{1,0:T(8,128)(2,1)}, u32[]{:S(2)}) copy-start(bf16[1536,1024]{1,0:T(8,128)(2,1)} %param.25) | copy-start | bytes 9437188
  7.2 145.1 %all-gather.4.cloned.1.call-start = ((), (), s32[]{:S(2)}) async-start(), calls=%async_computation.4 | async-start | bytes 1802240 | tf_op jit(solution)/shard_map/all_gather | solution.py:225
  8.0 144.3 %all-gather.6.cloned.1.call-start = ((), (), s32[]{:S(2)}) async-start(), calls=%async_computation.5 | async-start | bytes 7077888 | tf_op jit(solution)/shard_map/all_gather | solution.py:228
  8.7 194.6 %all-gather.8.cloned.1.call-start = ((), (), s32[]{:S(2)}) async-start(), calls=%async_computation.6 | async-start | bytes 7077888 | tf_op jit(solution)/shard_map/all_gather | solution.py:236
  17.4 6.3 copy-start.2
  31.8 9.0 %copy-start.96 = (pred[64,64]{0,1:T(8,128)(4,1)}, pred[64,64]{0,1:T(8,128)(4,1)S(1)}, u32[]{:S(2)}) copy-start(pred[64,64]{0,1:T(8,128)(4,1)S(1)} %iota_compare_fusion.3) | copy-start | bytes 12292
  36.5 47.3 %copy-start.86 = (f32[6,64,6]{1,2,0:T(8,128)}, f32[6,64,6]{1,2,0:T(8,128)S(1)}, u32[]{:S(2)}) copy-start(f32[6,64,6]{1,2,0:T(8,128)S(1)} %copy.344) | copy-start | bytes 27652
  38.0 10.7 %slice-start.6 = ((s8[4718592]{0:T(1024)(128)(4,1)}), s8[4194304]{0:T(1024)(128)(4,1)S(1)}, s32[]{:S(2)}) async-start(s8[4718592]{0:T(1024)(128)(4,1)} %bitcast.417), calls=%async_computation.16 | async-start | bytes 8388608
  40.9 7.8 slice-start.7
  64.7 35.6 %copy-start.127 = (f32[6]{0:T(128)}, f32[6]{0:T(128)S(1)}, u32[]{:S(2)}) copy-start(f32[6]{0:T(128)S(1)} %get-tuple-element.86) | copy-start | bytes 76
  64.7 36.5 %copy-start.129 = (f32[6]{0:T(128)}, f32[6]{0:T(128)S(1)}, u32[]{:S(2)}) copy-start(f32[6]{0:T(128)S(1)} %get-tuple-element.85) | copy-start | bytes 76
  64.7 37.4 %copy-start.125 = (f32[6]{0:T(128)}, f32[6]{0:T(128)S(1)}, u32[]{:S(2)}) copy-start(f32[6]{0:T(128)S(1)} %get-tuple-element.84) | copy-start | bytes 76
  83.7 11.2 %copy-start.90 = (f32[6,6,64]{2,1,0:T(8,128)}, f32[6,6,64]{2,1,0:T(8,128)S(1)}, u32[]{:S(2)}) copy-start(f32[6,6,64]{2,1,0:T(8,128)S(1)} %slice_reduce_fusion) | copy-start | bytes 27652
  90.2 15.8 %copy-start.12 = (f32[6,6,64,384]{3,2,1,0:T(8,128)}, f32[6,6,64,384]{3,2,1,0:T(8,128)S(1)}, u32[]{:S(2)}) copy-start(f32[6,6,64,384]{3,2,1,0:T(8,128)S(1)} %fusion.8) | copy-start | bytes 10616836
  94.8 7.3 copy-start.24
  106.0 6.3 copy-start.32
  157.6 131.4 %reduce-scatter.2.cloned.1.call-start = ((), (), s32[]{:S(2)}) async-start(), calls=%async_computation.7 | async-start | bytes 7077888 | tf_op jit(solution)/shard_map/reduce_scatter | solution.py:247
  203.3 8.0 slice-start.10
  258.2 24.0 %all-to-all-start.2 = ((bf16[352,4,256]{2,0,1:T(8,128)(2,1)}), bf16[352,4,256]{2,0,1:T(8,128)(2,1)}, u32[]{:S(2)}, u32[]{:S(2)}) async-start(bf16[352,4,256]{2,0,1:T(8,128)(2,1)} %bitcast.448), calls=%async_computation.3 | async-start | bytes 1441792 | tf_op jit(solution)/shard_map/all_to_all | solution.py:306
  282.1 237.9 %all-to-all-start.1 = ((bf16[2,4,256,352]{2,3,0,1:T(8,128)(2,1)}), bf16[2,4,256,352]{2,3,0,1:T(8,128)(2,1)}, u32[]{:S(2)}, u32[]{:S(2)}) async-start(bf16[2,4,256,352]{2,3,0,1:T(8,128)(2,1)} %pad_maximum_fusion.4), calls=%async_computation.2 | async-start | bytes 2883584 | tf_op jit(solution)/shard_map/all_to_all | solution.py:306
  286.5 387.7 %all-reduce.40.cloned.1.call-start = ((), (), s32[]{:S(2)}) async-start(), calls=%async_computation.8 | async-start | bytes 12582912 | tf_op jit(solution)/shard_map/psum | solution.py:265
  293.7 6.6 copy-start.67
  346.9 10.0 %copy-start.7 = (f32[384,6,256]{2,0,1:T(8,128)}, f32[384,6,256]{2,0,1:T(8,128)S(1)}, u32[]{:S(2)}) copy-start(f32[384,6,256]{2,0,1:T(8,128)S(1)} %copy.207) | copy-start | bytes 7077892
  351.8 46.1 %copy-start.35 = (f32[6,6,64,64]{2,3,1,0:T(8,128)}, f32[6,6,64,64]{2,3,1,0:T(8,128)S(1)}, u32[]{:S(2)}) copy-start(f32[6,6,64,64]{2,3,1,0:T(8,128)S(1)} %fusion.14) | copy-start | bytes 1769476
  363.6 10.9 %copy-start.23 = (f32[6,6,128,256]{3,2,1,0:T(8,128)}, f32[6,6,128,256]{3,2,1,0:T(8,128)S(1)}, u32[]{:S(2)}) copy-start(f32[6,6,128,256]{3,2,1,0:T(8,128)S(1)} %convolution_add_fusion) | copy-start | bytes 14155780
  374.9 9.4 %slice-start.2 = ((s8[4718592]{0:T(1024)(128)(4,1)}), s8[4194304]{0:T(1024)(128)(4,1)S(1)}, s32[]{:S(2)}) async-start(s8[4718592]{0:T(1024)(128)(4,1)} %bitcast.413), calls=%async_computation.12 | async-start | bytes 8388608
  377.8 6.6 slice-start.3
  397.9 6.7 copy-start.29
  404.6 6.2 copy-start.19
  404.6 6.2 copy-start.95
  419.7 7.2 copy-start.30
  421.4 7.8 slice-start.4
  468.8 6.2 copy-start.110
  474.9 6.0 copy-start.3
  484.5 8.8 %copy-start.63 = (bf16[384,1024]{1,0:T(8,128)(2,1)S(1)}, bf16[384,1024]{1,0:T(8,128)(2,1)}, u32[]{:S(2)}) copy-start(bf16[384,1024]{1,0:T(8,128)(2,1)} %param.15) | copy-start | bytes 2359300
  507.6 5.9 copy-start.82
  520.1 188.5 %all-to-all-start = ((bf16[8,384,1024]{2,1,0:T(8,128)(2,1)}), bf16[8,384,1024]{2,1,0:T(8,128)(2,1)}, u32[]{:S(2)}, u32[]{:S(2)}) async-start(bf16[8,384,1024]{2,1,0:T(8,128)(2,1)} %bitcast.439), calls=%async_computation | async-start | bytes 12582912 | tf_op jit(solution)/shard_map/all_to_all | solution.py:306
  524.8 335.0 %all-reduce.42.cloned.1.call-start = ((), (), s32[]{:S(2)}) async-start(), calls=%async_computation.9 | async-start | bytes 12582912 | tf_op jit(solution)/shard_map/psum | solution.py:340
  704.4 2.6 collective-permute-start
  707.0 9.5 %copy-start.22 = (f32[384,1024]{1,0:T(8,128)S(1)}, f32[384,1024]{1,0:T(8,128)}, u32[]{:S(2)}) copy-start(f32[384,1024]{1,0:T(8,128)} %copy-done.20) | copy-start | bytes 4718596
  707.0 8.1 collective-permute-start.1
  715.1 8.3 copy-start.121
  715.1 16.6 %copy-start.68 = (f32[384,1024]{1,0:T(8,128)S(1)}, f32[384,1024]{1,0:T(8,128)}, u32[]{:S(2)}) copy-start(f32[384,1024]{1,0:T(8,128)} %copy-done.67) | copy-start | bytes 4718596
  715.1 16.6 %copy-start.69 = (f32[384,1024]{1,0:T(8,128)S(1)}, f32[384,1024]{1,0:T(8,128)}, u32[]{:S(2)}) copy-start(f32[384,1024]{1,0:T(8,128)} %get-tuple-element.172) | copy-start | bytes 4718596
  715.1 7.3 collective-permute-start.2
  722.4 7.4 collective-permute-start.3
  729.8 9.8 %collective-permute-start.4 = (f32[26892]{0:T(1024)S(1)}, f32[26892]{0:T(1024)S(1)}, u32[]{:S(2)}, u32[]{:S(2)}) collective-permute-start(f32[26892]{0:T(1024)S(1)} %add.276), channel_id=1, source_target_pairs={{0,16},{8,24},{16,0},{24,8},{1,17},{9,25},{17,1},{25,9},{2,18},{10... | collective-permute-start | bytes 322712 | tf_op jit(solution)/shard_map/ppermute | solution.py:327
  859.9 9.4 %copy-start.1 = (bf16[1536,1024]{1,0:T(8,128)(2,1)S(1)}, bf16[1536,1024]{1,0:T(8,128)(2,1)}, u32[]{:S(2)}) copy-start(bf16[1536,1024]{1,0:T(8,128)(2,1)} %param.25) | copy-start | bytes 9437188
  (118 other events, 385.9 us)
Sparse Core Ops, SparseCore 0:
  9.6 38.3 all-gather.3
  49.8 43.6 all-gather.5
  157.7 45.5 all-gather.7
  227.3 61.7 reduce-scatter.1
  484.0 190.1 all-reduce.39
  698.7 161.1 all-reduce.41

commit v6 on v5

--- a/solution.py
+++ b/solution.py
@@ -221,10 +221,9 @@
     delta_out, core_back = jax.vjp(local_core, raw_proj, gate_logits, conv_w, a_log, dt_bias)
     mixed_f, out_norm_back = jax.vjp(out_norm, delta_out, out_gate, gain_o)
     mixed = mixed_f.astype(jnp.bfloat16)
-    gate_up_rows, down_rows = (
-        lax.all_gather(w_gate_up, "row", axis=1, tiled=True),
-        lax.all_gather(w_down, "row", axis=1, tiled=True),
-    )
+    stacked = jnp.concatenate([w_gate_up, w_down.T[None]], axis=0)
+    stacked_rows = lax.all_gather(stacked, "row", axis=1, tiled=True)
+    gate_up_rows, down_rows = stacked_rows[:2], stacked_rows[2].T
     cot_all = lax.all_gather(cotangent, "col", axis=0, tiled=True)
     mixed, gate_up_rows, down_rows, cot_all = lax.optimization_barrier(
         (mixed, gate_up_rows, down_rows, cot_all)
@@ -259,17 +258,15 @@
     grad_delta, grad_gate_out, grad_gain_o = out_norm_back(grad_mixed)
     grad_gate_b = grad_gate_out.astype(jnp.bfloat16)
     grad_gate_o = contract_rows(normed_in, grad_gate_b)
-    early_parts = (grad_out, grad_gate_o)
-    early_flat = flat_bf16(early_parts)
-    early_flat, grad_delta = lax.optimization_barrier((early_flat, grad_delta))
-    early_total = lax.psum(early_flat, ("row", "col"))
-    early = split_flat(early_total, early_parts)
+    early_b = (grad_out.astype(jnp.bfloat16), grad_gate_o.astype(jnp.bfloat16))
+    early_b, grad_delta = lax.optimization_barrier((early_b, grad_delta))
+    early_b = lax.psum(early_b, ("row", "col"))
+    early = [e.astype(jnp.float32) for e in early_b]
     grad_raw, grad_logits, grad_conv, grad_a_log, grad_dt_bias = core_back(grad_delta)
     grad_raw_b = grad_raw.astype(jnp.bfloat16)
     grad_logits_b = grad_logits.astype(jnp.bfloat16)
     grad_qkv = contract_rows(normed_in, grad_raw_b)
     grad_decay = contract_rows(normed_in, grad_logits_b)
-    block_out = (middle_out + ffn_out).astype(jnp.bfloat16)
     grad_normed_in = (
         contract_cols(grad_raw_b, w_qkv)
         + contract_cols(grad_logits_b, w_decay)
@@ -277,7 +274,18 @@
     )
     grad_in_norm, grad_gain_in = norm_in_back(grad_normed_in)
     grad_tokens = grad_middle + grad_in_norm
-    late = summed_bf16((grad_qkv,), after=early[0])
+    qkv_b, _, ffn_out = lax.optimization_barrier((grad_qkv.astype(jnp.bfloat16), early_b, ffn_out))
+    block_out = (middle_out + ffn_out).astype(jnp.bfloat16)
+    half = qkv_b.shape[1] // 2
+    late = [
+        jnp.concatenate(
+            [
+                lax.psum(qkv_b[:, :half], ("row", "col")).astype(jnp.float32),
+                summed_all_by_exchange(qkv_b[:, half:]),
+            ],
+            axis=1,
+        )
+    ]
     small = summed_f32(
         (grad_gain_in, grad_conv, grad_decay, grad_a_log, grad_dt_bias, grad_gain_o, grad_gain_mid)
     )
@@ -307,6 +315,16 @@
     return jnp.sum(got.astype(jnp.float32), axis=dim)
 
 
+def summed_all_by_exchange(part):
+    axes = ("row", "col")
+    n = lax.axis_size(axes)
+    rows = part.shape[0]
+    pieces = part.reshape((n, rows // n) + part.shape[1:])
+    mine = jnp.sum(lax.all_to_all(pieces, axes, 0, 0).astype(jnp.float32), axis=0)
+    shared = jnp.broadcast_to(mine.astype(jnp.bfloat16)[None], pieces.shape)
+    return lax.all_to_all(shared, axes, 0, 0).reshape(part.shape).astype(jnp.float32)
+
+
 def split_flat(total, parts):
     out, at = [], 0
     for p in parts:
@@ -329,17 +347,6 @@
     return split_flat(flat, parts)
 
 
-def flat_bf16(parts):
-    return jnp.concatenate([p.astype(jnp.bfloat16).reshape(-1) for p in parts])
-
-
-def summed_bf16(parts, after=None):
-    flat = flat_bf16(parts)
-    if after is not None:
-        flat, _ = lax.optimization_barrier((flat, after))
-    return split_flat(lax.psum(flat, ("row", "col")), parts)
-
-
 def solution(mesh):
     in_specs = (
         P(("row", "col"), None),

time: 888 us -> 999 us (1.12)
  waiting for transfers between devices: 326 us -> 465 us
  local copies, waits for them, and re-layouts: 152 us -> 123 us
  blocking collectives: 20.9 us -> 0 us
  starting transfers between devices: 19.9 us -> 37.9 us
  matrix products: 227 us -> 239 us
    all_to_all x3, waiting for transfers between devices: 0.82 us -> 108 us  [summed_by_exchange(): got = lax.all_to_all(pieces, axis, dim, dim, tiled=False)]
    all_to_all x0 -> x2, waiting for transfers between devices: none -> 50.9 us  [the longest x1 50.9 us: summed_all_by_exchange(): lax.all_to_all(pieces, axes, 0, 0).astype(jnp.float32)]
    psum x2, waiting for transfers between devices: 258 us -> 223 us  [the longest x1 127 us: per_device_body(): early_b = lax.psum(early_b, ('row', 'col'))]
    convert_element_type x3 -> x0, local copies, waits for them, and re-layouts: 24.6 us -> none  [split_flat(): out.append(total[at:at + p.size].reshape(p.shape).astype(jnp.float32))]
    ppermute x5, waiting for transfers between devices: 19.4 us -> 41.7 us  [summed_f32(): flat = flat + lax.ppermute(flat, axis, [(i, i ^ step) for i in range(n)])]
    all_gather x1 -> x0, blocking collectives: 20.9 us -> none  [per_device_body(): lax.all_gather(w_down, 'row', axis=1, tiled=True)]
    unnamed x320 -> x334, local copies, waits for them, and re-layouts: 25.7 us -> 25.5 us
  transfers between devices with their start and end apart: 14 -> 16, of which waited for: 9 -> 11; matrix products, arithmetic and copies ran while one was open for 51% -> 41% of each run, Pallas kernels for 0% -> 0%
where the time goes in v6:
time: 999 us; the launch traced here: 988 us
  waiting for transfers between devices  465 us (47%)
  matrix products  239 us (24%)
  local copies, waits for them, and re-layouts  123 us (12%)
  other arithmetic  105 us (11%)
  starting transfers between devices  37.9 us (4%)
  between operations  17 us (2%)
    psum x1, waiting for transfers between devices, per_device_body(): early_b = lax.psum(early_b, ('row', 'col'))  127 us
    all_to_all x3, waiting for transfers between devices, summed_by_exchange(): got = lax.all_to_all(pieces, axis, dim, dim, tiled=False)  108 us
    psum x1, waiting for transfers between devices, per_device_body(): lax.psum(qkv_b[:, :half], ('row', 'col')).astype(jnp.float32)  96 us
    all_to_all x1, waiting for transfers between devices, summed_all_by_exchange(): lax.all_to_all(pieces, axes, 0, 0).astype(jnp.float32)  50.9 us
    ppermute x5, waiting for transfers between devices, summed_f32(): flat = flat + lax.ppermute(flat, axis, [(i, i ^ step) for i in range(n)])  41.7 us
    all_gather x1, waiting for transfers between devices, per_device_body(): normed_all = lax.all_gather(normed_mid, 'col', axis=0, tiled=True)  40.7 us
    dot_general x7, matrix products, contract_rows(): lax.dot_general(left, right, (((0,), (0,)), ((), ())), preferred_element_...  37.5 us
    dot_general x7, matrix products, contract_cols(): lax.dot_general(left, right, (((1,), (1,)), ((), ())), preferred_element_...  33.3 us
  transfers between devices with their start and end apart: 16, of which 11 were waited for; matrix products, arithmetic and copies ran while one was open for 41% of the time, Pallas kernels for 0%

profile of v6, /device:TPU:0, one launch (start us, length us, event | category | flops | bytes accessed | tf_op | source)
XLA Modules:
  0.0 987.6 jit_solution(9304380372459884396)
XLA Ops:
  12.9 5.0 fusion.236
  18.8 7.0 fusion.5
  61.3 4.2 reshape.429
  93.3 4.6 fusion.27
  98.0 4.4 fusion.98
  127.4 7.0 multiply_convert_fusion.3
  145.8 7.4 fusion.253
  153.2 40.7 %all-gather.8.cloned.1.call-done = bf16[3072,1024]{1,0:T(8,128)(2,1)} async-done(((bf16[384,1024]{1,0:T(8,128)(2,1)}), bf16[3072,1024]{1,0:T(8,128)(2,1)}) %all-gather.8.cloned.1.call-update) | async-done | bytes 6291472 | tf_op jit(solution)/shard_map/all_gather | solution.py:235
  193.9 5.5 fusion.119
  200.4 6.4 multiply_convert_fusion
  210.3 5.6 add_convert_fusion
  216.0 7.9 convolution_convert_fusion
  223.9 5.2 all-to-all-start
  243.2 5.8 convolution_convert_fusion.6
  249.9 76.0 %all-to-all-done = bf16[8,384,1024]{2,1,0:T(8,128)(2,1)} async-done(((bf16[8,384,1024]{2,1,0:T(8,128)(2,1)}), bf16[8,384,1024]{2,1,0:T(8,128)(2,1)}, u32[]{:S(2)}, u32[]{:S(2)}) %all-to-all-start) | async-done | bytes 6291488 | tf_op jit(solution)/shard_map/all_to_all | solution.py:314
  326.0 4.7 all-to-all-start.4
  330.6 5.6 convert_reduce_fusion
  341.9 5.9 fusion.170
  353.5 5.5 convolution_convert_fusion.3
  361.1 5.3 convolution_convert_fusion.2
  376.4 5.0 fusion.22
  383.9 4.3 convolution_add_fusion
  404.2 4.6 fusion.9
  410.9 5.1 fusion.49
  416.0 4.3 fusion.6
  430.7 5.4 fusion.85
  438.4 4.7 fusion.53
  443.2 5.5 multiply_reduce_fusion.8
  459.4 6.6 broadcast_multiply_fusion
  489.8 5.2 add_add_fusion.4
  498.1 7.7 multiply_reduce_fusion.3
  512.4 6.2 convolution_convert_fusion.1
  518.6 127.1 %all-reduce.43.cloned.1.call-done = (bf16[1536,1024]{1,0:T(8,128)(2,1)}, bf16[1024,1536]{1,0:T(8,128)(2,1)}) async-done(((bf16[1536,1024]{1,0:T(8,128)(2,1)}, bf16[1024,1536]{1,0:T(8,128)(2,1)}), (bf16[1536,1024]{1,0:T(8,128)(2,1)}, bf16[1024,1536]{1,0:T(8,128)(2,1)})) %all-reduce.43.cloned.1.call-update) | async-done | bytes 6291472 | tf_op jit(solution)/shard_map/psum | solution.py:263
  645.7 6.0 fusion.244
  651.7 4.7 all-to-all-start.1
  656.4 6.7 convolution_convert_fusion.5
  666.0 6.7 convolution_convert_fusion.4
  676.9 50.9 %all-to-all-done.1 = bf16[32,32,1536]{2,1,0:T(8,128)(2,1)} async-done(((bf16[32,32,1536]{2,1,0:T(8,128)(2,1)}), bf16[32,32,1536]{2,1,0:T(8,128)(2,1)}, u32[]{:S(2)}, u32[]{:S(2)}) %all-to-all-start.1) | async-done | bytes 3145760 | tf_op jit(solution)/shard_map/all_to_all | solution.py:323
  727.8 4.3 all-to-all-start.3
  734.5 31.9 %all-to-all-done.3 = bf16[2,4,256,352]{2,3,0,1:T(8,128)(2,1)} async-done(((bf16[2,4,256,352]{2,3,0,1:T(8,128)(2,1)}), bf16[2,4,256,352]{2,3,0,1:T(8,128)(2,1)}, u32[]{:S(2)}, u32[]{:S(2)}) %all-to-all-start.3) | async-done | bytes 1441824 | tf_op jit(solution)/shard_map/all_to_all | solution.py:314
  786.2 4.9 fusion.254
  801.4 8.7 collective-permute-start.2
  814.6 11.5 %collective-permute-done.3 = f32[26892]{0:T(1024)S(1)} collective-permute-done((f32[26892]{0:T(1024)S(1)}, f32[26892]{0:T(1024)S(1)}, u32[]{:S(2)}, u32[]{:S(2)}) %collective-permute-start.3) | collective-permute-done | bytes 107600 | tf_op jit(solution)/shard_map/ppermute | solution.py:345
  826.1 4.3 collective-permute-start.4
  834.8 24.5 %collective-permute-done.4 = f32[26892]{0:T(1024)S(1)} collective-permute-done((f32[26892]{0:T(1024)S(1)}, f32[26892]{0:T(1024)S(1)}, u32[]{:S(2)}, u32[]{:S(2)}) %collective-permute-start.4) | collective-permute-done | bytes 107600 | tf_op jit(solution)/shard_map/ppermute | solution.py:345
  863.2 5.6 convert_element_type.141
  874.8 96.0 %all-reduce.41.cloned.1.call-done = bf16[1024,1536]{1,0:T(8,128)(2,1)} async-done(((bf16[1024,1536]{1,0:T(8,128)(2,1)}), bf16[1024,1536]{1,0:T(8,128)(2,1)}) %all-reduce.41.cloned.1.call-update) | async-done | bytes 3145744 | tf_op jit(solution)/shard_map/psum | solution.py:283
  970.9 9.5 maximum_convert_fusion
  (556 shorter events, 282.7 us)
Async XLA Ops:
  7.2 131.8 %copy-start = (bf16[1536,1024]{1,0:T(8,128)(2,1)S(1)}, bf16[1536,1024]{1,0:T(8,128)(2,1)}, u32[]{:S(2)}) copy-start(bf16[1536,1024]{1,0:T(8,128)(2,1)} %param.25) | copy-start | bytes 9437188
  7.2 127.2 %all-gather.4.cloned.1.call-start = ((), (), s32[]{:S(2)}) async-start(), calls=%async_computation.6 | async-start | bytes 2703360 | tf_op jit(solution)/shard_map/all_gather | solution.py:225
  9.4 129.6 %all-gather.6.cloned.1.call-start = ((), (), s32[]{:S(2)}) async-start(), calls=%async_computation.7 | async-start | bytes 7077888 | tf_op jit(solution)/shard_map/all_gather | solution.py:227
  10.1 183.8 %all-gather.8.cloned.1.call-start = ((), (), s32[]{:S(2)}) async-start(), calls=%async_computation.8 | async-start | bytes 7077888 | tf_op jit(solution)/shard_map/all_gather | solution.py:235
  12.9 5.9 copy-start.100
  12.9 5.9 copy-start.106
  18.0 7.8 copy-start.2
  34.8 8.1 copy-start.98
  38.5 48.5 %copy-start.84 = (f32[6,64,6]{1,2,0:T(8,128)}, f32[6,64,6]{1,2,0:T(8,128)S(1)}, u32[]{:S(2)}) copy-start(f32[6,64,6]{1,2,0:T(8,128)S(1)} %copy.342) | copy-start | bytes 27652
  38.6 76.8 %copy-start.72 = (pred[6,64,64]{1,2,0:T(8,128)(4,1)}, pred[6,64,64]{1,2,0:T(8,128)(4,1)S(1)}, u32[]{:S(2)}) copy-start(pred[6,64,64]{1,2,0:T(8,128)(4,1)S(1)} %compare_and_fusion) | copy-start | bytes 73732
  40.0 75.4 %copy-start.56 = (f32[6,6,64]{2,1,0:T(8,128)}, f32[6,6,64]{2,1,0:T(8,128)S(1)}, u32[]{:S(2)}) copy-start(f32[6,6,64]{2,1,0:T(8,128)S(1)} %reduce_window_sum.22) | copy-start | bytes 27652
  40.0 75.4 %copy-start.86 = (f32[6,6,64]{2,1,0:T(8,128)}, f32[6,6,64]{2,1,0:T(8,128)S(1)}, u32[]{:S(2)}) copy-start(f32[6,6,64]{2,1,0:T(8,128)S(1)} %get-tuple-element.100) | copy-start | bytes 27652
  40.0 11.9 %slice-start.6 = ((s8[4718592]{0:T(1024)(128)(4,1)}), s8[4194304]{0:T(1024)(128)(4,1)S(1)}, s32[]{:S(2)}) async-start(s8[4718592]{0:T(1024)(128)(4,1)} %bitcast.422), calls=%async_computation.18 | async-start | bytes 8388608
  42.9 9.0 slice-start.7
  67.6 44.8 %copy-start.90 = (f32[6,64,6]{1,2,0:T(8,128)}, f32[6,64,6]{1,2,0:T(8,128)S(1)}, u32[]{:S(2)}) copy-start(f32[6,64,6]{1,2,0:T(8,128)S(1)} %copy.178) | copy-start | bytes 27652
  67.8 36.5 %copy-start.135 = (f32[6]{0:T(128)}, f32[6]{0:T(128)S(1)}, u32[]{:S(2)}) copy-start(f32[6]{0:T(128)S(1)} %get-tuple-element.89) | copy-start | bytes 76
  86.9 11.1 %copy-start.92 = (f32[6,6,64]{2,1,0:T(8,128)}, f32[6,6,64]{2,1,0:T(8,128)S(1)}, u32[]{:S(2)}) copy-start(f32[6,6,64]{2,1,0:T(8,128)S(1)} %slice_reduce_fusion) | copy-start | bytes 27652
  93.3 15.8 %copy-start.9 = (f32[6,6,64,384]{3,2,1,0:T(8,128)}, f32[6,6,64,384]{3,2,1,0:T(8,128)S(1)}, u32[]{:S(2)}) copy-start(f32[6,6,64,384]{3,2,1,0:T(8,128)S(1)} %fusion.8) | copy-start | bytes 10616836
  97.9 7.3 copy-start.17
  109.1 6.4 copy-start.25
  145.6 190.6 %reduce-scatter.2.cloned.1.call-start = ((), (), s32[]{:S(2)}) async-start(), calls=%async_computation.9 | async-start | bytes 7077888 | tf_op jit(solution)/shard_map/reduce_scatter | solution.py:246
  193.9 6.5 copy-start.149
  223.9 102.1 %all-to-all-start = ((bf16[8,384,1024]{2,1,0:T(8,128)(2,1)}), bf16[8,384,1024]{2,1,0:T(8,128)(2,1)}, u32[]{:S(2)}, u32[]{:S(2)}) async-start(bf16[8,384,1024]{2,1,0:T(8,128)(2,1)} %bitcast.443), calls=%async_computation.1 | async-start | bytes 12582912 | tf_op jit(solution)/shard_map/all_to_all | solution.py:314
  326.0 325.8 %all-to-all-start.4 = ((bf16[352,4,256]{2,0,1:T(8,128)(2,1)}), bf16[352,4,256]{2,0,1:T(8,128)(2,1)}, u32[]{:S(2)}, u32[]{:S(2)}) async-start(bf16[352,4,256]{2,0,1:T(8,128)(2,1)} %bitcast.452), calls=%async_computation.5 | async-start | bytes 1441792 | tf_op jit(solution)/shard_map/all_to_all | solution.py:314
  330.6 315.1 %all-reduce.43.cloned.1.call-start = ((), (), s32[]{:S(2)}) async-start(), calls=%async_computation.11 | async-start | bytes 12582912 | tf_op jit(solution)/shard_map/psum | solution.py:263
  341.1 6.7 copy-start.63
  376.4 47.7 %copy-start.28 = (f32[6,6,64,64]{2,3,1,0:T(8,128)}, f32[6,6,64,64]{2,3,1,0:T(8,128)S(1)}, u32[]{:S(2)}) copy-start(f32[6,6,64,64]{2,3,1,0:T(8,128)S(1)} %fusion.14) | copy-start | bytes 1769476
  388.2 12.5 %copy-start.16 = (f32[6,6,128,256]{3,2,1,0:T(8,128)}, f32[6,6,128,256]{3,2,1,0:T(8,128)S(1)}, u32[]{:S(2)}) copy-start(f32[6,6,128,256]{3,2,1,0:T(8,128)S(1)} %convolution_add_fusion) | copy-start | bytes 14155780
  401.1 9.7 slice-start.2
  404.2 6.7 slice-start.3
  424.1 6.6 copy-start.22
  448.7 7.3 copy-start.23
  450.5 8.8 slice-start.4
  489.8 7.6 slice-start.9
  489.8 8.3 copy-start.54
  498.1 7.7 copy-start.111
  498.1 7.7 copy-start.134
  651.7 76.0 %all-to-all-start.1 = ((bf16[32,32,1536]{2,1,0:T(8,128)(2,1)}), bf16[32,32,1536]{2,1,0:T(8,128)(2,1)}, u32[]{:S(2)}, u32[]{:S(2)}) async-start(bf16[32,32,1536]{2,1,0:T(8,128)(2,1)} %bitcast.426), calls=%async_computation.2 | async-start | bytes 6291456 | tf_op jit(solution)/shard_map/all_to_all | solution.py:323
  727.8 38.5 %all-to-all-start.3 = ((bf16[2,4,256,352]{2,3,0,1:T(8,128)(2,1)}), bf16[2,4,256,352]{2,3,0,1:T(8,128)(2,1)}, u32[]{:S(2)}, u32[]{:S(2)}) async-start(bf16[2,4,256,352]{2,3,0,1:T(8,128)(2,1)} %pad_maximum_fusion.3), calls=%async_computation.4 | async-start | bytes 2883584 | tf_op jit(solution)/shard_map/all_to_all | solution.py:314
  768.3 202.5 %all-to-all-start.2 = ((bf16[32,32,1536]{2,1,0:T(8,128)(2,1)}), bf16[32,32,1536]{2,1,0:T(8,128)(2,1)}, u32[]{:S(2)}, u32[]{:S(2)}) async-start(bf16[32,32,1536]{2,1,0:T(8,128)(2,1)} %broadcast_in_dim.179), calls=%async_computation.3 | async-start | bytes 6291456 | tf_op jit(solution)/shard_map/all_to_all | solution.py:325
  772.1 198.8 %all-reduce.41.cloned.1.call-start = ((), (), s32[]{:S(2)}) async-start(), calls=%async_computation.10 | async-start | bytes 6291456 | tf_op jit(solution)/shard_map/psum | solution.py:283
  793.7 1.3 collective-permute-start
  795.1 6.3 collective-permute-start.1
  798.8 15.8 %copy-start.127 = (f32[384]{0:T(512)S(1)}, f32[384]{0:T(512)}, u32[]{:S(2)}) copy-start(f32[384]{0:T(512)} %copy-done.126) | copy-start | bytes 4612
  801.4 13.1 %collective-permute-start.2 = (f32[26892]{0:T(1024)S(1)}, f32[26892]{0:T(1024)S(1)}, u32[]{:S(2)}, u32[]{:S(2)}) collective-permute-start(f32[26892]{0:T(1024)S(1)} %add.276), channel_id=1, source_target_pairs={{0,4},{1,5},{2,6},{3,7},{4,0},{5,1},{6,2},{7,3},{8,12},{9,13},{10,... | collective-permute-start | bytes 322712 | tf_op jit(solution)/shard_map/ppermute | solution.py:345
  814.5 11.7 %collective-permute-start.3 = (f32[26892]{0:T(1024)S(1)}, f32[26892]{0:T(1024)S(1)}, u32[]{:S(2)}, u32[]{:S(2)}) collective-permute-start(f32[26892]{0:T(1024)S(1)} %add.277), channel_id=1, source_target_pairs={{0,8},{8,0},{16,24},{24,16},{1,9},{9,1},{17,25},{25,17},{2,10},{10... | collective-permute-start | bytes 322712 | tf_op jit(solution)/shard_map/ppermute | solution.py:345
  826.1 33.1 %collective-permute-start.4 = (f32[26892]{0:T(1024)S(1)}, f32[26892]{0:T(1024)S(1)}, u32[]{:S(2)}, u32[]{:S(2)}) collective-permute-start(f32[26892]{0:T(1024)S(1)} %add.278), channel_id=1, source_target_pairs={{0,16},{8,24},{16,0},{24,8},{1,17},{9,25},{17,1},{25,9},{2,18},{10... | collective-permute-start | bytes 322712 | tf_op jit(solution)/shard_map/ppermute | solution.py:345
  970.9 9.5 copy-start.1
  (128 other events, 433.4 us)
Sparse Core Ops, SparseCore 0:
  10.2 50.0 all-gather.3
  62.1 43.5 all-gather.5
  145.7 48.1 all-gather.7
  216.1 103.7 reduce-scatter.1
  489.9 155.7 all-reduce.42
  830.6 140.2 all-reduce.40

commit v7 on v6

--- a/solution.py
+++ b/solution.py
@@ -260,13 +260,14 @@
     grad_gate_o = contract_rows(normed_in, grad_gate_b)
     early_b = (grad_out.astype(jnp.bfloat16), grad_gate_o.astype(jnp.bfloat16))
     early_b, grad_delta = lax.optimization_barrier((early_b, grad_delta))
-    early_b = lax.psum(early_b, ("row", "col"))
+    early_b = tuple(summed_in_two_steps(e) for e in early_b)
     early = [e.astype(jnp.float32) for e in early_b]
     grad_raw, grad_logits, grad_conv, grad_a_log, grad_dt_bias = core_back(grad_delta)
     grad_raw_b = grad_raw.astype(jnp.bfloat16)
     grad_logits_b = grad_logits.astype(jnp.bfloat16)
     grad_qkv = contract_rows(normed_in, grad_raw_b)
     grad_decay = contract_rows(normed_in, grad_logits_b)
+    block_out = (middle_out + ffn_out).astype(jnp.bfloat16)
     grad_normed_in = (
         contract_cols(grad_raw_b, w_qkv)
         + contract_cols(grad_logits_b, w_decay)
@@ -274,18 +275,8 @@
     )
     grad_in_norm, grad_gain_in = norm_in_back(grad_normed_in)
     grad_tokens = grad_middle + grad_in_norm
-    qkv_b, _, ffn_out = lax.optimization_barrier((grad_qkv.astype(jnp.bfloat16), early_b, ffn_out))
-    block_out = (middle_out + ffn_out).astype(jnp.bfloat16)
-    half = qkv_b.shape[1] // 2
-    late = [
-        jnp.concatenate(
-            [
-                lax.psum(qkv_b[:, :half], ("row", "col")).astype(jnp.float32),
-                summed_all_by_exchange(qkv_b[:, half:]),
-            ],
-            axis=1,
-        )
-    ]
+    qkv_b, _ = lax.optimization_barrier((grad_qkv.astype(jnp.bfloat16), early_b))
+    late = [summed_in_two_steps(qkv_b).astype(jnp.float32)]
     small = summed_f32(
         (grad_gain_in, grad_conv, grad_decay, grad_a_log, grad_dt_bias, grad_gain_o, grad_gain_mid)
     )
@@ -315,14 +306,10 @@
     return jnp.sum(got.astype(jnp.float32), axis=dim)
 
 
-def summed_all_by_exchange(part):
+def summed_in_two_steps(part):
     axes = ("row", "col")
-    n = lax.axis_size(axes)
-    rows = part.shape[0]
-    pieces = part.reshape((n, rows // n) + part.shape[1:])
-    mine = jnp.sum(lax.all_to_all(pieces, axes, 0, 0).astype(jnp.float32), axis=0)
-    shared = jnp.broadcast_to(mine.astype(jnp.bfloat16)[None], pieces.shape)
-    return lax.all_to_all(shared, axes, 0, 0).reshape(part.shape).astype(jnp.float32)
+    mine = lax.psum_scatter(part, axes, scatter_dimension=0, tiled=True)
+    return lax.all_gather(mine, axes, axis=0, tiled=True)
 
 
 def split_flat(total, parts):

time: 999 us -> 1000 us (level)
  waiting for transfers between devices: 465 us -> 497 us
  starting transfers between devices: 37.9 us -> 17.6 us
    psum x2 -> x0, waiting for transfers between devices: 223 us -> none  [the longest x1 127 us: per_device_body(): early_b = lax.psum(early_b, ('row', 'col'))]
    reduce_scatter x0 -> x3, waiting for transfers between devices: none -> 196 us  [summed_in_two_steps(): mine = lax.psum_scatter(part, axes, scatter_dimension=0, tiled=True)]
    all_gather x0 -> x3, waiting for transfers between devices: none -> 94 us  [summed_in_two_steps(): return lax.all_gather(mine, axes, axis=0, tiled=True)]
    reduce_scatter x1, waiting for transfers between devices: 0.01 us -> 55.3 us  [per_device_body(): lax.psum_scatter(grad_nm_part, 'col', scatter_dimension=0, tiled=True)]
    all_to_all x2 -> x0, waiting for transfers between devices: 50.9 us -> none  [the longest x1 50.9 us: summed_all_by_exchange(): lax.all_to_all(pieces, axes, 0, 0).astype(jnp.float32)]
    ppermute x5, waiting for transfers between devices: 41.7 us -> 11 us  [summed_f32(): flat = flat + lax.ppermute(flat, axis, [(i, i ^ step) for i in range(n)])]
    all_to_all x3, waiting for transfers between devices: 108 us -> 90.9 us  [summed_by_exchange(): got = lax.all_to_all(pieces, axis, dim, dim, tiled=False)]
    ppermute x5, starting transfers between devices: 14.9 us -> 2.9 us  [summed_f32(): flat = flat + lax.ppermute(flat, axis, [(i, i ^ step) for i in range(n)])]
  transfers between devices with their start and end apart: 16 -> 18, of which waited for: 11 -> 12; matrix products, arithmetic and copies ran while one was open for 41% -> 37% of each run, Pallas kernels for 0% -> 0%
where the time goes in v7:
time: 1000 us; the launch traced here: 989 us
  waiting for transfers between devices  497 us (50%)
  matrix products  240 us (24%)
  local copies, waits for them, and re-layouts  114 us (11%)
  other arithmetic  103 us (10%)
  starting transfers between devices  17.6 us (2%)
  between operations  17.3 us (2%)
    reduce_scatter x3, waiting for transfers between devices, summed_in_two_steps(): mine = lax.psum_scatter(part, axes, scatter_dimension=0, tiled=True)  196 us
    all_gather x3, waiting for transfers between devices, summed_in_two_steps(): return lax.all_gather(mine, axes, axis=0, tiled=True)  94 us
    all_to_all x3, waiting for transfers between devices, summed_by_exchange(): got = lax.all_to_all(pieces, axis, dim, dim, tiled=False)  90.9 us
    reduce_scatter x1, waiting for transfers between devices, per_device_body(): lax.psum_scatter(grad_nm_part, 'col', scatter_dimension=0, tiled=True)  55.3 us
    all_gather x1, waiting for transfers between devices, per_device_body(): normed_all = lax.all_gather(normed_mid, 'col', axis=0, tiled=True)  48.1 us
    dot_general x7, matrix products, contract_rows(): lax.dot_general(left, right, (((0,), (0,)), ((), ())), preferred_element_...  37.1 us
    dot_general x7, matrix products, contract_cols(): lax.dot_general(left, right, (((1,), (1,)), ((), ())), preferred_element_...  32.1 us
    unnamed x374, local copies, waits for them, and re-layouts  23.2 us
  transfers between devices with their start and end apart: 18, of which 12 were waited for; matrix products, arithmetic and copies ran while one was open for 37% of the time, Pallas kernels for 0%

profile of v7, /device:TPU:0, one launch (start us, length us, event | category | flops | bytes accessed | tf_op | source)
XLA Modules:
  0.0 988.8 jit_solution(17941658125685633204)
XLA Ops:
  12.9 5.0 fusion.236
  18.7 6.9 fusion.5
  61.1 4.2 reshape.422
  93.2 4.6 fusion.27
  97.8 4.4 fusion.98
  127.2 7.0 multiply_convert_fusion.3
  138.8 4.1 multiply_reduce_fusion.7
  145.6 48.1 %all-gather.11.cloned.1.call-done = bf16[3072,1024]{1,0:T(8,128)(2,1)} async-done(((bf16[384,1024]{1,0:T(8,128)(2,1)}), bf16[3072,1024]{1,0:T(8,128)(2,1)}) %all-gather.11.cloned.1.call-update) | async-done | bytes 6291472 | tf_op jit(solution)/shard_map/all_gather | solution.py:235
  193.7 5.5 fusion.118
  199.3 4.5 fusion.122
  203.8 7.1 multiply_convert_fusion
  214.5 5.6 add_convert_fusion
  226.8 55.3 %reduce-scatter.5.cloned.1.call-done = bf16[384,1024]{1,0:T(8,128)(2,1)} async-done(((bf16[3072,1024]{1,0:T(8,128)(2,1)}), bf16[384,1024]{1,0:T(8,128)(2,1)}) %reduce-scatter.5.cloned.1.call-update) | async-done | bytes 786448 | tf_op jit(solution)/shard_map/reduce_scatter | solution.py:246
  287.8 5.7 fusion.170
  293.5 4.0 mul.840
  299.5 5.5 convolution_convert_fusion.3
  308.8 5.0 convolution_convert_fusion.2
  328.8 5.0 fusion.22
  333.8 5.5 convolution_add_fusion
  356.5 6.5 fusion.49
  363.0 56.8 %reduce-scatter.7.cloned.1.call-done = bf16[48,1024]{1,0:T(8,128)(2,1)} async-done(((bf16[1536,1024]{1,0:T(8,128)(2,1)}), bf16[48,1024]{1,0:T(8,128)(2,1)}) %reduce-scatter.7.cloned.1.call-update) | async-done | bytes 98320 | tf_op jit(solution)/shard_map/reduce_scatter | solution.py:311
  422.7 4.6 fusion.39
  431.3 4.6 fusion.9
  435.9 5.3 fusion.85
  443.4 7.7 fusion.6
  456.1 4.0 fusion.53
  460.2 4.1 multiply_reduce_fusion.8
  473.9 6.3 broadcast_multiply_fusion
  506.6 19.8 %reduce-scatter.9.cloned.1.call-done = bf16[32,1536]{1,0:T(8,128)(2,1)} async-done(((bf16[1024,1536]{1,0:T(8,128)(2,1)}), bf16[32,1536]{1,0:T(8,128)(2,1)}) %reduce-scatter.9.cloned.1.call-update) | async-done | bytes 98320 | tf_op jit(solution)/shard_map/reduce_scatter | solution.py:311
  526.4 5.2 add_add_fusion.4
  533.7 7.7 multiply_reduce_fusion.3
  548.0 6.2 convolution_convert_fusion
  554.2 33.3 %all-gather.13.cloned.1.call-done = bf16[1536,1024]{1,0:T(8,128)(2,1)} async-done(((bf16[48,1024]{1,0:T(8,128)(2,1)}), bf16[1536,1024]{1,0:T(8,128)(2,1)}) %all-gather.13.cloned.1.call-update) | async-done | bytes 3145744 | tf_op jit(solution)/shard_map/all_gather | solution.py:312
  587.5 60.7 %all-gather.15.cloned.1.call-done = bf16[1024,1536]{1,0:T(8,128)(2,1)} async-done(((bf16[32,1536]{1,0:T(8,128)(2,1)}), bf16[1024,1536]{1,0:T(8,128)(2,1)}) %all-gather.15.cloned.1.call-update) | async-done | bytes 3145744 | tf_op jit(solution)/shard_map/all_gather | solution.py:312
  648.2 119.9 %reduce-scatter.11.cloned.1.call-done = bf16[32,3072]{1,0:T(8,128)(2,1)} async-done(((bf16[1024,3072]{1,0:T(8,128)(2,1)}), bf16[32,3072]{1,0:T(8,128)(2,1)}) %reduce-scatter.11.cloned.1.call-update) | async-done | bytes 196624 | tf_op jit(solution)/shard_map/reduce_scatter | solution.py:311
  768.2 5.8 convolution_convert_fusion.6
  778.6 6.7 convolution_convert_fusion.5
  790.0 6.7 convolution_convert_fusion.4
  801.8 5.1 all-to-all-start.1
  806.8 8.0 convolution_convert_fusion.1
  814.8 46.0 %all-to-all-done.1 = bf16[2,4,256,352]{2,3,0,1:T(8,128)(2,1)} async-done(((bf16[2,4,256,352]{2,3,0,1:T(8,128)(2,1)}), bf16[2,4,256,352]{2,3,0,1:T(8,128)(2,1)}, u32[]{:S(2)}, u32[]{:S(2)}) %all-to-all-start.1) | async-done | bytes 1441824 | tf_op jit(solution)/shard_map/all_to_all | solution.py:305
  860.8 5.1 all-to-all-start
  882.1 4.9 fusion.252
  893.2 44.9 %all-to-all-done = bf16[8,384,1024]{2,1,0:T(8,128)(2,1)} async-done(((bf16[8,384,1024]{2,1,0:T(8,128)(2,1)}), bf16[8,384,1024]{2,1,0:T(8,128)(2,1)}, u32[]{:S(2)}, u32[]{:S(2)}) %all-to-all-start) | async-done | bytes 6291488 | tf_op jit(solution)/shard_map/all_to_all | solution.py:305
  938.1 4.4 convert_reduce_fusion
  947.5 5.8 collective-permute-done.3
  963.1 5.6 convert_element_type.137
  972.2 9.4 convert_element_type.136
  (602 shorter events, 267.3 us)
Async XLA Ops:
  7.2 131.6 %copy-start = (bf16[1536,1024]{1,0:T(8,128)(2,1)S(1)}, bf16[1536,1024]{1,0:T(8,128)(2,1)}, u32[]{:S(2)}) copy-start(bf16[1536,1024]{1,0:T(8,128)(2,1)} %param.25) | copy-start | bytes 9437188
  7.2 127.0 %all-gather.7.cloned.1.call-start = ((), (), s32[]{:S(2)}) async-start(), calls=%async_computation.7 | async-start | bytes 2703360 | tf_op jit(solution)/shard_map/all_gather | solution.py:225
  9.4 129.4 %all-gather.9.cloned.1.call-start = ((), (), s32[]{:S(2)}) async-start(), calls=%async_computation.8 | async-start | bytes 7077888 | tf_op jit(solution)/shard_map/all_gather | solution.py:227
  10.1 183.6 %all-gather.11.cloned.1.call-start = ((), (), s32[]{:S(2)}) async-start(), calls=%async_computation.9 | async-start | bytes 7077888 | tf_op jit(solution)/shard_map/all_gather | solution.py:235
  17.9 7.7 copy-start.2
  34.7 8.1 copy-start.119
  38.4 48.5 %copy-start.99 = (f32[6,64,6]{1,2,0:T(8,128)}, f32[6,64,6]{1,2,0:T(8,128)S(1)}, u32[]{:S(2)}) copy-start(f32[6,64,6]{1,2,0:T(8,128)S(1)} %copy.342) | copy-start | bytes 27652
  38.5 76.7 %copy-start.79 = (pred[6,64,64]{1,2,0:T(8,128)(4,1)}, pred[6,64,64]{1,2,0:T(8,128)(4,1)S(1)}, u32[]{:S(2)}) copy-start(pred[6,64,64]{1,2,0:T(8,128)(4,1)S(1)} %compare_and_fusion) | copy-start | bytes 73732
  39.9 75.4 %copy-start.57 = (f32[6,6,64]{2,1,0:T(8,128)}, f32[6,6,64]{2,1,0:T(8,128)S(1)}, u32[]{:S(2)}) copy-start(f32[6,6,64]{2,1,0:T(8,128)S(1)} %reduce_window_sum.22) | copy-start | bytes 27652
  39.9 75.3 %copy-start.101 = (f32[6,6,64]{2,1,0:T(8,128)}, f32[6,6,64]{2,1,0:T(8,128)S(1)}, u32[]{:S(2)}) copy-start(f32[6,6,64]{2,1,0:T(8,128)S(1)} %get-tuple-element.96) | copy-start | bytes 27652
  39.9 11.9 %slice-start.6 = ((s8[4718592]{0:T(1024)(128)(4,1)}), s8[4194304]{0:T(1024)(128)(4,1)S(1)}, s32[]{:S(2)}) async-start(s8[4718592]{0:T(1024)(128)(4,1)} %bitcast.418), calls=%async_computation.23 | async-start | bytes 8388608
  42.8 8.9 slice-start.7
  67.4 44.8 %copy-start.107 = (f32[6,64,6]{1,2,0:T(8,128)}, f32[6,64,6]{1,2,0:T(8,128)S(1)}, u32[]{:S(2)}) copy-start(f32[6,64,6]{1,2,0:T(8,128)S(1)} %copy.178) | copy-start | bytes 27652
  67.6 36.5 %copy-start.155 = (f32[6]{0:T(128)}, f32[6]{0:T(128)S(1)}, u32[]{:S(2)}) copy-start(f32[6]{0:T(128)S(1)} %get-tuple-element.87) | copy-start | bytes 76
  86.7 11.1 %copy-start.110 = (f32[6,6,64]{2,1,0:T(8,128)}, f32[6,6,64]{2,1,0:T(8,128)S(1)}, u32[]{:S(2)}) copy-start(f32[6,6,64]{2,1,0:T(8,128)S(1)} %slice_reduce_fusion) | copy-start | bytes 27652
  93.1 15.8 %copy-start.9 = (f32[6,6,64,384]{3,2,1,0:T(8,128)}, f32[6,6,64,384]{3,2,1,0:T(8,128)S(1)}, u32[]{:S(2)}) copy-start(f32[6,6,64,384]{3,2,1,0:T(8,128)S(1)} %fusion.8) | copy-start | bytes 10616836
  145.4 136.6 %reduce-scatter.5.cloned.1.call-start = ((), (), s32[]{:S(2)}) async-start(), calls=%async_computation.10 | async-start | bytes 7077888 | tf_op jit(solution)/shard_map/reduce_scatter | solution.py:246
  193.7 10.1 %slice-start.10 = ((s8[6291456]{0:T(1024)(128)(4,1)}), s8[4194304]{0:T(1024)(128)(4,1)S(1)}, s32[]{:S(2)}) async-start(s8[6291456]{0:T(1024)(128)(4,1)} %bitcast.480), calls=%async_computation.27 | async-start | bytes 8388608
  220.1 199.6 %reduce-scatter.7.cloned.1.call-start = ((), (), s32[]{:S(2)}) async-start(), calls=%async_computation.11 | async-start | bytes 3244032 | tf_op jit(solution)/shard_map/reduce_scatter | solution.py:311
  317.4 208.9 %reduce-scatter.9.cloned.1.call-start = ((), (), s32[]{:S(2)}) async-start(), calls=%async_computation.13 | async-start | bytes 3244032 | tf_op jit(solution)/shard_map/reduce_scatter | solution.py:311
  318.0 269.4 %all-gather.13.cloned.1.call-start = ((), (), s32[]{:S(2)}) async-start(), calls=%async_computation.12 | async-start | bytes 3244032 | tf_op jit(solution)/shard_map/all_gather | solution.py:312
  328.7 27.7 %copy-start.19 = (f32[6,6,64,256]{3,2,1,0:T(8,128)}, f32[6,6,64,256]{3,2,1,0:T(8,128)S(1)}, u32[]{:S(2)}) copy-start(f32[6,6,64,256]{3,2,1,0:T(8,128)S(1)} %fusion.16) | copy-start | bytes 7077892
  333.8 22.7 %slice-start.2 = ((s8[4718592]{0:T(1024)(128)(4,1)}), s8[4194304]{0:T(1024)(128)(4,1)S(1)}, s32[]{:S(2)}) async-start(s8[4718592]{0:T(1024)(128)(4,1)} %bitcast.414), calls=%async_computation.19 | async-start | bytes 8388608
  339.3 9.3 copy-start.16
  343.2 11.2 %copy-start.91 = (f32[1,6,128,128]{3,2,1,0:T(8,128)}, f32[1,6,128,128]{3,2,1,0:T(8,128)S(1)}, u32[]{:S(2)}) copy-start(f32[1,6,128,128]{3,2,1,0:T(8,128)S(1)} %convolution_bitcast_fusion.3) | copy-start | bytes 1179652
  343.2 13.3 %slice-start.3 = ((s8[4718592]{0:T(1024)(128)(4,1)}), s8[524288]{0:T(1024)(128)(4,1)S(1)}, s32[]{:S(2)}) async-start(s8[4718592]{0:T(1024)(128)(4,1)} %bitcast.414), calls=%async_computation.20 | async-start | bytes 1048576
  346.2 8.3 copy-start.93
  419.8 228.4 %all-gather.15.cloned.1.call-start = ((), (), s32[]{:S(2)}) async-start(), calls=%async_computation.14 | async-start | bytes 3244032 | tf_op jit(solution)/shard_map/all_gather | solution.py:312
  443.4 7.7 copy-start.31
  443.4 7.7 copy-start.34
  443.4 7.8 copy-start.37
  466.0 7.8 slice-start.4
  504.1 27.6 %slice-start.8 = ((s8[4718592]{0:T(1024)(128)(4,1)}), s8[524288]{0:T(1024)(128)(4,1)S(1)}, s32[]{:S(2)}) async-start(s8[4718592]{0:T(1024)(128)(4,1)} %bitcast.420), calls=%async_computation.25 | async-start | bytes 1048576
  526.4 241.8 %reduce-scatter.11.cloned.1.call-start = ((), (), s32[]{:S(2)}) async-start(), calls=%async_computation.15 | async-start | bytes 6488064 | tf_op jit(solution)/shard_map/reduce_scatter | solution.py:311
  533.7 7.7 copy-start.132
  533.7 7.7 copy-start.154
  648.2 324.0 %all-gather.17.cloned.1.call-start = ((), (), s32[]{:S(2)}) async-start(), calls=%async_computation.16 | async-start | bytes 6488064 | tf_op jit(solution)/shard_map/all_gather | solution.py:312
  774.9 26.8 %all-to-all-start.2 = ((bf16[352,4,256]{2,0,1:T(8,128)(2,1)}), bf16[352,4,256]{2,0,1:T(8,128)(2,1)S(1)}, u32[]{:S(2)}, u32[]{:S(2)}) async-start(bf16[352,4,256]{2,0,1:T(8,128)(2,1)} %bitcast.447), calls=%async_computation.6 | async-start | bytes 1441792 | tf_op jit(solution)/shard_map/all_to_all | solution.py:305
  801.8 13.0 %copy-start.84 = (bf16[352,4,256]{2,0,1:T(8,128)(2,1)}, bf16[352,4,256]{2,0,1:T(8,128)(2,1)S(1)}, u32[]{:S(2)}) copy-start(bf16[352,4,256]{2,0,1:T(8,128)(2,1)S(1)} %all-to-all-done.2) | copy-start | bytes 2162692
  801.8 59.0 %all-to-all-start.1 = ((bf16[2,4,256,352]{2,3,0,1:T(8,128)(2,1)}), bf16[2,4,256,352]{2,3,0,1:T(8,128)(2,1)}, u32[]{:S(2)}, u32[]{:S(2)}) async-start(bf16[2,4,256,352]{2,3,0,1:T(8,128)(2,1)} %pad_maximum_fusion.3), calls=%async_computation.5 | async-start | bytes 2883584 | tf_op jit(solution)/shard_map/all_to_all | solution.py:305
  860.8 77.3 %all-to-all-start = ((bf16[8,384,1024]{2,1,0:T(8,128)(2,1)}), bf16[8,384,1024]{2,1,0:T(8,128)(2,1)}, u32[]{:S(2)}, u32[]{:S(2)}) async-start(bf16[8,384,1024]{2,1,0:T(8,128)(2,1)} %bitcast.438), calls=%async_computation | async-start | bytes 12582912 | tf_op jit(solution)/shard_map/all_to_all | solution.py:305
  888.5 2.9 collective-permute-start
  891.5 51.0 %collective-permute-start.1 = (f32[26892]{0:T(1024)S(1)}, f32[26892]{0:T(1024)S(1)}, u32[]{:S(2)}, u32[]{:S(2)}) collective-permute-start(f32[26892]{0:T(1024)S(1)} %add.275), channel_id=1, source_target_pairs={{0,2},{1,3},{2,0},{3,1},{4,6},{5,7},{6,4},{7,5},{8,10},{9,11},{10,... | collective-permute-start | bytes 322712 | tf_op jit(solution)/shard_map/ppermute | solution.py:332
  942.6 10.8 %copy-start.71 = (f32[384,1024]{1,0:T(8,128)S(1)}, f32[384,1024]{1,0:T(8,128)}, u32[]{:S(2)}) copy-start(f32[384,1024]{1,0:T(8,128)} %copy-done.70) | copy-start | bytes 4718596
  942.6 4.8 collective-permute-start.2
  947.4 5.9 collective-permute-start.3
  953.3 5.9 collective-permute-start.4
  972.2 9.4 copy-start.1
  (150 other events, 528.5 us)
Sparse Core Ops, SparseCore 0:
  10.2 50.0 all-gather.6
  62.1 43.5 all-gather.8
  145.5 48.1 all-gather.10
  220.2 61.7 reduce-scatter.4
  317.5 102.1 reduce-scatter.6
  425.1 101.2 reduce-scatter.8
  529.2 58.2 all-gather.12
  590.3 57.8 all-gather.14
  654.4 113.7 reduce-scatter.10
  770.9 92.3 all-gather.16

commit v8 on v7

--- a/solution.py
+++ b/solution.py
@@ -245,7 +245,7 @@
     ).astype(jnp.bfloat16)
     grad_normed_mid = lax.psum_scatter(grad_nm_part, "col", scatter_dimension=0, tiled=True)
     grad_normed_mid = grad_normed_mid.astype(jnp.float32)
-    ffn_out = summed_by_exchange(ffn_part, "col", 0)
+    ffn_out = lax.psum_scatter(ffn_part, "col", scatter_dimension=0, tiled=True)
     grad_gate_up, grad_down = (
         summed_by_exchange(grad_gu_part.astype(jnp.bfloat16), "row", 1),
         summed_by_exchange(grad_down_part.astype(jnp.bfloat16), "row", 1),
@@ -260,14 +260,14 @@
     grad_gate_o = contract_rows(normed_in, grad_gate_b)
     early_b = (grad_out.astype(jnp.bfloat16), grad_gate_o.astype(jnp.bfloat16))
     early_b, grad_delta = lax.optimization_barrier((early_b, grad_delta))
-    early_b = tuple(summed_in_two_steps(e) for e in early_b)
+    early_b = lax.psum(early_b, ("row", "col"))
     early = [e.astype(jnp.float32) for e in early_b]
     grad_raw, grad_logits, grad_conv, grad_a_log, grad_dt_bias = core_back(grad_delta)
     grad_raw_b = grad_raw.astype(jnp.bfloat16)
     grad_logits_b = grad_logits.astype(jnp.bfloat16)
     grad_qkv = contract_rows(normed_in, grad_raw_b)
     grad_decay = contract_rows(normed_in, grad_logits_b)
-    block_out = (middle_out + ffn_out).astype(jnp.bfloat16)
+    block_out = (middle_out + ffn_out.astype(jnp.float32)).astype(jnp.bfloat16)
     grad_normed_in = (
         contract_cols(grad_raw_b, w_qkv)
         + contract_cols(grad_logits_b, w_decay)
@@ -276,7 +276,7 @@
     grad_in_norm, grad_gain_in = norm_in_back(grad_normed_in)
     grad_tokens = grad_middle + grad_in_norm
     qkv_b, _ = lax.optimization_barrier((grad_qkv.astype(jnp.bfloat16), early_b))
-    late = [summed_in_two_steps(qkv_b).astype(jnp.float32)]
+    late = [lax.psum(qkv_b, ("row", "col")).astype(jnp.float32)]
     small = summed_f32(
         (grad_gain_in, grad_conv, grad_decay, grad_a_log, grad_dt_bias, grad_gain_o, grad_gain_mid)
     )
@@ -306,12 +306,6 @@
     return jnp.sum(got.astype(jnp.float32), axis=dim)
 
 
-def summed_in_two_steps(part):
-    axes = ("row", "col")
-    mine = lax.psum_scatter(part, axes, scatter_dimension=0, tiled=True)
-    return lax.all_gather(mine, axes, axis=0, tiled=True)
-
-
 def split_flat(total, parts):
     out, at = [], 0
     for p in parts:

time: 1000 us -> 738 us (0.74)
  waiting for transfers between devices: 497 us -> 258 us
  local copies, waits for them, and re-layouts: 114 us -> 101 us
    reduce_scatter x3 -> x1, waiting for transfers between devices: 196 us -> 0.01 us  [per_device_body(): ffn_out = lax.psum_scatter(ffn_part, 'col', scatter_dimension=0, tiled=True)]
    psum x0 -> x2, waiting for transfers between devices: none -> 132 us  [the longest x1 132 us: per_device_body(): late = [lax.psum(qkv_b, ('row', 'col')).astype(jnp.float32)]]
    all_gather x3 -> x0, waiting for transfers between devices: 94 us -> none  [summed_in_two_steps(): return lax.all_gather(mine, axes, axis=0, tiled=True)]
    all_to_all x3 -> x2, waiting for transfers between devices: 90.9 us -> 11.6 us  [summed_by_exchange(): got = lax.all_to_all(pieces, axis, dim, dim, tiled=False)]
    unnamed x374 -> x306, local copies, waits for them, and re-layouts: 23.2 us -> 20.8 us
  transfers between devices with their start and end apart: 18 -> 14, of which waited for: 12 -> 7; matrix products, arithmetic and copies ran while one was open for 37% -> 48% of each run, Pallas kernels for 0% -> 0%
where the time goes in v8:
time: 738 us; the launch traced here: 728 us
  waiting for transfers between devices  258 us (35%)
  matrix products  234 us (32%)
  other arithmetic  104 us (14%)
  local copies, waits for them, and re-layouts  101 us (14%)
  between operations  16.4 us (2%)
  starting transfers between devices  14.5 us (2%)
    psum x1, waiting for transfers between devices, per_device_body(): late = [lax.psum(qkv_b, ('row', 'col')).astype(jnp.float32)]  132 us
    reduce_scatter x1, waiting for transfers between devices, per_device_body(): lax.psum_scatter(grad_nm_part, 'col', scatter_dimension=0, tiled=True)  55 us
    all_gather x1, waiting for transfers between devices, per_device_body(): normed_all = lax.all_gather(normed_mid, 'col', axis=0, tiled=True)  48.6 us
    dot_general x7, matrix products, contract_rows(): lax.dot_general(left, right, (((0,), (0,)), ((), ())), preferred_element_...  35.7 us
    dot_general x7, matrix products, contract_cols(): lax.dot_general(left, right, (((1,), (1,)), ((), ())), preferred_element_...  34.5 us
    unnamed x306, local copies, waits for them, and re-layouts  20.8 us
    dot_general x10, matrix products, _mm(): return jnp.einsum('...ij,...jk->...ik', a, b, precision=HI)  16.8 us
  transfers between devices with their start and end apart: 14, of which 7 were waited for; matrix products, arithmetic and copies ran while one was open for 48% of the time, Pallas kernels for 0%

profile of v8, /device:TPU:0, one launch (start us, length us, event | category | flops | bytes accessed | tf_op | source)
XLA Modules:
  0.0 727.7 jit_solution(14982151389918584998)
XLA Ops:
  11.7 5.0 fusion.236
  16.9 6.2 fusion.5
  44.7 3.6 fusion.74
  57.7 4.0 reshape.419
  89.9 4.6 fusion.27
  94.6 4.6 fusion.98
  123.9 7.0 multiply_convert_fusion.3
  140.9 48.6 %all-gather.8.cloned.1.call-done = bf16[3072,1024]{1,0:T(8,128)(2,1)} async-done(((bf16[384,1024]{1,0:T(8,128)(2,1)}), bf16[3072,1024]{1,0:T(8,128)(2,1)}) %all-gather.8.cloned.1.call-update) | async-done | bytes 6291472 | tf_op jit(solution)/shard_map/all_gather | solution.py:235
  189.5 5.5 fusion.118
  195.1 4.5 fusion.122
  199.6 7.1 multiply_convert_fusion
  206.7 3.5 fusion.120
  210.2 5.6 add_convert_fusion
  222.8 55.0 %reduce-scatter.5.cloned.1.call-done = bf16[384,1024]{1,0:T(8,128)(2,1)} async-done(((bf16[3072,1024]{1,0:T(8,128)(2,1)}), bf16[384,1024]{1,0:T(8,128)(2,1)}) %reduce-scatter.5.cloned.1.call-update) | async-done | bytes 786448 | tf_op jit(solution)/shard_map/reduce_scatter | solution.py:246
  283.3 5.7 fusion.170
  289.1 4.0 mul.840
  295.0 5.4 convolution_convert_fusion.3
  302.2 5.1 convolution_convert_fusion.2
  307.3 3.6 add_add_fusion
  312.6 6.7 convolution_convert_fusion.5
  322.4 5.3 convolution_convert_fusion.4
  328.4 6.1 convolution_convert_fusion.6
  335.4 4.6 all-to-all-start.1
  342.4 5.4 convolution_convert_fusion.1
  350.0 4.9 fusion.14
  355.0 5.0 fusion.22
  362.5 4.5 convolution_add_fusion
  381.4 5.6 fusion.9
  389.1 5.1 fusion.49
  394.2 5.6 fusion.6
  399.8 5.5 fusion.7
  407.8 6.3 broadcast_multiply_fusion
  423.2 6.4 fusion.85
  431.1 3.8 fusion.53
  434.9 4.9 multiply_reduce_fusion.8
  476.4 5.2 add_add_fusion.4
  483.0 6.1 multiply_reduce_fusion.3
  499.1 9.2 %add_convert_fusion.1 = bf16[384,3072]{1,0:T(8,128)(2,1)} fusion(f32[384,3072]{1,0:T(8,128)} %copy-done.3, f32[383,3072]{1,0:T(8,128)} %fusion.2, f32[382,3072]{1,0:T(8,128)} %fusion.3, f32[381,3072]{1,0:T(8,128)} %fusion.4, f32[3072]{0:T(1024)S(1)} %bitcast.456), kind=kLoop, calls=%fused_computation.16 | loop fusion | flops 5898240 | bytes 21172224 | tf_op jit(solution)/shard_map/convert_element_type | solution.py:266
  508.4 5.0 all-to-all-start
  513.4 4.9 fusion.253
  518.4 5.7 convolution_convert_fusion
  524.1 5.7 fusion.252
  535.4 11.6 %all-to-all-done = bf16[2,4,256,352]{2,3,0,1:T(8,128)(2,1)S(1)} async-done(((bf16[2,4,256,352]{2,3,0,1:T(8,128)(2,1)}), bf16[2,4,256,352]{2,3,0,1:T(8,128)(2,1)S(1)}, u32[]{:S(2)}, u32[]{:S(2)}) %all-to-all-start) | async-done | bytes 1441824 | tf_op jit(solution)/shard_map/all_to_all | solution.py:305
  553.0 3.6 fusion.45
  560.9 5.3 collective-permute-done.4
  570.2 5.6 convert_element_type.137
  579.3 132.0 %all-reduce.41.cloned.1.call-done = bf16[1024,3072]{1,0:T(8,128)(2,1)} async-done(((bf16[1024,3072]{1,0:T(8,128)(2,1)}), bf16[1024,3072]{1,0:T(8,128)(2,1)}) %all-reduce.41.cloned.1.call-update) | async-done | bytes 6291472 | tf_op jit(solution)/shard_map/psum | solution.py:279
  711.3 9.4 %convert_element_type.136 = f32[1024,3072]{1,0:T(8,128)} convert(bf16[1024,3072]{1,0:T(8,128)(2,1)} %all-reduce.41.cloned.1.call-done) | non-fusion elementwise | flops 3145728 | bytes 18874368 | tf_op jit(solution)/shard_map/convert_element_type | solution.py:279
  (521 shorter events, 227.5 us)
Async XLA Ops:
  7.2 128.3 %copy-start = (bf16[1536,1024]{1,0:T(8,128)(2,1)S(1)}, bf16[1536,1024]{1,0:T(8,128)(2,1)}, u32[]{:S(2)}) copy-start(bf16[1536,1024]{1,0:T(8,128)(2,1)} %param.25) | copy-start | bytes 9437188
  7.2 123.6 %all-gather.4.cloned.1.call-start = ((), (), s32[]{:S(2)}) async-start(), calls=%async_computation.4 | async-start | bytes 2703360 | tf_op jit(solution)/shard_map/all_gather | solution.py:225
  9.4 126.1 %all-gather.6.cloned.1.call-start = ((), (), s32[]{:S(2)}) async-start(), calls=%async_computation.5 | async-start | bytes 7077888 | tf_op jit(solution)/shard_map/all_gather | solution.py:227
  10.1 179.4 %all-gather.8.cloned.1.call-start = ((), (), s32[]{:S(2)}) async-start(), calls=%async_computation.6 | async-start | bytes 7077888 | tf_op jit(solution)/shard_map/all_gather | solution.py:235
  16.8 6.3 copy-start.2
  31.2 9.2 %copy-start.100 = (pred[64,64]{0,1:T(8,128)(4,1)}, pred[64,64]{0,1:T(8,128)(4,1)S(1)}, u32[]{:S(2)}) copy-start(pred[64,64]{0,1:T(8,128)(4,1)S(1)} %iota_compare_fusion.3) | copy-start | bytes 12292
  35.9 47.2 %copy-start.90 = (f32[6,64,6]{1,2,0:T(8,128)}, f32[6,64,6]{1,2,0:T(8,128)S(1)}, u32[]{:S(2)}) copy-start(f32[6,64,6]{1,2,0:T(8,128)S(1)} %copy.342) | copy-start | bytes 27652
  37.5 10.8 %slice-start.4 = ((s8[4718592]{0:T(1024)(128)(4,1)}), s8[4194304]{0:T(1024)(128)(4,1)S(1)}, s32[]{:S(2)}) async-start(s8[4718592]{0:T(1024)(128)(4,1)} %bitcast.415), calls=%async_computation.15 | async-start | bytes 8388608
  40.4 7.9 %slice-start.5 = ((s8[4718592]{0:T(1024)(128)(4,1)}), s8[524288]{0:T(1024)(128)(4,1)S(1)}, s32[]{:S(2)}) async-start(s8[4718592]{0:T(1024)(128)(4,1)} %bitcast.415), calls=%async_computation.16 | async-start | bytes 1048576
  89.9 16.0 %copy-start.13 = (f32[6,6,64,384]{3,2,1,0:T(8,128)}, f32[6,6,64,384]{3,2,1,0:T(8,128)S(1)}, u32[]{:S(2)}) copy-start(f32[6,6,64,384]{3,2,1,0:T(8,128)S(1)} %fusion.8) | copy-start | bytes 10616836
  94.5 7.5 %copy-start.25 = (f32[6,6,128,256]{3,2,1,0:T(8,128)}, f32[6,6,128,256]{3,2,1,0:T(8,128)S(1)}, u32[]{:S(2)}) copy-start(f32[6,6,128,256]{3,2,1,0:T(8,128)S(1)} %fusion.27) | copy-start | bytes 14155780
  105.9 6.0 copy-start.31
  140.7 137.1 %reduce-scatter.5.cloned.1.call-start = ((), (), s32[]{:S(2)}) async-start(), calls=%async_computation.8 | async-start | bytes 7077888 | tf_op jit(solution)/shard_map/reduce_scatter | solution.py:246
  189.5 10.1 %slice-start.8 = ((s8[6291456]{0:T(1024)(128)(4,1)}), s8[4194304]{0:T(1024)(128)(4,1)S(1)}, s32[]{:S(2)}) async-start(s8[6291456]{0:T(1024)(128)(4,1)} %bitcast.475), calls=%async_computation.19 | async-start | bytes 8388608
  215.9 308.2 %all-reduce.43.cloned.1.call-start = ((), (), s32[]{:S(2)}) async-start(), calls=%async_computation.10 | async-start | bytes 12582912 | tf_op jit(solution)/shard_map/psum | solution.py:263
  282.5 6.6 copy-start.66
  335.4 173.0 %all-to-all-start.1 = ((bf16[352,4,256]{2,0,1:T(8,128)(2,1)}), bf16[352,4,256]{2,0,1:T(8,128)(2,1)}, u32[]{:S(2)}, u32[]{:S(2)}) async-start(bf16[352,4,256]{2,0,1:T(8,128)(2,1)} %bitcast.394), calls=%async_computation.3 | async-start | bytes 1441792 | tf_op jit(solution)/shard_map/all_to_all | solution.py:305
  340.0 218.7 %reduce-scatter.3.cloned.1.call-start = ((), (), s32[]{:S(2)}) async-start(), calls=%async_computation.7 | async-start | bytes 7077888 | tf_op jit(solution)/shard_map/reduce_scatter | solution.py:248
  350.0 10.0 %copy-start.7 = (f32[384,6,256]{2,0,1:T(8,128)}, f32[384,6,256]{2,0,1:T(8,128)S(1)}, u32[]{:S(2)}) copy-start(f32[384,6,256]{2,0,1:T(8,128)S(1)} %copy.207) | copy-start | bytes 7077892
  355.0 50.3 %copy-start.34 = (f32[6,6,64,64]{2,3,1,0:T(8,128)}, f32[6,6,64,64]{2,3,1,0:T(8,128)S(1)}, u32[]{:S(2)}) copy-start(f32[6,6,64,64]{2,3,1,0:T(8,128)S(1)} %fusion.14) | copy-start | bytes 1769476
  367.0 11.1 %copy-start.24 = (f32[6,6,128,256]{3,2,1,0:T(8,128)}, f32[6,6,128,256]{3,2,1,0:T(8,128)S(1)}, u32[]{:S(2)}) copy-start(f32[6,6,128,256]{3,2,1,0:T(8,128)S(1)} %convolution_add_fusion) | copy-start | bytes 14155780
  368.7 18.3 %copy-start.81 = (f32[1,6,128,128]{3,2,1,0:T(8,128)}, f32[1,6,128,128]{3,2,1,0:T(8,128)S(1)}, u32[]{:S(2)}) copy-start(f32[1,6,128,128]{3,2,1,0:T(8,128)S(1)} %convolution_bitcast_fusion.3) | copy-start | bytes 1179652
  370.9 16.2 %copy-start.83 = (f32[1,6,128,128]{3,2,1,0:T(8,128)}, f32[1,6,128,128]{3,2,1,0:T(8,128)S(1)}, u32[]{:S(2)}) copy-start(f32[1,6,128,128]{3,2,1,0:T(8,128)S(1)} %convolution_bitcast_fusion.2) | copy-start | bytes 1179652
  372.8 14.2 %copy-start.85 = (f32[1,6,128,128]{3,2,1,0:T(8,128)}, f32[1,6,128,128]{3,2,1,0:T(8,128)S(1)}, u32[]{:S(2)}) copy-start(f32[1,6,128,128]{3,2,1,0:T(8,128)S(1)} %convolution_bitcast_fusion.1) | copy-start | bytes 1179652
  377.2 9.9 %copy-start.87 = (f32[1,6,128,128]{3,2,1,0:T(8,128)}, f32[1,6,128,128]{3,2,1,0:T(8,128)S(1)}, u32[]{:S(2)}) copy-start(f32[1,6,128,128]{3,2,1,0:T(8,128)S(1)} %convolution_bitcast_fusion) | copy-start | bytes 1179652
  378.6 10.4 %slice-start.2 = ((s8[4718592]{0:T(1024)(128)(4,1)}), s8[4194304]{0:T(1024)(128)(4,1)S(1)}, s32[]{:S(2)}) async-start(s8[4718592]{0:T(1024)(128)(4,1)} %bitcast.413), calls=%async_computation.13 | async-start | bytes 8388608
  381.4 7.6 %slice-start.3 = ((s8[4718592]{0:T(1024)(128)(4,1)}), s8[524288]{0:T(1024)(128)(4,1)S(1)}, s32[]{:S(2)}) async-start(s8[4718592]{0:T(1024)(128)(4,1)} %bitcast.413), calls=%async_computation.14 | async-start | bytes 1048576
  394.2 5.7 copy-start.37
  394.2 5.7 copy-start.40
  394.2 5.7 copy-start.43
  423.1 7.9 %copy-start.20 = (f32[6,64,6,128]{3,2,1,0:T(8,128)S(1)}, f32[6,64,6,128]{3,2,1,0:T(8,128)}, u32[]{:S(2)}) copy-start(f32[6,64,6,128]{3,2,1,0:T(8,128)} %reshape.412) | copy-start | bytes 3538948
  423.1 7.9 %copy-start.99 = (f32[6,6,64]{2,1,0:T(8,128)S(1)}, f32[6,6,64]{2,1,0:T(8,128)}, u32[]{:S(2)}) copy-start(f32[6,6,64]{2,1,0:T(8,128)} %copy-done.98) | copy-start | bytes 27652
  475.1 6.6 slice-start.6
  476.4 5.8 slice-start.7
  476.4 6.6 copy-start.59
  483.0 6.2 copy-start.113
  489.1 6.6 copy-start.3
  508.4 38.6 %all-to-all-start = ((bf16[2,4,256,352]{2,3,0,1:T(8,128)(2,1)}), bf16[2,4,256,352]{2,3,0,1:T(8,128)(2,1)S(1)}, u32[]{:S(2)}, u32[]{:S(2)}) async-start(bf16[2,4,256,352]{2,3,0,1:T(8,128)(2,1)} %pad_maximum_fusion.3), calls=%async_computation.2 | async-start | bytes 2883584 | tf_op jit(solution)/shard_map/all_to_all | solution.py:305
  513.4 197.9 %all-reduce.41.cloned.1.call-start = ((), (), s32[]{:S(2)}) async-start(), calls=%async_computation.9 | async-start | bytes 12582912 | tf_op jit(solution)/shard_map/psum | solution.py:279
  524.1 5.8 copy-start.89
  524.1 5.8 copy-start.121
  531.9 2.0 collective-permute-start
  533.9 15.8 %copy-start.124 = (f32[384]{0:T(512)S(1)}, f32[384]{0:T(512)}, u32[]{:S(2)}) copy-start(f32[384]{0:T(512)} %copy-done.123) | copy-start | bytes 4612
  533.9 14.2 %collective-permute-start.1 = (f32[26892]{0:T(1024)S(1)}, f32[26892]{0:T(1024)S(1)}, u32[]{:S(2)}, u32[]{:S(2)}) collective-permute-start(f32[26892]{0:T(1024)S(1)} %add.277), channel_id=1, source_target_pairs={{0,2},{1,3},{2,0},{3,1},{4,6},{5,7},{6,4},{7,5},{8,10},{9,11},{10,... | collective-permute-start | bytes 322712 | tf_op jit(solution)/shard_map/ppermute | solution.py:326
  548.1 4.8 collective-permute-start.2
  552.9 4.8 collective-permute-start.3
  557.8 8.5 %collective-permute-start.4 = (f32[26892]{0:T(1024)S(1)}, f32[26892]{0:T(1024)S(1)}, u32[]{:S(2)}, u32[]{:S(2)}) collective-permute-start(f32[26892]{0:T(1024)S(1)} %add.280), channel_id=1, source_target_pairs={{0,16},{8,24},{16,0},{24,8},{1,17},{9,25},{17,1},{25,9},{2,18},{10... | collective-permute-start | bytes 322712 | tf_op jit(solution)/shard_map/ppermute | solution.py:326
  711.3 9.4 %copy-start.1 = (bf16[1536,1024]{1,0:T(8,128)(2,1)S(1)}, bf16[1536,1024]{1,0:T(8,128)(2,1)}, u32[]{:S(2)}) copy-start(bf16[1536,1024]{1,0:T(8,128)(2,1)} %param.25) | copy-start | bytes 9437188
  (112 other events, 382.2 us)
Sparse Core Ops, SparseCore 0:
  10.2 50.0 all-gather.3
  62.1 43.5 all-gather.5
  140.8 48.6 all-gather.7
  216.0 61.7 reduce-scatter.4
  311.0 170.0 all-reduce.42
  485.0 63.8 reduce-scatter.2
  555.1 156.1 all-reduce.40

commit v9 on v8

--- a/solution.py
+++ b/solution.py
@@ -245,7 +245,7 @@
     ).astype(jnp.bfloat16)
     grad_normed_mid = lax.psum_scatter(grad_nm_part, "col", scatter_dimension=0, tiled=True)
     grad_normed_mid = grad_normed_mid.astype(jnp.float32)
-    ffn_out = lax.psum_scatter(ffn_part, "col", scatter_dimension=0, tiled=True)
+    ffn_out = summed_by_exchange(ffn_part, "col", 0)
     grad_gate_up, grad_down = (
         summed_by_exchange(grad_gu_part.astype(jnp.bfloat16), "row", 1),
         summed_by_exchange(grad_down_part.astype(jnp.bfloat16), "row", 1),
@@ -257,17 +257,20 @@
     grad_mixed = contract_cols(grad_middle_b, w_out)
     grad_delta, grad_gate_out, grad_gain_o = out_norm_back(grad_mixed)
     grad_gate_b = grad_gate_out.astype(jnp.bfloat16)
-    grad_gate_o = contract_rows(normed_in, grad_gate_b)
-    early_b = (grad_out.astype(jnp.bfloat16), grad_gate_o.astype(jnp.bfloat16))
+    grad_gate_o_t = contract_rows(grad_gate_b, normed_in)
+    early_b = jnp.concatenate(
+        [grad_out.astype(jnp.bfloat16), grad_gate_o_t.astype(jnp.bfloat16)], axis=0
+    )
     early_b, grad_delta = lax.optimization_barrier((early_b, grad_delta))
     early_b = lax.psum(early_b, ("row", "col"))
-    early = [e.astype(jnp.float32) for e in early_b]
+    rows_out = grad_out.shape[0]
+    early = [early_b[:rows_out].astype(jnp.float32), early_b[rows_out:].T.astype(jnp.float32)]
     grad_raw, grad_logits, grad_conv, grad_a_log, grad_dt_bias = core_back(grad_delta)
     grad_raw_b = grad_raw.astype(jnp.bfloat16)
     grad_logits_b = grad_logits.astype(jnp.bfloat16)
     grad_qkv = contract_rows(normed_in, grad_raw_b)
     grad_decay = contract_rows(normed_in, grad_logits_b)
-    block_out = (middle_out + ffn_out.astype(jnp.float32)).astype(jnp.bfloat16)
+    block_out = (middle_out + ffn_out).astype(jnp.bfloat16)
     grad_normed_in = (
         contract_cols(grad_raw_b, w_qkv)
         + contract_cols(grad_logits_b, w_decay)

time: 738 us -> 796 us (1.079)
  waiting for transfers between devices: 258 us -> 297 us
  local copies, waits for them, and re-layouts: 101 us -> 111 us
    psum x1, waiting for transfers between devices: 0.01 us -> 102 us  [per_device_body(): early_b = lax.psum(early_b, ('row', 'col'))]
    reduce_scatter x1, waiting for transfers between devices: 55 us -> 0.01 us  [per_device_body(): lax.psum_scatter(grad_nm_part, 'col', scatter_dimension=0, tiled=True)]
    psum x1, waiting for transfers between devices: 132 us -> 120 us  [per_device_body(): late = [lax.psum(qkv_b, ('row', 'col')).astype(jnp.float32)]]
    unnamed x306 -> x361, local copies, waits for them, and re-layouts: 20.8 us -> 29.9 us
  transfers between devices with their start and end apart: 14 -> 14, of which waited for: 7 -> 7; matrix products, arithmetic and copies ran while one was open for 48% -> 50% of each run, Pallas kernels for 0% -> 0%
where the time goes in v9:
time: 796 us; the launch traced here: 785 us
  waiting for transfers between devices  297 us (37%)
  matrix products  233 us (29%)
  local copies, waits for them, and re-layouts  111 us (14%)
  other arithmetic  105 us (13%)
  starting transfers between devices  22.1 us (3%)
  between operations  17.1 us (2%)
    psum x1, waiting for transfers between devices, per_device_body(): late = [lax.psum(qkv_b, ('row', 'col')).astype(jnp.float32)]  120 us
    psum x1, waiting for transfers between devices, per_device_body(): early_b = lax.psum(early_b, ('row', 'col'))  102 us
    all_gather x1, waiting for transfers between devices, per_device_body(): normed_all = lax.all_gather(normed_mid, 'col', axis=0, tiled=True)  48.1 us
    dot_general x7, matrix products, contract_rows(): lax.dot_general(left, right, (((0,), (0,)), ((), ())), preferred_element_...  37.4 us
    dot_general x7, matrix products, contract_cols(): lax.dot_general(left, right, (((1,), (1,)), ((), ())), preferred_element_...  30.3 us
    unnamed x361, local copies, waits for them, and re-layouts  29.9 us
    dot_general x10, matrix products, _mm(): return jnp.einsum('...ij,...jk->...ik', a, b, precision=HI)  16.8 us
  transfers between devices with their start and end apart: 14, of which 7 were waited for; matrix products, arithmetic and copies ran while one was open for 50% of the time, Pallas kernels for 0%

profile of v9, /device:TPU:0, one launch (start us, length us, event | category | flops | bytes accessed | tf_op | source)
XLA Modules:
  0.0 785.4 jit_solution(1537393536005365256)
XLA Ops:
  11.7 5.0 fusion.236
  16.9 6.2 fusion.5
  45.6 3.6 fusion.74
  58.6 4.0 reshape.422
  90.7 4.6 fusion.27
  95.4 4.6 fusion.98
  124.7 7.0 multiply_convert_fusion.3
  141.8 48.1 %all-gather.8.cloned.1.call-done = bf16[3072,1024]{1,0:T(8,128)(2,1)} async-done(((bf16[384,1024]{1,0:T(8,128)(2,1)}), bf16[3072,1024]{1,0:T(8,128)(2,1)}) %all-gather.8.cloned.1.call-update) | async-done | bytes 6291472 | tf_op jit(solution)/shard_map/all_gather | solution.py:235
  189.9 5.5 fusion.118
  195.5 4.5 fusion.122
  200.0 7.1 multiply_convert_fusion
  210.6 5.6 add_convert_fusion
  216.2 5.8 convolution_convert_fusion.6
  223.0 5.0 all-to-all-start.2
  228.0 7.5 convolution_convert_fusion.5
  240.1 7.2 convolution_convert_fusion.4
  252.4 5.0 all-to-all-start.1
  269.5 7.9 %convolution_convert_fusion.1 = bf16[3072,1024]{1,0:T(8,128)(2,1)} fusion(bf16[3072,352]{0,1:T(8,128)(2,1)} %get-tuple-element.113, bf16[352,1024]{1,0:T(8,128)(2,1)} %slice_bitcast_fusion.8), kind=kOutput, calls=%fused_computation.6 | convolution fusion | flops 2217738240 | bytes 9175040 | tf_op jit(solution)/shard_map/dot_general | solution.py:239
  279.4 12.5 %all-to-all-done.1 = bf16[2,4,256,352]{2,3,0,1:T(8,128)(2,1)} async-done(((bf16[2,4,256,352]{2,3,0,1:T(8,128)(2,1)}), bf16[2,4,256,352]{2,3,0,1:T(8,128)(2,1)}, u32[]{:S(2)}, u32[]{:S(2)}) %all-to-all-start.1) | async-done | bytes 1441824 | tf_op jit(solution)/shard_map/all_to_all | solution.py:308
  292.0 4.8 all-to-all-start
  305.0 5.8 fusion.170
  316.5 5.4 convolution_convert_fusion.3
  324.0 3.5 convolution_convert_fusion.2
  331.0 3.6 add_add_fusion
  336.9 4.1 fusion.14
  341.1 5.0 fusion.22
  348.6 4.5 convolution_add_fusion
  368.8 4.6 fusion.9
  375.5 5.1 fusion.49
  380.7 4.4 fusion.6
  385.1 3.7 fusion.7
  395.4 5.7 fusion.85
  403.3 4.7 fusion.53
  408.2 5.5 multiply_reduce_fusion.8
  427.6 6.2 broadcast_multiply_fusion
  453.0 5.3 add_add_fusion.4
  459.8 6.1 multiply_reduce_fusion.3
  475.9 3.9 fusion.253
  479.9 6.7 add_convert_fusion.1
  491.7 7.4 convolution_convert_fusion
  500.8 102.1 %all-reduce.40.cloned.1.call-done = bf16[3072,1024]{1,0:T(8,128)(2,1)} async-done(((bf16[3072,1024]{1,0:T(8,128)(2,1)}), bf16[3072,1024]{1,0:T(8,128)(2,1)}) %all-reduce.40.cloned.1.call-update) | async-done | bytes 6291472 | tf_op jit(solution)/shard_map/psum | solution.py:265
  603.0 4.5 convert_reduce_fusion
  613.8 5.7 collective-permute-done.3
  622.9 6.0 collective-permute-done.4
  632.8 9.2 %slice_convert_fusion = (f32[1536,1024]{1,0:T(8,128)}, f32[1024,1536]{0,1:T(8,128)}) fusion(bf16[3072,1024]{1,0:T(8,128)(2,1)} %all-reduce.40.cloned.1.call-done), kind=kLoop, calls=%fused_computation.37 | loop fusion | flops 3145728 | bytes 18874368 | tf_op jit(solution)/shard_map/convert_element_type | solution.py:267
  642.0 6.7 copy.244
  648.7 120.0 %all-reduce.42.cloned.1.call-done = bf16[1024,3072]{1,0:T(8,128)(2,1)} async-done(((bf16[1024,3072]{1,0:T(8,128)(2,1)}), bf16[1024,3072]{1,0:T(8,128)(2,1)}) %all-reduce.42.cloned.1.call-update) | async-done | bytes 6291472 | tf_op jit(solution)/shard_map/psum | solution.py:282
  768.7 9.4 %convert_element_type.139 = f32[1024,3072]{1,0:T(8,128)} convert(bf16[1024,3072]{1,0:T(8,128)(2,1)} %all-reduce.42.cloned.1.call-done) | non-fusion elementwise | flops 3145728 | bytes 18874368 | tf_op jit(solution)/shard_map/convert_element_type | solution.py:282
  (579 shorter events, 241.9 us)
Async XLA Ops:
  7.2 129.1 %copy-start = (bf16[1536,1024]{1,0:T(8,128)(2,1)S(1)}, bf16[1536,1024]{1,0:T(8,128)(2,1)}, u32[]{:S(2)}) copy-start(bf16[1536,1024]{1,0:T(8,128)(2,1)} %param.25) | copy-start | bytes 9437188
  7.2 124.5 %all-gather.4.cloned.1.call-start = ((), (), s32[]{:S(2)}) async-start(), calls=%async_computation.4 | async-start | bytes 2703360 | tf_op jit(solution)/shard_map/all_gather | solution.py:225
  9.4 126.9 %all-gather.6.cloned.1.call-start = ((), (), s32[]{:S(2)}) async-start(), calls=%async_computation.5 | async-start | bytes 7077888 | tf_op jit(solution)/shard_map/all_gather | solution.py:227
  10.1 179.8 %all-gather.8.cloned.1.call-start = ((), (), s32[]{:S(2)}) async-start(), calls=%async_computation.6 | async-start | bytes 7077888 | tf_op jit(solution)/shard_map/all_gather | solution.py:235
  32.2 8.1 %copy-start.102 = (pred[64,64]{0,1:T(8,128)(4,1)}, pred[64,64]{0,1:T(8,128)(4,1)S(1)}, u32[]{:S(2)}) copy-start(pred[64,64]{0,1:T(8,128)(4,1)S(1)} %iota_compare_fusion.3) | copy-start | bytes 12292
  35.8 48.3 %copy-start.87 = (f32[6,64,6]{1,2,0:T(8,128)}, f32[6,64,6]{1,2,0:T(8,128)S(1)}, u32[]{:S(2)}) copy-start(f32[6,64,6]{1,2,0:T(8,128)S(1)} %copy.346) | copy-start | bytes 27652
  36.0 76.8 %copy-start.77 = (pred[6,64,64]{1,2,0:T(8,128)(4,1)}, pred[6,64,64]{1,2,0:T(8,128)(4,1)S(1)}, u32[]{:S(2)}) copy-start(pred[6,64,64]{1,2,0:T(8,128)(4,1)S(1)} %compare_and_fusion) | copy-start | bytes 73732
  37.3 75.4 %copy-start.61 = (f32[6,6,64]{2,1,0:T(8,128)}, f32[6,6,64]{2,1,0:T(8,128)S(1)}, u32[]{:S(2)}) copy-start(f32[6,6,64]{2,1,0:T(8,128)S(1)} %reduce_window_sum.22) | copy-start | bytes 27652
  37.3 75.4 %copy-start.89 = (f32[6,6,64]{2,1,0:T(8,128)}, f32[6,6,64]{2,1,0:T(8,128)S(1)}, u32[]{:S(2)}) copy-start(f32[6,6,64]{2,1,0:T(8,128)S(1)} %get-tuple-element.108) | copy-start | bytes 27652
  37.4 11.9 %slice-start.8 = ((s8[4718592]{0:T(1024)(128)(4,1)}), s8[4194304]{0:T(1024)(128)(4,1)S(1)}, s32[]{:S(2)}) async-start(s8[4718592]{0:T(1024)(128)(4,1)} %bitcast.422), calls=%async_computation.18 | async-start | bytes 8388608
  40.3 8.9 %slice-start.9 = ((s8[4718592]{0:T(1024)(128)(4,1)}), s8[524288]{0:T(1024)(128)(4,1)S(1)}, s32[]{:S(2)}) async-start(s8[4718592]{0:T(1024)(128)(4,1)} %bitcast.422), calls=%async_computation.19 | async-start | bytes 1048576
  64.6 45.1 %copy-start.94 = (f32[6,64,6]{1,2,0:T(8,128)}, f32[6,64,6]{1,2,0:T(8,128)S(1)}, u32[]{:S(2)}) copy-start(f32[6,64,6]{1,2,0:T(8,128)S(1)} %copy.181) | copy-start | bytes 27652
  64.9 35.2 %copy-start.137 = (f32[6]{0:T(128)}, f32[6]{0:T(128)S(1)}, u32[]{:S(2)}) copy-start(f32[6]{0:T(128)S(1)} %get-tuple-element.101) | copy-start | bytes 76
  64.9 36.1 %copy-start.141 = (f32[6]{0:T(128)}, f32[6]{0:T(128)S(1)}, u32[]{:S(2)}) copy-start(f32[6]{0:T(128)S(1)} %get-tuple-element.100) | copy-start | bytes 76
  64.9 37.0 %copy-start.143 = (f32[6]{0:T(128)}, f32[6]{0:T(128)S(1)}, u32[]{:S(2)}) copy-start(f32[6]{0:T(128)S(1)} %get-tuple-element.99) | copy-start | bytes 76
  64.9 37.9 %copy-start.139 = (f32[6]{0:T(128)}, f32[6]{0:T(128)S(1)}, u32[]{:S(2)}) copy-start(f32[6]{0:T(128)S(1)} %get-tuple-element.98) | copy-start | bytes 76
  84.0 11.4 %copy-start.96 = (f32[6,6,64]{2,1,0:T(8,128)}, f32[6,6,64]{2,1,0:T(8,128)S(1)}, u32[]{:S(2)}) copy-start(f32[6,6,64]{2,1,0:T(8,128)S(1)} %slice_reduce_fusion) | copy-start | bytes 27652
  90.7 16.0 %copy-start.10 = (f32[6,6,64,384]{3,2,1,0:T(8,128)}, f32[6,6,64,384]{3,2,1,0:T(8,128)S(1)}, u32[]{:S(2)}) copy-start(f32[6,6,64,384]{3,2,1,0:T(8,128)S(1)} %fusion.8) | copy-start | bytes 10616836
  95.3 7.5 copy-start.21
  141.6 157.9 %reduce-scatter.2.cloned.1.call-start = ((), (), s32[]{:S(2)}) async-start(), calls=%async_computation.7 | async-start | bytes 7077888 | tf_op jit(solution)/shard_map/reduce_scatter | solution.py:246
  189.9 10.1 %slice-start.14 = ((s8[6291456]{0:T(1024)(128)(4,1)}), s8[4194304]{0:T(1024)(128)(4,1)S(1)}, s32[]{:S(2)}) async-start(s8[6291456]{0:T(1024)(128)(4,1)} %bitcast.486), calls=%async_computation.24 | async-start | bytes 8388608
  223.0 29.4 %all-to-all-start.2 = ((bf16[352,4,256]{2,0,1:T(8,128)(2,1)}), bf16[352,4,256]{2,0,1:T(8,128)(2,1)}, u32[]{:S(2)}, u32[]{:S(2)}) async-start(bf16[352,4,256]{2,0,1:T(8,128)(2,1)} %bitcast.451), calls=%async_computation.3 | async-start | bytes 1441792 | tf_op jit(solution)/shard_map/all_to_all | solution.py:308
  252.4 39.5 %all-to-all-start.1 = ((bf16[2,4,256,352]{2,3,0,1:T(8,128)(2,1)}), bf16[2,4,256,352]{2,3,0,1:T(8,128)(2,1)}, u32[]{:S(2)}, u32[]{:S(2)}) async-start(bf16[2,4,256,352]{2,3,0,1:T(8,128)(2,1)} %pad_maximum_fusion.4), calls=%async_computation.2 | async-start | bytes 2883584 | tf_op jit(solution)/shard_map/all_to_all | solution.py:308
  292.0 311.0 %all-to-all-start = ((bf16[8,384,1024]{2,1,0:T(8,128)(2,1)}), bf16[8,384,1024]{2,1,0:T(8,128)(2,1)}, u32[]{:S(2)}, u32[]{:S(2)}) async-start(bf16[8,384,1024]{2,1,0:T(8,128)(2,1)} %bitcast.442), calls=%async_computation | async-start | bytes 12582912 | tf_op jit(solution)/shard_map/all_to_all | solution.py:308
  296.7 306.2 %all-reduce.40.cloned.1.call-start = ((), (), s32[]{:S(2)}) async-start(), calls=%async_computation.8 | async-start | bytes 12582912 | tf_op jit(solution)/shard_map/psum | solution.py:265
  304.1 6.6 copy-start.67
  341.1 47.7 %copy-start.33 = (f32[6,6,64,64]{2,3,1,0:T(8,128)}, f32[6,6,64,64]{2,3,1,0:T(8,128)S(1)}, u32[]{:S(2)}) copy-start(f32[6,6,64,64]{2,3,1,0:T(8,128)S(1)} %fusion.14) | copy-start | bytes 1769476
  353.1 12.5 %copy-start.20 = (f32[6,6,128,256]{3,2,1,0:T(8,128)}, f32[6,6,128,256]{3,2,1,0:T(8,128)S(1)}, u32[]{:S(2)}) copy-start(f32[6,6,128,256]{3,2,1,0:T(8,128)S(1)} %convolution_add_fusion) | copy-start | bytes 14155780
  366.0 9.5 %slice-start.4 = ((s8[4718592]{0:T(1024)(128)(4,1)}), s8[4194304]{0:T(1024)(128)(4,1)S(1)}, s32[]{:S(2)}) async-start(s8[4718592]{0:T(1024)(128)(4,1)} %bitcast.418), calls=%async_computation.14 | async-start | bytes 8388608
  368.8 6.7 slice-start.5
  388.8 6.5 copy-start.27
  413.7 7.2 copy-start.28
  415.5 11.9 %slice-start.6 = ((s8[4718592]{0:T(1024)(128)(4,1)}), s8[4194304]{0:T(1024)(128)(4,1)S(1)}, s32[]{:S(2)}) async-start(s8[4718592]{0:T(1024)(128)(4,1)} %bitcast.420), calls=%async_computation.16 | async-start | bytes 8388608
  420.9 6.5 slice-start.7
  447.4 10.9 %slice-start.10 = ((s8[4718592]{0:T(1024)(128)(4,1)}), s8[524288]{0:T(1024)(128)(4,1)S(1)}, s32[]{:S(2)}) async-start(s8[4718592]{0:T(1024)(128)(4,1)} %bitcast.424), calls=%async_computation.20 | async-start | bytes 1048576
  447.4 321.3 %all-reduce.42.cloned.1.call-start = ((), (), s32[]{:S(2)}) async-start(), calls=%async_computation.9 | async-start | bytes 12582912 | tf_op jit(solution)/shard_map/psum | solution.py:282
  452.9 6.9 slice-start.11
  466.0 6.6 copy-start.3
  475.9 10.7 %slice-start.12 = ((s8[6291456]{0:T(1024)(128)(4,1)}), s8[4194304]{0:T(1024)(128)(4,1)S(1)}, s32[]{:S(2)}) async-start(s8[6291456]{0:T(1024)(128)(4,1)} %bitcast.484), calls=%async_computation.22 | async-start | bytes 8388608
  479.9 6.7 slice-start.13
  491.3 7.8 collective-permute-start
  499.1 108.4 %collective-permute-start.1 = (f32[26892]{0:T(1024)S(1)}, f32[26892]{0:T(1024)S(1)}, u32[]{:S(2)}, u32[]{:S(2)}) collective-permute-start(f32[26892]{0:T(1024)S(1)} %add.273), channel_id=1, source_target_pairs={{0,2},{1,3},{2,0},{3,1},{4,6},{5,7},{6,4},{7,5},{8,10},{9,11},{10,... | collective-permute-start | bytes 322712 | tf_op jit(solution)/shard_map/ppermute | solution.py:329
  607.6 13.8 %copy-start.68 = (f32[384,1024]{1,0:T(8,128)S(1)}, f32[384,1024]{1,0:T(8,128)}, u32[]{:S(2)}) copy-start(f32[384,1024]{1,0:T(8,128)} %copy-done.67) | copy-start | bytes 4718596
  607.6 13.8 %copy-start.69 = (f32[384,1024]{1,0:T(8,128)S(1)}, f32[384,1024]{1,0:T(8,128)}, u32[]{:S(2)}) copy-start(f32[384,1024]{1,0:T(8,128)} %get-tuple-element.186) | copy-start | bytes 4718596
  607.6 4.8 collective-permute-start.2
  612.4 7.0 collective-permute-start.3
  619.5 9.4 %collective-permute-start.4 = (f32[26892]{0:T(1024)S(1)}, f32[26892]{0:T(1024)S(1)}, u32[]{:S(2)}, u32[]{:S(2)}) collective-permute-start(f32[26892]{0:T(1024)S(1)} %add.276), channel_id=1, source_target_pairs={{0,16},{8,24},{16,0},{24,8},{1,17},{9,25},{17,1},{25,9},{2,18},{10... | collective-permute-start | bytes 322712 | tf_op jit(solution)/shard_map/ppermute | solution.py:329
  768.7 9.4 %copy-start.1 = (bf16[1536,1024]{1,0:T(8,128)(2,1)S(1)}, bf16[1536,1024]{1,0:T(8,128)(2,1)}, u32[]{:S(2)}) copy-start(bf16[1536,1024]{1,0:T(8,128)(2,1)} %param.25) | copy-start | bytes 9437188
  (139 other events, 439.0 us)
Sparse Core Ops, SparseCore 0:
  10.2 50.0 all-gather.3
  62.1 43.5 all-gather.5
  141.7 48.1 all-gather.7
  216.4 61.7 reduce-scatter.1
  447.5 155.3 all-reduce.39
  609.0 159.6 all-reduce.41
